TPU v7x, 512 devices: a whole 4x8x8 slice. The times are simulated.
512 devices in a mesh: energy: 64 (over y, z_lo, core), domain: 8 (over z_hi, x).
Axes of the slice: x: 4, y: 8, z: 8 (z_hi: 2, z_lo: 4; z = z_hi * 4 + z_lo), core: 2. Of those that a mesh axis runs over, the one named last changes fastest.
Arguments:
- green_slab: bfloat16 [64, 8, 2, 3, 64, 2048], P('energy', 'domain'), may hold values from -6 to 6
- self_energy: float32 [64, 8, 2, 2, 2048], P('energy', 'domain'), may hold values from -3 to 3
- pattern: int32 [8, 2560], P('domain'), may hold values from 0 to 5119, as said below
- screened: bfloat16 [64, 8, 2, 64, 80], P('energy', 'domain'), may hold values from -0.625 to 0.625
Outputs:
- screened_lesser: float32 [64, 8, 2, 64, 64], P('energy', 'domain')
Inputs may be any that keep to these rules, and one draw needn't show every extreme that they name: `pattern`: within each domain the 2560 positions are distinct flat positions r * 80 + c; the first and the last position of the matrix are always retained.
All inputs are finite; a program needn't handle non-finite values.
Results may differ from a plain program's by a relative error of at most 0.007.
Values may be sent and summed in bfloat16 or wider, within the bound.
No kernel may reach another device: no remote copies, remote signals or barrier semaphores. Data moves between devices by JAX's collectives and lax.ppermute only.
A program may use at most 64 MiB of HBM per device.

v0:
```python
import math

import jax
import jax.numpy as jnp
from jax import lax
from jax.sharding import PartitionSpec as P

EDGE = 16


def padded_2(cells, sides, width):
    for axis, dim in sides:
        count = lax.axis_size(axis)
        ends = count - 1
        head = lax.slice_in_dim(cells, 0, width, axis=dim)
        tail = lax.slice_in_dim(cells, cells.shape[dim] - width, cells.shape[dim], axis=dim)
        cells = jnp.concatenate(
            [
                lax.ppermute(tail, axis, [(i, (i + 1) % count) for i in range(ends)]),
                cells,
                lax.ppermute(head, axis, [((i + 1) % count, i) for i in range(ends)]),
            ],
            axis=dim,
        )
    return cells


def passed_along(x, axis, by):
    length = lax.axis_size(axis)
    pairs = [(i, i + by) for i in range(length) if 0 <= i + by < length]
    return lax.ppermute(x, axis, pairs)


def slab_adjoint(left_real, left_imag, right_real, right_imag):
    real_sum = jnp.einsum(
        "qjrb,jsb->qrs", left_real, right_real, preferred_element_type=jnp.float32
    ) + jnp.einsum("qjrb,jsb->qrs", left_imag, right_imag, preferred_element_type=jnp.float32)
    imag_sum = jnp.einsum(
        "qjrb,jsb->qrs", left_imag, right_real, preferred_element_type=jnp.float32
    ) - jnp.einsum("qjrb,jsb->qrs", left_real, right_imag, preferred_element_type=jnp.float32)
    return (real_sum, imag_sum)


def times_adjoint(left_real, left_imag, right_real, right_imag):
    real_sum = jnp.dot(left_real, right_real.T, preferred_element_type=jnp.float32) + jnp.dot(
        left_imag, right_imag.T, preferred_element_type=jnp.float32
    )
    imag_sum = jnp.dot(left_imag, right_real.T, preferred_element_type=jnp.float32) - jnp.dot(
        left_real, right_imag.T, preferred_element_type=jnp.float32
    )
    return (real_sum, imag_sum)


def complex_product(left_real, left_imag, right_real, right_imag):
    real_sum = jnp.dot(left_real, right_real, preferred_element_type=jnp.float32) - jnp.dot(
        left_imag, right_imag, preferred_element_type=jnp.float32
    )
    imag_sum = jnp.dot(left_real, right_imag, preferred_element_type=jnp.float32) + jnp.dot(
        left_imag, right_real, preferred_element_type=jnp.float32
    )
    return (real_sum, imag_sum)


def element_values(own_slab, next_edge, diag_rates, pattern_row):
    block_order = own_slab.shape[3]
    factor = 1.0 / math.sqrt(3.0 * block_order)
    rate_real = jnp.transpose(diag_rates[:, :, 0], (1, 0, 2))[:, :, None, :]
    rate_imag = jnp.transpose(diag_rates[:, :, 1], (1, 0, 2))[:, :, None, :]
    slab_real = own_slab[0].astype(jnp.float32)[None]
    slab_imag = own_slab[1].astype(jnp.float32)[None]
    weighted_real = ((slab_real * rate_real - slab_imag * rate_imag) * factor).astype(jnp.bfloat16)
    weighted_imag = ((slab_real * rate_imag + slab_imag * rate_real) * factor).astype(jnp.bfloat16)
    near_real, near_imag = slab_adjoint(weighted_real, weighted_imag, own_slab[0], own_slab[1])
    edge_real, edge_imag = slab_adjoint(
        weighted_real[:, 1:3], weighted_imag[:, 1:3], next_edge[0], next_edge[1]
    )
    joined_real = jnp.concatenate([near_real, edge_real], axis=2).reshape(2, -1)
    joined_imag = jnp.concatenate([near_imag, edge_imag], axis=2).reshape(2, -1)
    picked_real = jnp.take(joined_real, pattern_row, axis=1)
    picked_imag = jnp.take(joined_imag, pattern_row, axis=1)
    return jnp.stack([picked_real, picked_imag], axis=1).astype(jnp.bfloat16)


def lagged_sums(by_element):
    energy_count = by_element.shape[0]
    column_count = by_element.shape[3]
    lesser = by_element[:, 0].astype(jnp.float32)
    backward = by_element[::-1, 1].astype(jnp.float32)
    real_part = (
        lesser[:, None, 0] * backward[None, :, 0] - lesser[:, None, 1] * backward[None, :, 1]
    )
    imag_part = (
        lesser[:, None, 0] * backward[None, :, 1] + lesser[:, None, 1] * backward[None, :, 0]
    )
    joined = jnp.concatenate([real_part, imag_part], axis=2)
    padded = jnp.pad(joined, ((0, 0), (0, energy_count + 1), (0, 0)))
    flat_rows = padded.reshape(energy_count * (2 * energy_count + 1), 2 * column_count)
    skewed = flat_rows[: energy_count * 2 * energy_count].reshape(
        energy_count, 2 * energy_count, 2 * column_count
    )
    totals = jnp.sum(skewed, axis=0)[energy_count - 1 : 2 * energy_count - 1]
    factor = 1.0 / math.sqrt(energy_count)
    return (totals.reshape(energy_count, 2, column_count) * factor).astype(jnp.bfloat16)


def screen(polar_row, pattern_row, screen_block):
    row_count = screen_block.shape[1]
    col_count = screen_block.shape[2]
    flat_dense = (
        jnp.zeros((2, row_count * col_count), jnp.bfloat16).at[:, pattern_row].set(polar_row)
    )
    dense_pol = flat_dense.reshape(2, row_count, col_count)
    inner_real, inner_imag = times_adjoint(
        dense_pol[0], dense_pol[1], screen_block[0], screen_block[1]
    )
    inner_real = inner_real.astype(jnp.bfloat16)
    inner_imag = inner_imag.astype(jnp.bfloat16)
    near_real = screen_block[0][:, :row_count]
    near_imag = screen_block[1][:, :row_count]
    across_real, across_imag = complex_product(
        near_real, near_imag, dense_pol[0][:, row_count:], dense_pol[1][:, row_count:]
    )
    across_real = across_real.astype(jnp.bfloat16)
    across_imag = across_imag.astype(jnp.bfloat16)
    first_real, first_imag = complex_product(near_real, near_imag, inner_real, inner_imag)
    second_real, second_imag = times_adjoint(
        screen_block[0][:, row_count:], screen_block[1][:, row_count:], across_real, across_imag
    )
    return jnp.stack([first_real + second_real, first_imag + second_imag], axis=0)


def body(green_slab, self_energy, pattern, screened):
    nearby = padded_2(self_energy, (("domain", 1),), 1)
    edge_block = green_slab[0, 0, :, 0:2, :EDGE, :]
    following = passed_along(edge_block, "domain", -1)
    values = element_values(green_slab[0, 0], following, nearby[0], pattern[0])[None]
    by_element = lax.all_to_all(values, "energy", split_axis=3, concat_axis=0, tiled=True)
    polarization = lagged_sums(by_element)
    per_energy = lax.all_to_all(polarization, "energy", split_axis=0, concat_axis=2, tiled=True)
    result = screen(per_energy[0], pattern[0], screened[0, 0])
    return result[None, None]


def solution(mesh):
    placed = (
        P("energy", "domain", None, None, None, None),
        P("energy", "domain", None, None, None),
        P("domain", None),
        P("energy", "domain", None, None, None),
    )
    return jax.shard_map(
        body,
        mesh=mesh,
        in_specs=placed,
        out_specs=P("energy", "domain", None, None, None),
        check_vma=False,
    )
```

profile of v0, /device:TPU:7, one launch (start us, length us, event | category | flops | bytes accessed | tf_op | source)
XLA Modules:
  0.0 152.5 jit_solution(12286453965259205942)
XLA Ops:
  0.0 10.5 %collective-permute-start = (f32[1,1,2,2,2048]{4,3,2,1,0:T(2,128)}, f32[1,1,2,2,2048]{4,3,2,1,0:T(2,128)S(1)}, u32[]{:S(2)}, u32[]{:S(2)}) collective-permute-start(f32[1,1,2,2,2048]{4,3,2,1,0:T(2,128)} %param.7), channel_id=1, source_target_pairs={{0,1},{1,2},{2,3},{3,4},{4,5},{5,6},{6,7},{8,9},{9,10},{10,11},{11... | collective-permute-start | bytes 98312 | tf_op jit(solution)/shard_map/ppermute | solution.py:19
  10.5 1.9 %collective-permute-start.1 = (f32[1,1,2,2,2048]{4,3,2,1,0:T(2,128)}, f32[1,1,2,2,2048]{4,3,2,1,0:T(2,128)S(1)}, u32[]{:S(2)}, u32[]{:S(2)}) collective-permute-start(f32[1,1,2,2,2048]{4,3,2,1,0:T(2,128)} %param.7), channel_id=1, source_target_pairs={{1,0},{2,1},{3,2},{4,3},{5,4},{6,5},{7,6},{9,8},{10,9},{11,10},{12... | collective-permute-start | bytes 98312 | tf_op jit(solution)/shard_map/ppermute | solution.py:21
  12.5 1.0 slice_bitcast_fusion.1
  13.5 1.9 %collective-permute-start.2 = (bf16[2,2,16,2048]{3,2,1,0:T(8,128)(2,1)S(1)}, bf16[2,2,16,2048]{3,2,1,0:T(8,128)(2,1)}, u32[]{:S(2)}, u32[]{:S(2)}) collective-permute-start(bf16[2,2,16,2048]{3,2,1,0:T(8,128)(2,1)S(1)} %slice_bitcast_fusion.1), channel_id=1, source_target_pairs={{1,0},{2,1},{3,2},{4,3},{5,4},{6,5},{7,6},{9,8},{10,9},{11,10},{12... | collective-permute-start | bytes 786440 | tf_op jit(solution)/shard_map/ppermute | solution.py:31
  15.4 1.7 %bitcast_convert_fusion.3 = (f32[3,64,2048]{2,1,0:T(8,128)S(1)}, f32[3,64,2048]{2,1,0:T(8,128)S(1)}) fusion(bf16[1,1,2,3,64,2048]{5,4,3,2,1,0:T(8,128)(2,1)} %param.6), kind=kLoop, calls=%fused_computation.97 | loop fusion | flops 786432 | bytes 4718592 | tf_op jit(solution)/shard_map/convert_element_type | solution.py:69
  17.3 4.2 %collective-permute-done.1 = f32[1,1,2,2,2048]{4,3,2,1,0:T(2,128)S(1)} collective-permute-done((f32[1,1,2,2,2048]{4,3,2,1,0:T(2,128)}, f32[1,1,2,2,2048]{4,3,2,1,0:T(2,128)S(1)}, u32[]{:S(2)}, u32[]{:S(2)}) %collective-permute-start.1) | collective-permute-done | bytes 32800 | tf_op jit(solution)/shard_map/ppermute | solution.py:21
  21.5 0.1 fusion.115
  21.8 1.9 %fusion.53 = f32[2,64,64]{2,1,0:T(8,128)S(1)} fusion(f32[2,3,2048]{2,1,0:T(4,128)S(1)} %copy.86, f32[3,64,2048]{2,1,0:T(8,128)S(1)} %get-tuple-element.9, f32[2,3,2048]{2,1,0:T(4,128)S(1)} %copy.85, f32[3,64,2048]{2,1,0:T(8,128)S(1)} %get-tuple-element.8, bf16[1,1,2,3,64,2048]{5,4,3,2,1,0:T(8,128)(2,1)} %param.6), kind=kOutput, calls=%fused_computation.69 | convolution fusion | flops 104595456 | bytes 4063232 | tf_op jit(solution)/shard_map/qjrb,jsb->qrs/dot_general | solution.py:40
  23.7 0.7 fusion.52
  24.4 1.3 fusion.51
  25.6 1.3 fusion.49
  27.0 1.4 collective-permute-done.2
  28.4 1.4 fusion.63
  29.8 1.5 fusion.61
  31.2 0.1 copy.89
  31.4 0.1 pad_maximum_fusion.2
  31.5 1.6 %copy.107 = bf16[2,64,80]{0,2,1:T(8,128)(2,1)} copy(bf16[2,64,80]{2,1,0:T(8,128)(2,1)S(1)} %pad_maximum_fusion.2) | data formatting | bytes 40960 | tf_op jit(solution)/shard_map/reshape | solution.py:78
  33.1 1.4 fusion.62
  34.5 1.5 fusion.65
  36.0 0.1 copy.87
  36.1 0.1 pad_maximum_fusion.1
  36.2 0.6 copy.106
  36.8 5.7 %gather_fusion.1 = bf16[2560,2]{1,0:T(8,128)(2,1)S(1)} fusion(bf16[2,5120]{0,1:T(8,128)(2,1)} %bitcast.152, s32[3072]{0:T(1024)S(1)} %pad_clamp_fusion), kind=kCustom, calls=%fused_computation.1.clone | custom fusion | bytes 30720 | tf_op jit(solution)/shard_map/jit(_take)/gather | solution.py:80
  42.5 5.1 %gather_fusion = bf16[2560,2]{1,0:T(8,128)(2,1)S(1)} fusion(bf16[2,5120]{0,1:T(8,128)(2,1)S(1)} %bitcast.153, s32[3072]{0:T(1024)S(1)} %pad_clamp_fusion), kind=kCustom, calls=%fused_computation.clone | custom fusion | bytes 30720 | tf_op jit(solution)/shard_map/jit(_take)/gather | solution.py:79
  47.6 1.4 fusion.72
  49.0 0.3 pad_maximum_fusion
  49.3 11.6 %copy.91 = bf16[1,2,2,2560]{1,2,0,3:T(2,128)(2,1)} copy(bf16[1,2,2,2560]{1,3,2,0:T(8,128)(2,1)S(1)} %pad_maximum_fusion) | data formatting | bytes 40960 | tf_op jit(solution)/shard_map/stack | solution.py:81
  60.9 17.1 %all-to-all-start = ((bf16[1,2,2,2560]{1,2,0,3:T(2,128)(2,1)}), bf16[1,2,2,2560]{1,2,0,3:T(2,128)(2,1)S(1)}, u32[]{:S(2)}, u32[]{:S(2)}) async-start(bf16[1,2,2,2560]{1,2,0,3:T(2,128)(2,1)} %copy.91), calls=%async_computation | async-start | bytes 2621440 | tf_op jit(solution)/shard_map/all_to_all | solution.py:137
  78.0 34.2 %all-to-all-done = bf16[1,2,2,2560]{1,2,0,3:T(2,128)(2,1)S(1)} async-done(((bf16[1,2,2,2560]{1,2,0,3:T(2,128)(2,1)}), bf16[1,2,2,2560]{1,2,0,3:T(2,128)(2,1)S(1)}, u32[]{:S(2)}, u32[]{:S(2)}) %all-to-all-start) | async-done | bytes 20512 | tf_op jit(solution)/shard_map/all_to_all | solution.py:137
  112.1 1.4 copy.93
  113.6 0.1 rev.3
  113.7 0.7 multiply_subtract_fusion
  114.5 3.0 %select_maximum_fusion = f32[64,129,80]{1,0,2:T(8,128)} fusion(f32[64,64,40]{1,0,2:T(8,128)S(1)} %get-tuple-element.13, f32[64,64,40]{1,0,2:T(8,128)S(1)} %get-tuple-element.12), kind=kLoop, calls=%fused_computation.3 | loop fusion | flops 2641920 | bytes 3952640 | tf_op jit(solution)/shard_map/concatenate | solution.py:95
  117.5 4.5 %reshape.116 = f32[8256,80]{0,1:T(8,128)S(1)} reshape(f32[64,129,80]{1,0,2:T(8,128)} %select_maximum_fusion) | data formatting | bytes 5283840 | tf_op jit(solution)/shard_map/reshape | solution.py:97
  122.0 0.2 slice_bitcast_fusion
  122.2 0.5 copy.112
  122.7 0.3 bitcast_reduce_fusion
  122.9 0.1 fusion.80
  123.0 0.7 copy.94
  123.7 6.0 %all-to-all-start.1 = ((bf16[64,2,40]{2,1,0:T(2,128)(2,1)}), bf16[64,2,40]{2,1,0:T(2,128)(2,1)S(1)}, u32[]{:S(2)}, u32[]{:S(2)}) async-start(bf16[64,2,40]{2,1,0:T(2,128)(2,1)} %copy.94), calls=%async_computation.1 | async-start | bytes 65536 | tf_op jit(solution)/shard_map/all_to_all | solution.py:139
  129.7 9.5 %all-to-all-done.1 = bf16[64,2,40]{2,1,0:T(2,128)(2,1)S(1)} async-done(((bf16[64,2,40]{2,1,0:T(2,128)(2,1)}), bf16[64,2,40]{2,1,0:T(2,128)(2,1)S(1)}, u32[]{:S(2)}, u32[]{:S(2)}) %all-to-all-start.1) | async-done | bytes 10272 | tf_op jit(solution)/shard_map/all_to_all | solution.py:139
  139.3 0.1 reshape.137
  139.4 0.4 copy.96
  139.8 7.5 %scatter_custom_fusion = bf16[2,5120]{0,1:T(8,128)(2,1)S(1)} fusion(s32[2560]{0:T(1024)S(1)} %fusion.104, bf16[2560,2]{1,0:T(8,128)(2,1)S(1)} %copy.96, bf16[]{:T(256)} %constant.1.clone.1), kind=kCustom, calls=%fused_computation.100 | custom fusion | bytes 20482 | tf_op jit(solution)/shard_map/scatter | solution.py:110
  147.3 1.2 slice_reduce_fusion.1
  148.5 0.1 squeeze.68
  148.6 0.1 fusion.114
  148.7 0.1 squeeze.70
  148.8 0.1 fusion.113
  149.0 0.2 fusion.92
  149.2 0.2 fusion.88
  149.4 0.2 fusion.66
  149.7 0.2 fusion.86
  149.9 0.2 fusion.82
  150.1 0.1 fusion.58
  150.2 0.2 fusion.102
  150.4 0.1 fusion.59
  150.6 0.2 fusion.98
  150.8 0.2 convolution_subtract_fusion.1
  150.9 0.2 fusion.67
  151.2 0.2 convolution_add_fusion
  151.4 0.2 fusion.57
  151.6 0.2 fusion.55
  151.8 0.7 copy.97
  (31 shorter events, 0.4 us)
Async XLA Ops:
  0.0 17.2 %collective-permute-start = (f32[1,1,2,2,2048]{4,3,2,1,0:T(2,128)}, f32[1,1,2,2,2048]{4,3,2,1,0:T(2,128)S(1)}, u32[]{:S(2)}, u32[]{:S(2)}) collective-permute-start(f32[1,1,2,2,2048]{4,3,2,1,0:T(2,128)} %param.7), channel_id=1, source_target_pairs={{0,1},{1,2},{2,3},{3,4},{4,5},{5,6},{6,7},{8,9},{9,10},{10,11},{11... | collective-permute-start | bytes 98312 | tf_op jit(solution)/shard_map/ppermute | solution.py:19
  10.5 10.9 %collective-permute-start.1 = (f32[1,1,2,2,2048]{4,3,2,1,0:T(2,128)}, f32[1,1,2,2,2048]{4,3,2,1,0:T(2,128)S(1)}, u32[]{:S(2)}, u32[]{:S(2)}) collective-permute-start(f32[1,1,2,2,2048]{4,3,2,1,0:T(2,128)} %param.7), channel_id=1, source_target_pairs={{1,0},{2,1},{3,2},{4,3},{5,4},{6,5},{7,6},{9,8},{10,9},{11,10},{12... | collective-permute-start | bytes 98312 | tf_op jit(solution)/shard_map/ppermute | solution.py:21
  13.5 3.7 %copy-start.4 = (s32[1,2560]{1,0:T(1,128)S(1)}, s32[1,2560]{1,0:T(1,128)}, u32[]{:S(2)}) copy-start(s32[1,2560]{1,0:T(1,128)} %param.8) | copy-start | bytes 30724
  13.5 8.0 %copy-start.6 = (f32[1,1,2,2,2048]{4,3,2,1,0:T(2,128)S(1)}, f32[1,1,2,2,2048]{4,3,2,1,0:T(2,128)}, u32[]{:S(2)}) copy-start(f32[1,1,2,2,2048]{4,3,2,1,0:T(2,128)} %param.7) | copy-start | bytes 98308
  13.5 14.9 %collective-permute-start.2 = (bf16[2,2,16,2048]{3,2,1,0:T(8,128)(2,1)S(1)}, bf16[2,2,16,2048]{3,2,1,0:T(8,128)(2,1)}, u32[]{:S(2)}, u32[]{:S(2)}) collective-permute-start(bf16[2,2,16,2048]{3,2,1,0:T(8,128)(2,1)S(1)} %slice_bitcast_fusion.1), channel_id=1, source_target_pairs={{1,0},{2,1},{3,2},{4,3},{5,4},{6,5},{7,6},{9,8},{10,9},{11,10},{12... | collective-permute-start | bytes 786440 | tf_op jit(solution)/shard_map/ppermute | solution.py:31
  21.8 1.9 %copy-start = (bf16[1,1,2,3,64,2048]{5,4,3,2,1,0:T(8,128)(2,1)S(1)}, bf16[1,1,2,3,64,2048]{5,4,3,2,1,0:T(8,128)(2,1)}, u32[]{:S(2)}) copy-start(bf16[1,1,2,3,64,2048]{5,4,3,2,1,0:T(8,128)(2,1)} %param.6) | copy-start | bytes 4718596
  29.8 1.6 %copy-start.3 = (bf16[2,64,64]{2,1,0:T(8,128)(2,1)S(1)}, bf16[2,64,64]{2,1,0:T(8,128)(2,1)}, u32[]{:S(2)}) copy-start(bf16[2,64,64]{2,1,0:T(8,128)(2,1)} %fusion.51) | copy-start | bytes 49156
  34.5 1.6 %copy-start.2 = (bf16[2,64,64]{2,1,0:T(8,128)(2,1)S(1)}, bf16[2,64,64]{2,1,0:T(8,128)(2,1)}, u32[]{:S(2)}) copy-start(bf16[2,64,64]{2,1,0:T(8,128)(2,1)} %fusion.49) | copy-start | bytes 49156
  60.9 17.1 %copy-start.1 = (bf16[1,1,2,64,80]{4,3,2,1,0:T(8,128)(2,1)S(1)}, bf16[1,1,2,64,80]{4,3,2,1,0:T(8,128)(2,1)}, u32[]{:S(2)}) copy-start(bf16[1,1,2,64,80]{4,3,2,1,0:T(8,128)(2,1)} %param.9) | copy-start | bytes 61444
  60.9 51.3 %all-to-all-start = ((bf16[1,2,2,2560]{1,2,0,3:T(2,128)(2,1)}), bf16[1,2,2,2560]{1,2,0,3:T(2,128)(2,1)S(1)}, u32[]{:S(2)}, u32[]{:S(2)}) async-start(bf16[1,2,2,2560]{1,2,0,3:T(2,128)(2,1)} %copy.91), calls=%async_computation | async-start | bytes 2621440 | tf_op jit(solution)/shard_map/all_to_all | solution.py:137
  122.7 7.0 %copy-start.5 = (s32[1,2560]{1,0:T(1,128)S(1)}, s32[1,2560]{1,0:T(1,128)}, u32[]{:S(2)}) copy-start(s32[1,2560]{1,0:T(1,128)} %param.8) | copy-start | bytes 30724
  123.7 15.5 %all-to-all-start.1 = ((bf16[64,2,40]{2,1,0:T(2,128)(2,1)}), bf16[64,2,40]{2,1,0:T(2,128)(2,1)S(1)}, u32[]{:S(2)}, u32[]{:S(2)}) async-start(bf16[64,2,40]{2,1,0:T(2,128)(2,1)} %copy.94), calls=%async_computation.1 | async-start | bytes 65536 | tf_op jit(solution)/shard_map/all_to_all | solution.py:139
where the time goes:
time: 153 us
  waiting for transfers between devices  49.3 us (32%)
  local copies, waits for them, and re-layouts  43.6 us (28%)
  starting transfers between devices  37.4 us (24%)
  matrix products  14 us (9%)
  other arithmetic  7.8 us (5%)
    all_to_all x1, waiting for transfers between devices, body(): lax.all_to_all(values, 'energy', split_axis=3, concat_axis=0, tiled=True)  34.2 us
    all_to_all x1, starting transfers between devices, body(): lax.all_to_all(values, 'energy', split_axis=3, concat_axis=0, tiled=True)  17.1 us
    another operation x1, local copies, waits for them, and re-layouts, element_values(): return jnp.stack([picked_real, picked_imag], axis=1).astype(jnp.bfloat16)  11.6 us
    ppermute x1, starting transfers between devices, padded_2(): lax.ppermute(tail, axis, [(i, (i + 1) % count) for i in range(ends)])  10.5 us
    all_to_all x1, waiting for transfers between devices, body(): lax.all_to_all(polarization, 'energy', split_axis=0, concat_axis=2, tiled...  9.51 us
    scatter x1, local copies, waits for them, and re-layouts, screen(): jnp.zeros((2, row_count * col_count), jnp.bfloat16).at[:, pattern_row]  7.46 us
    all_to_all x1, starting transfers between devices, body(): lax.all_to_all(polarization, 'energy', split_axis=0, concat_axis=2, tiled...  5.96 us
    gather x1, local copies, waits for them, and re-layouts, element_values(): picked_imag = jnp.take(joined_imag, pattern_row, axis=1)  5.71 us
  transfers between devices with their start and end apart: 5, of which 4 were waited for; matrix products, arithmetic and copies ran while one was open for 5% of the time, Pallas kernels for 0%

commit v1 on v0

--- a/solution.py
+++ b/solution.py
@@ -129,15 +129,27 @@
     return jnp.stack([first_real + second_real, first_imag + second_imag], axis=0)
 
 
+def own_lag(gathered):
+    energy_count = gathered.shape[0]
+    lag = lax.axis_index("energy")
+    lesser = gathered[:, 0].astype(jnp.float32)
+    greater = jnp.roll(gathered[:, 1].astype(jnp.float32), lag, axis=0)
+    inside = (jnp.arange(energy_count) >= lag)[:, None, None]
+    greater = jnp.where(inside, greater, 0.0)
+    real_sum = jnp.sum(lesser[:, 0] * greater[:, 0] - lesser[:, 1] * greater[:, 1], axis=0)
+    imag_sum = jnp.sum(lesser[:, 0] * greater[:, 1] + lesser[:, 1] * greater[:, 0], axis=0)
+    factor = 1.0 / math.sqrt(energy_count)
+    return (jnp.stack([real_sum, imag_sum], axis=0) * factor).astype(jnp.bfloat16)
+
+
 def body(green_slab, self_energy, pattern, screened):
     nearby = padded_2(self_energy, (("domain", 1),), 1)
     edge_block = green_slab[0, 0, :, 0:2, :EDGE, :]
     following = passed_along(edge_block, "domain", -1)
-    values = element_values(green_slab[0, 0], following, nearby[0], pattern[0])[None]
-    by_element = lax.all_to_all(values, "energy", split_axis=3, concat_axis=0, tiled=True)
-    polarization = lagged_sums(by_element)
-    per_energy = lax.all_to_all(polarization, "energy", split_axis=0, concat_axis=2, tiled=True)
-    result = screen(per_energy[0], pattern[0], screened[0, 0])
+    values = element_values(green_slab[0, 0], following, nearby[0], pattern[0])
+    gathered = lax.all_gather(values, "energy")
+    polarization = own_lag(gathered)
+    result = screen(polarization, pattern[0], screened[0, 0])
     return result[None, None]
 
 

time: 153 us -> 205 us (1.34)
  waiting for transfers between devices: 49.3 us -> 129 us
  starting transfers between devices: 37.4 us -> 14.4 us
  local copies, waits for them, and re-layouts: 43.6 us -> 27.1 us
  between operations: 0.4 us -> 13.7 us
    all_gather x0 -> x1, waiting for transfers between devices: none -> 123 us  [body(): gathered = lax.all_gather(values, 'energy')]
    all_to_all x2 -> x0, waiting for transfers between devices: 43.7 us -> none  [the longest x1 34.2 us: body(): lax.all_to_all(values, 'energy', split_axis=3, concat_axis=0, tiled=True)]
    all_to_all x2 -> x0, starting transfers between devices: 23 us -> none  [the longest x1 17.1 us: body(): lax.all_to_all(values, 'energy', split_axis=3, concat_axis=0, tiled=True)]
    another operation x1 -> x2, local copies, waits for them, and re-layouts: 11.6 us -> 0.94 us  [element_values(): return jnp.stack([picked_real, picked_imag], axis=1).astype(jnp.bfloat16)]
    reshape x1 -> x0, local copies, waits for them, and re-layouts: 4.5 us -> none  [lagged_sums(): padded.reshape(energy_count * (2 * energy_count + 1), 2 * column_count)]
    concatenate x1 -> x0, other arithmetic: 2.99 us -> none  [lagged_sums(): joined = jnp.concatenate([real_part, imag_part], axis=2)]
    slice x0 -> x1, local copies, waits for them, and re-layouts: none -> 2.18 us  [own_lag(): lesser = gathered[:, 0].astype(jnp.float32)]
  transfers between devices with their start and end apart: 5 -> 4, of which waited for: 4 -> 3; matrix products, arithmetic and copies ran while one was open for 5% -> 4% of each run, Pallas kernels for 0% -> 0%
where the time goes in v1:
time: 205 us; the launch traced here: 204 us
  waiting for transfers between devices  129 us (63%)
  local copies, waits for them, and re-layouts  27.1 us (13%)
  starting transfers between devices  14.4 us (7%)
  between operations  13.7 us (7%)
  matrix products  12.8 us (6%)
  other arithmetic  6.8 us (3%)
    all_gather x1, waiting for transfers between devices, body(): gathered = lax.all_gather(values, 'energy')  123 us
    ppermute x1, starting transfers between devices, padded_2(): lax.ppermute(tail, axis, [(i, (i + 1) % count) for i in range(ends)])  10.5 us
    scatter x1, local copies, waits for them, and re-layouts, screen(): jnp.zeros((2, row_count * col_count), jnp.bfloat16).at[:, pattern_row]  7.46 us
    gather x1, local copies, waits for them, and re-layouts, element_values(): picked_imag = jnp.take(joined_imag, pattern_row, axis=1)  6.12 us
    gather x1, local copies, waits for them, and re-layouts, element_values(): picked_real = jnp.take(joined_real, pattern_row, axis=1)  5.06 us
  transfers between devices with their start and end apart: 4, of which 3 were waited for; matrix products, arithmetic and copies ran while one was open for 4% of the time, Pallas kernels for 0%

profile of v1, /device:TPU:7, one launch (start us, length us, event | category | flops | bytes accessed | tf_op | source)
XLA Modules:
  0.0 203.6 jit_solution(8327814624986610543)
XLA Ops:
  6.5 10.5 %collective-permute-start = (f32[1,1,2,2,2048]{4,3,2,1,0:T(2,128)}, f32[1,1,2,2,2048]{4,3,2,1,0:T(2,128)S(1)}, u32[]{:S(2)}, u32[]{:S(2)}) collective-permute-start(f32[1,1,2,2,2048]{4,3,2,1,0:T(2,128)} %param.7), channel_id=1, source_target_pairs={{0,1},{1,2},{2,3},{3,4},{4,5},{5,6},{6,7},{8,9},{9,10},{10,11},{11... | collective-permute-start | bytes 98312 | tf_op jit(solution)/shard_map/ppermute | solution.py:19
  17.1 1.9 collective-permute-start.1
  19.0 1.0 slice_bitcast_fusion
  20.0 1.9 collective-permute-start.2
  21.9 0.7 reduce.3
  22.7 0.0 copy-start.5
  22.7 0.0 copy-start
  22.7 1.9 bitcast_convert_fusion.3
  24.6 0.0 collective-permute-done
  24.6 3.4 %collective-permute-done.1 = f32[1,1,2,2,2048]{4,3,2,1,0:T(2,128)S(1)} collective-permute-done((f32[1,1,2,2,2048]{4,3,2,1,0:T(2,128)}, f32[1,1,2,2,2048]{4,3,2,1,0:T(2,128)S(1)}, u32[]{:S(2)}, u32[]{:S(2)}) %collective-permute-start.1) | collective-permute-done | bytes 32800 | tf_op jit(solution)/shard_map/ppermute | solution.py:21
  28.1 0.1 fusion.118
  28.1 0.1 copy_bitcast_fusion.2
  28.3 0.7 fusion.53
  29.0 0.7 fusion.52
  29.7 1.3 fusion.51
  30.9 1.3 fusion.49
  32.3 2.6 %collective-permute-done.2 = bf16[2,2,16,2048]{3,2,1,0:T(8,128)(2,1)} collective-permute-done((bf16[2,2,16,2048]{3,2,1,0:T(8,128)(2,1)S(1)}, bf16[2,2,16,2048]{3,2,1,0:T(8,128)(2,1)}, u32[]{:S(2)}, u32[]{:S(2)}) %collective-permute-start.2) | collective-permute-done | bytes 262176 | tf_op jit(solution)/shard_map/ppermute | solution.py:31
  34.9 1.4 fusion.62
  36.3 1.4 fusion.65
  37.7 0.1 copy.56
  37.9 1.4 fusion.63
  39.3 0.0 copy-start.2
  39.3 1.4 fusion.61
  40.8 0.1 copy.58
  40.9 0.0 copy-done.3
  40.9 0.1 pad_maximum_fusion
  41.0 0.6 copy.74
  41.6 0.1 pad_maximum_fusion.1
  41.7 0.6 copy.75
  42.3 5.1 %gather_fusion = bf16[2560,2]{1,0:T(8,128)(2,1)S(1)} fusion(bf16[2,5120]{0,1:T(8,128)(2,1)S(1)} %bitcast.128, s32[3072]{0:T(1024)S(1)} %pad_clamp_fusion), kind=kCustom, calls=%fused_computation.clone | custom fusion | bytes 30720 | tf_op jit(solution)/shard_map/jit(_take)/gather | solution.py:79
  47.4 6.1 %gather_fusion.1 = bf16[2560,2]{1,0:T(8,128)(2,1)} fusion(bf16[2,5120]{0,1:T(8,128)(2,1)S(1)} %bitcast.129, s32[3072]{0:T(1024)S(1)} %pad_clamp_fusion), kind=kCustom, calls=%fused_computation.1.clone | custom fusion | bytes 30720 | tf_op jit(solution)/shard_map/jit(_take)/gather | solution.py:80
  53.5 2.3 %fusion.72 = (bf16[1,2,1,2560]{1,3,2,0:T(8,128)(2,1)S(1)}, bf16[1,2,1,2560]{1,3,2,0:T(8,128)(2,1)S(1)}) fusion(bf16[2560,2]{1,0:T(8,128)(2,1)S(1)} %gather_fusion, pred[2560]{0:T(1024)(128)(4,1)S(1)} %compare_and_fusion, bf16[2560,2]{1,0:T(8,128)(2,1)} %gather_fusion.1), kind=kLoop, calls=%fused_computation.94 | loop fusion | flops 10240 | bytes 43520 | tf_op jit(solution)/shard_map/stack | solution.py:81
  55.9 0.5 copy.60
  56.3 0.5 copy.61
  56.8 0.7 pad_maximum_fusion.2
  57.5 0.0 all-gather.2.cloned.1.call-update
  57.6 122.8 %all-gather.2.cloned.1.call-done = bf16[64,2,2,2560]{3,2,1,0:T(2,128)(2,1)} async-done(((bf16[1,2,2,2560]{3,2,1,0:T(2,128)(2,1)}), bf16[64,2,2,2560]{3,2,1,0:T(2,128)(2,1)}) %all-gather.2.cloned.1.call-update) | async-done | bytes 1310736 | tf_op jit(solution)/shard_map/all_gather | solution.py:150
  180.4 2.2 %fusion.117 = (bf16[64,1,2,2560]{3,2,1,0:T(2,128)(2,1)S(1)}, bf16[64,1,2,2560]{3,2,1,0:T(2,128)(2,1)S(1)}) fusion(bf16[64,2,2,2560]{3,2,1,0:T(2,128)(2,1)} %all-gather.2.cloned.1.call-done), kind=kLoop, calls=%fused_computation.161 | loop fusion | bytes 2621440 | tf_op jit(solution)/shard_map/slice | solution.py:135
  182.6 0.1 fusion.75
  182.7 0.1 copy.86
  182.8 0.5 convert_select_fusion
  183.3 0.2 subtract_reduce_fusion
  183.7 0.4 copy.64
  184.1 7.5 %scatter_custom_fusion = bf16[2,5120]{0,1:T(8,128)(2,1)S(1)} fusion(s32[2560]{0:T(1024)S(1)} %fusion.105, bf16[2560,2]{1,0:T(8,128)(2,1)S(1)} %copy.64, bf16[]{:T(256)} %constant.38.clone.1), kind=kCustom, calls=%fused_computation.102 | custom fusion | bytes 20482 | tf_op jit(solution)/shard_map/scatter | solution.py:110
  191.5 1.2 slice_reduce_fusion.1
  192.8 0.1 squeeze.72
  192.9 0.1 squeeze.74
  193.0 0.2 fusion.93
  193.2 0.2 fusion.89
  193.4 0.2 fusion.66
  193.7 0.2 fusion.83
  193.9 0.2 fusion.87
  194.1 0.1 fusion.115
  194.2 0.1 fusion.116
  194.4 0.2 fusion.67
  194.6 0.1 fusion.59
  194.7 0.1 fusion.58
  194.9 0.2 fusion.103
  195.1 0.2 fusion.99
  195.2 0.2 convolution_subtract_fusion.1
  195.4 0.2 convolution_add_fusion
  195.6 0.2 fusion.57
  195.8 0.2 fusion.55
  196.0 0.7 copy.65
  (22 shorter events, 0.3 us)
Async XLA Ops:
  6.5 173.9 %all-gather.2.cloned.1.call-start = ((), (), s32[]{:S(2)}) async-start(), calls=%async_computation | async-start | bytes 1331200 | tf_op jit(solution)/shard_map/all_gather | solution.py:150
  6.5 18.1 %collective-permute-start = (f32[1,1,2,2,2048]{4,3,2,1,0:T(2,128)}, f32[1,1,2,2,2048]{4,3,2,1,0:T(2,128)S(1)}, u32[]{:S(2)}, u32[]{:S(2)}) collective-permute-start(f32[1,1,2,2,2048]{4,3,2,1,0:T(2,128)} %param.7), channel_id=1, source_target_pairs={{0,1},{1,2},{2,3},{3,4},{4,5},{5,6},{6,7},{8,9},{9,10},{10,11},{11... | collective-permute-start | bytes 98312 | tf_op jit(solution)/shard_map/ppermute | solution.py:19
  17.1 10.9 %collective-permute-start.1 = (f32[1,1,2,2,2048]{4,3,2,1,0:T(2,128)}, f32[1,1,2,2,2048]{4,3,2,1,0:T(2,128)S(1)}, u32[]{:S(2)}, u32[]{:S(2)}) collective-permute-start(f32[1,1,2,2,2048]{4,3,2,1,0:T(2,128)} %param.7), channel_id=1, source_target_pairs={{1,0},{2,1},{3,2},{4,3},{5,4},{6,5},{7,6},{9,8},{10,9},{11,10},{12... | collective-permute-start | bytes 98312 | tf_op jit(solution)/shard_map/ppermute | solution.py:21
  20.0 14.9 %collective-permute-start.2 = (bf16[2,2,16,2048]{3,2,1,0:T(8,128)(2,1)S(1)}, bf16[2,2,16,2048]{3,2,1,0:T(8,128)(2,1)}, u32[]{:S(2)}, u32[]{:S(2)}) collective-permute-start(bf16[2,2,16,2048]{3,2,1,0:T(8,128)(2,1)S(1)} %slice_bitcast_fusion), channel_id=1, source_target_pairs={{1,0},{2,1},{3,2},{4,3},{5,4},{6,5},{7,6},{9,8},{10,9},{11,10},{12... | collective-permute-start | bytes 786440 | tf_op jit(solution)/shard_map/ppermute | solution.py:31
  22.7 5.3 %copy-start.5 = (f32[1,1,2,2,2048]{4,3,2,1,0:T(2,128)S(1)}, f32[1,1,2,2,2048]{4,3,2,1,0:T(2,128)}, u32[]{:S(2)}) copy-start(f32[1,1,2,2,2048]{4,3,2,1,0:T(2,128)} %param.7) | copy-start | bytes 98308
  22.7 5.6 %copy-start = (bf16[1,1,2,3,64,2048]{5,4,3,2,1,0:T(8,128)(2,1)S(1)}, bf16[1,1,2,3,64,2048]{5,4,3,2,1,0:T(8,128)(2,1)}, u32[]{:S(2)}) copy-start(bf16[1,1,2,3,64,2048]{5,4,3,2,1,0:T(8,128)(2,1)} %param.6) | copy-start | bytes 4718596
  39.3 1.6 copy-start.3
  39.3 2.3 %copy-start.2 = (bf16[2,64,64]{2,1,0:T(8,128)(2,1)S(1)}, bf16[2,64,64]{2,1,0:T(8,128)(2,1)}, u32[]{:S(2)}) copy-start(bf16[2,64,64]{2,1,0:T(8,128)(2,1)} %fusion.51) | copy-start | bytes 49156
  53.5 4.0 %copy-start.4 = (s32[1,2560]{1,0:T(1,128)S(1)}, s32[1,2560]{1,0:T(1,128)}, u32[]{:S(2)}) copy-start(s32[1,2560]{1,0:T(1,128)} %param.8) | copy-start | bytes 30724
  53.5 4.1 %copy-start.1 = (bf16[1,1,2,64,80]{4,3,2,1,0:T(8,128)(2,1)S(1)}, bf16[1,1,2,64,80]{4,3,2,1,0:T(8,128)(2,1)}, u32[]{:S(2)}) copy-start(bf16[1,1,2,64,80]{4,3,2,1,0:T(8,128)(2,1)} %param.9) | copy-start | bytes 61444
Sparse Core Ops, SparseCore 0:
  57.6 122.7 all-gather.1

commit v2 on v0

--- a/solution.py
+++ b/solution.py
@@ -133,8 +133,10 @@
     nearby = padded_2(self_energy, (("domain", 1),), 1)
     edge_block = green_slab[0, 0, :, 0:2, :EDGE, :]
     following = passed_along(edge_block, "domain", -1)
-    values = element_values(green_slab[0, 0], following, nearby[0], pattern[0])[None]
-    by_element = lax.all_to_all(values, "energy", split_axis=3, concat_axis=0, tiled=True)
+    values = element_values(green_slab[0, 0], following, nearby[0], pattern[0])
+    chunks = lax.axis_size("energy")
+    values = values.reshape(2, 2, chunks, -1).transpose(2, 0, 1, 3)
+    by_element = lax.all_to_all(values, "energy", split_axis=0, concat_axis=0, tiled=True)
     polarization = lagged_sums(by_element)
     per_energy = lax.all_to_all(polarization, "energy", split_axis=0, concat_axis=2, tiled=True)
     result = screen(per_energy[0], pattern[0], screened[0, 0])

time: 153 us -> 117 us (0.76)
  waiting for transfers between devices: 49.3 us -> 25.3 us
  local copies, waits for them, and re-layouts: 43.6 us -> 32.5 us
  starting transfers between devices: 37.4 us -> 35.7 us
    all_to_all x1, waiting for transfers between devices: 34.2 us -> 10.1 us  [body(): lax.all_to_all(values, 'energy', split_axis=0, concat_axis=0, tiled=True)]
    another operation x1 -> x2, local copies, waits for them, and re-layouts: 11.6 us -> 1.67 us  [element_values(): return jnp.stack([picked_real, picked_imag], axis=1).astype(jnp.bfloat16)]
    all_to_all x1, starting transfers between devices: 5.96 us -> 4.42 us  [body(): lax.all_to_all(polarization, 'energy', split_axis=0, concat_axis=2, tiled...]
  transfers between devices with their start and end apart: 5 -> 5, of which waited for: 4 -> 4; matrix products, arithmetic and copies ran while one was open for 5% -> 7% of each run, Pallas kernels for 0% -> 0%
where the time goes in v2:
time: 117 us; the launch traced here: 116 us
  starting transfers between devices  35.7 us (31%)
  local copies, waits for them, and re-layouts  32.5 us (28%)
  waiting for transfers between devices  25.3 us (22%)
  matrix products  14 us (12%)
  other arithmetic  8.32 us (7%)
    all_to_all x1, starting transfers between devices, body(): lax.all_to_all(values, 'energy', split_axis=0, concat_axis=0, tiled=True)  16.9 us
    ppermute x1, starting transfers between devices, padded_2(): lax.ppermute(tail, axis, [(i, (i + 1) % count) for i in range(ends)])  10.5 us
    all_to_all x1, waiting for transfers between devices, body(): lax.all_to_all(values, 'energy', split_axis=0, concat_axis=0, tiled=True)  10.1 us
    all_to_all x1, waiting for transfers between devices, body(): lax.all_to_all(polarization, 'energy', split_axis=0, concat_axis=2, tiled...  9.61 us
    scatter x1, local copies, waits for them, and re-layouts, screen(): jnp.zeros((2, row_count * col_count), jnp.bfloat16).at[:, pattern_row]  7.46 us
    gather x1, local copies, waits for them, and re-layouts, element_values(): picked_imag = jnp.take(joined_imag, pattern_row, axis=1)  5.7 us
    gather x1, local copies, waits for them, and re-layouts, element_values(): picked_real = jnp.take(joined_real, pattern_row, axis=1)  5.07 us
    reshape x1, local copies, waits for them, and re-layouts, lagged_sums(): padded.reshape(energy_count * (2 * energy_count + 1), 2 * column_count)  4.5 us
  transfers between devices with their start and end apart: 5, of which 4 were waited for; matrix products, arithmetic and copies ran while one was open for 7% of the time, Pallas kernels for 0%

profile of v2, /device:TPU:7, one launch (start us, length us, event | category | flops | bytes accessed | tf_op | source)
XLA Modules:
  0.0 116.3 jit_solution(4712106516777002500)
XLA Ops:
  0.0 10.5 %collective-permute-start = (f32[1,1,2,2,2048]{4,3,2,1,0:T(2,128)}, f32[1,1,2,2,2048]{4,3,2,1,0:T(2,128)S(1)}, u32[]{:S(2)}, u32[]{:S(2)}) collective-permute-start(f32[1,1,2,2,2048]{4,3,2,1,0:T(2,128)} %param.7), channel_id=1, source_target_pairs={{0,1},{1,2},{2,3},{3,4},{4,5},{5,6},{6,7},{8,9},{9,10},{10,11},{11... | collective-permute-start | bytes 98312 | tf_op jit(solution)/shard_map/ppermute | solution.py:19
  10.5 1.9 %collective-permute-start.1 = (f32[1,1,2,2,2048]{4,3,2,1,0:T(2,128)}, f32[1,1,2,2,2048]{4,3,2,1,0:T(2,128)S(1)}, u32[]{:S(2)}, u32[]{:S(2)}) collective-permute-start(f32[1,1,2,2,2048]{4,3,2,1,0:T(2,128)} %param.7), channel_id=1, source_target_pairs={{1,0},{2,1},{3,2},{4,3},{5,4},{6,5},{7,6},{9,8},{10,9},{11,10},{12... | collective-permute-start | bytes 98312 | tf_op jit(solution)/shard_map/ppermute | solution.py:21
  12.5 1.0 slice_bitcast_fusion.1
  13.5 1.9 %collective-permute-start.2 = (bf16[2,2,16,2048]{3,2,1,0:T(8,128)(2,1)S(1)}, bf16[2,2,16,2048]{3,2,1,0:T(8,128)(2,1)}, u32[]{:S(2)}, u32[]{:S(2)}) collective-permute-start(bf16[2,2,16,2048]{3,2,1,0:T(8,128)(2,1)S(1)} %slice_bitcast_fusion.1), channel_id=1, source_target_pairs={{1,0},{2,1},{3,2},{4,3},{5,4},{6,5},{7,6},{9,8},{10,9},{11,10},{12... | collective-permute-start | bytes 786440 | tf_op jit(solution)/shard_map/ppermute | solution.py:31
  15.4 1.7 %bitcast_convert_fusion.3 = (f32[3,64,2048]{2,1,0:T(8,128)S(1)}, f32[3,64,2048]{2,1,0:T(8,128)S(1)}) fusion(bf16[1,1,2,3,64,2048]{5,4,3,2,1,0:T(8,128)(2,1)} %param.6), kind=kLoop, calls=%fused_computation.96 | loop fusion | flops 786432 | bytes 4718592 | tf_op jit(solution)/shard_map/convert_element_type | solution.py:69
  17.3 4.2 %collective-permute-done.1 = f32[1,1,2,2,2048]{4,3,2,1,0:T(2,128)S(1)} collective-permute-done((f32[1,1,2,2,2048]{4,3,2,1,0:T(2,128)}, f32[1,1,2,2,2048]{4,3,2,1,0:T(2,128)S(1)}, u32[]{:S(2)}, u32[]{:S(2)}) %collective-permute-start.1) | collective-permute-done | bytes 32800 | tf_op jit(solution)/shard_map/ppermute | solution.py:21
  21.8 1.9 %fusion.53 = f32[2,64,64]{2,1,0:T(8,128)S(1)} fusion(f32[2,3,2048]{2,1,0:T(4,128)S(1)} %copy.55, f32[3,64,2048]{2,1,0:T(8,128)S(1)} %get-tuple-element.9, f32[2,3,2048]{2,1,0:T(4,128)S(1)} %copy.54, f32[3,64,2048]{2,1,0:T(8,128)S(1)} %get-tuple-element.8, bf16[1,1,2,3,64,2048]{5,4,3,2,1,0:T(8,128)(2,1)} %param.6), kind=kOutput, calls=%fused_computation.68 | convolution fusion | flops 104595456 | bytes 4063232 | tf_op jit(solution)/shard_map/qjrb,jsb->qrs/dot_general | solution.py:40
  23.7 0.7 fusion.52
  24.4 1.3 %fusion.51 = bf16[2,64,64]{2,1,0:T(8,128)(2,1)} fusion(f32[2,64,64]{2,1,0:T(8,128)S(1)} %fusion.53, f32[2,3,2048]{2,1,0:T(4,128)S(1)} %copy.55, f32[3,64,2048]{2,1,0:T(8,128)S(1)} %get-tuple-element.9, f32[2,3,2048]{2,1,0:T(4,128)S(1)} %copy.54, f32[3,64,2048]{2,1,0:T(8,128)S(1)} %get-tuple-element.8, bf16[1,1,2,3,64,2048]{5,4,3,2,1,0:T(8,128)(2,1)S(1)} %copy-done), kind=kOutput, calls=%fused_computation.66 | convolution fusion | flops 104611840 | bytes 4145152 | tf_op jit(solution)/shard_map/qjrb,jsb->qrs/dot_general | solution.py:38
  25.6 1.3 %fusion.49 = bf16[2,64,64]{2,1,0:T(8,128)(2,1)} fusion(f32[2,64,64]{2,1,0:T(8,128)S(1)} %fusion.52, f32[2,3,2048]{2,1,0:T(4,128)S(1)} %copy.55, f32[3,64,2048]{2,1,0:T(8,128)S(1)} %get-tuple-element.9, f32[2,3,2048]{2,1,0:T(4,128)S(1)} %copy.54, f32[3,64,2048]{2,1,0:T(8,128)S(1)} %get-tuple-element.8, bf16[1,1,2,3,64,2048]{5,4,3,2,1,0:T(8,128)(2,1)S(1)} %copy-done), kind=kOutput, calls=%fused_computation.64 | convolution fusion | flops 104611840 | bytes 4145152 | tf_op jit(solution)/shard_map/qjrb,jsb->qrs/dot_general | solution.py:37
  27.0 1.4 %collective-permute-done.2 = bf16[2,2,16,2048]{3,2,1,0:T(8,128)(2,1)} collective-permute-done((bf16[2,2,16,2048]{3,2,1,0:T(8,128)(2,1)S(1)}, bf16[2,2,16,2048]{3,2,1,0:T(8,128)(2,1)}, u32[]{:S(2)}, u32[]{:S(2)}) %collective-permute-start.2) | collective-permute-done | bytes 262176 | tf_op jit(solution)/shard_map/ppermute | solution.py:31
  28.4 1.4 %fusion.63 = f32[2,64,16]{1,2,0:T(8,128)S(1)} fusion(f32[2,3,2048]{2,1,0:T(4,128)S(1)} %copy.55, f32[3,64,2048]{2,1,0:T(8,128)S(1)} %get-tuple-element.9, f32[2,3,2048]{2,1,0:T(4,128)S(1)} %copy.54, f32[3,64,2048]{2,1,0:T(8,128)S(1)} %get-tuple-element.8, bf16[2,2,16,2048]{3,2,1,0:T(8,128)(2,1)} %collective-permute-done.2), kind=kOutput, calls=%fused_computation.84 | convolution fusion | flops 20709376 | bytes 3383296 | tf_op jit(solution)/shard_map/qjrb,jsb->qrs/dot_general | solution.py:40
  29.8 1.5 %fusion.61 = bf16[2,64,16]{1,2,0:T(8,128)(2,1)S(1)} fusion(f32[2,64,16]{1,2,0:T(8,128)S(1)} %fusion.63, f32[2,3,2048]{2,1,0:T(4,128)S(1)} %copy.55, f32[3,64,2048]{2,1,0:T(8,128)S(1)} %get-tuple-element.9, f32[2,3,2048]{2,1,0:T(4,128)S(1)} %copy.54, f32[3,64,2048]{2,1,0:T(8,128)S(1)} %get-tuple-element.8, bf16[2,2,16,2048]{3,2,1,0:T(8,128)(2,1)} %collective-permute-done.2), kind=kOutput, calls=%fused_computation.82 | convolution fusion | flops 20713472 | bytes 3387392 | tf_op jit(solution)/shard_map/qjrb,jsb->qrs/dot_general | solution.py:38
  31.2 0.1 copy.58
  31.4 0.1 pad_maximum_fusion.1
  31.5 1.6 %copy.77 = bf16[2,64,80]{0,2,1:T(8,128)(2,1)} copy(bf16[2,64,80]{2,1,0:T(8,128)(2,1)S(1)} %pad_maximum_fusion.1) | data formatting | bytes 40960 | tf_op jit(solution)/shard_map/reshape | solution.py:78
  33.1 1.4 %fusion.62 = f32[2,64,16]{1,2,0:T(8,128)S(1)} fusion(f32[2,3,2048]{2,1,0:T(4,128)S(1)} %copy.55, f32[3,64,2048]{2,1,0:T(8,128)S(1)} %get-tuple-element.9, f32[2,3,2048]{2,1,0:T(4,128)S(1)} %copy.54, f32[3,64,2048]{2,1,0:T(8,128)S(1)} %get-tuple-element.8, bf16[2,2,16,2048]{3,2,1,0:T(8,128)(2,1)} %collective-permute-done.2), kind=kOutput, calls=%fused_computation.83 | convolution fusion | flops 20709376 | bytes 3383296 | tf_op jit(solution)/shard_map/qjrb,jsb->qrs/dot_general | solution.py:37
  34.5 1.5 %fusion.65 = bf16[2,64,16]{1,2,0:T(8,128)(2,1)S(1)} fusion(f32[2,64,16]{1,2,0:T(8,128)S(1)} %fusion.62, f32[2,3,2048]{2,1,0:T(4,128)S(1)} %copy.55, f32[3,64,2048]{2,1,0:T(8,128)S(1)} %get-tuple-element.9, f32[2,3,2048]{2,1,0:T(4,128)S(1)} %copy.54, f32[3,64,2048]{2,1,0:T(8,128)S(1)} %get-tuple-element.8, bf16[2,2,16,2048]{3,2,1,0:T(8,128)(2,1)} %collective-permute-done.2), kind=kOutput, calls=%fused_computation.86 | convolution fusion | flops 20713472 | bytes 3387392 | tf_op jit(solution)/shard_map/qjrb,jsb->qrs/dot_general | solution.py:35
  36.0 0.1 copy.56
  36.1 0.1 pad_maximum_fusion
  36.2 0.6 copy.76
  36.8 5.7 %gather_fusion.1 = bf16[2560,2]{1,0:T(8,128)(2,1)S(1)} fusion(bf16[2,5120]{0,1:T(8,128)(2,1)} %bitcast.143, s32[3072]{0:T(1024)S(1)} %pad_clamp_fusion), kind=kCustom, calls=%fused_computation.1.clone | custom fusion | bytes 30720 | tf_op jit(solution)/shard_map/jit(_take)/gather | solution.py:80
  42.5 5.1 %gather_fusion = bf16[2560,2]{1,0:T(8,128)(2,1)S(1)} fusion(bf16[2,5120]{0,1:T(8,128)(2,1)S(1)} %bitcast.144, s32[3072]{0:T(1024)S(1)} %pad_clamp_fusion), kind=kCustom, calls=%fused_computation.clone | custom fusion | bytes 30720 | tf_op jit(solution)/shard_map/jit(_take)/gather | solution.py:79
  47.6 1.4 %bitcast_convert_fusion.1 = (bf16[2,2560]{0,1:T(8,128)(2,1)S(1)}, bf16[2,2560]{0,1:T(8,128)(2,1)S(1)}) fusion(bf16[2560,2]{1,0:T(8,128)(2,1)S(1)} %gather_fusion, pred[2560]{0:T(1024)(128)(4,1)S(1)} %compare_and_fusion, bf16[2560,2]{1,0:T(8,128)(2,1)S(1)} %gather_fusion.1), kind=kLoop, calls=%fused_computation.60 | loop fusion | flops 10240 | bytes 43520 | tf_op jit(solution)/shard_map/convert.5
  49.0 0.8 copy.60
  49.8 0.8 copy.61
  50.6 0.8 maximum_bitcast_fusion.1
  51.5 16.9 %all-to-all-start = ((bf16[64,2,2,40]{3,2,1,0:T(2,128)(2,1)}), bf16[64,2,2,40]{3,2,1,0:T(2,128)(2,1)S(1)}, u32[]{:S(2)}, u32[]{:S(2)}) async-start(bf16[64,2,2,40]{3,2,1,0:T(2,128)(2,1)} %maximum_bitcast_fusion.1), calls=%async_computation | async-start | bytes 131072 | tf_op jit(solution)/shard_map/all_to_all | solution.py:139
  68.4 10.1 %all-to-all-done = bf16[64,2,2,40]{3,2,1,0:T(2,128)(2,1)S(1)} async-done(((bf16[64,2,2,40]{3,2,1,0:T(2,128)(2,1)}), bf16[64,2,2,40]{3,2,1,0:T(2,128)(2,1)S(1)}, u32[]{:S(2)}, u32[]{:S(2)}) %all-to-all-start) | async-done | bytes 20512 | tf_op jit(solution)/shard_map/all_to_all | solution.py:139
  78.6 0.1 copy.81
  78.7 0.1 rev.3
  78.8 0.1 copy.80
  78.9 0.7 multiply_subtract_fusion
  79.7 3.0 %select_maximum_fusion = f32[64,129,80]{1,0,2:T(8,128)} fusion(f32[64,64,40]{1,0,2:T(8,128)S(1)} %get-tuple-element.13, f32[64,64,40]{1,0,2:T(8,128)S(1)} %get-tuple-element.12), kind=kLoop, calls=%fused_computation.3 | loop fusion | flops 2641920 | bytes 3952640 | tf_op jit(solution)/shard_map/concatenate | solution.py:95
  82.7 4.5 %reshape.90 = f32[8256,80]{0,1:T(8,128)S(1)} reshape(f32[64,129,80]{1,0,2:T(8,128)} %select_maximum_fusion) | data formatting | bytes 5283840 | tf_op jit(solution)/shard_map/reshape | solution.py:97
  87.2 0.2 slice_bitcast_fusion
  87.4 0.5 copy.82
  87.9 0.3 bitcast_reduce_fusion
  88.2 0.7 copy.64
  88.9 4.4 %all-to-all-start.1 = ((bf16[64,2,40]{2,1,0:T(2,128)(2,1)}), bf16[64,2,40]{2,1,0:T(2,128)(2,1)S(1)}, u32[]{:S(2)}, u32[]{:S(2)}) async-start(bf16[64,2,40]{2,1,0:T(2,128)(2,1)} %copy.64), calls=%async_computation.1 | async-start | bytes 65536 | tf_op jit(solution)/shard_map/all_to_all | solution.py:141
  93.4 9.6 %all-to-all-done.1 = bf16[64,2,40]{2,1,0:T(2,128)(2,1)S(1)} async-done(((bf16[64,2,40]{2,1,0:T(2,128)(2,1)}), bf16[64,2,40]{2,1,0:T(2,128)(2,1)S(1)}, u32[]{:S(2)}, u32[]{:S(2)}) %all-to-all-start.1) | async-done | bytes 10272 | tf_op jit(solution)/shard_map/all_to_all | solution.py:141
  103.0 0.1 reshape.111
  103.1 0.4 copy.66
  103.6 7.5 %scatter_custom_fusion = bf16[2,5120]{0,1:T(8,128)(2,1)S(1)} fusion(s32[2560]{0:T(1024)S(1)} %fusion.101, bf16[2560,2]{1,0:T(8,128)(2,1)S(1)} %copy.66, bf16[]{:T(256)} %constant.1.clone.1), kind=kCustom, calls=%fused_computation.97 | custom fusion | bytes 20482 | tf_op jit(solution)/shard_map/scatter | solution.py:110
  111.0 1.2 %slice_reduce_fusion.1 = (bf16[5120]{0:T(1024)(128)(2,1)S(1)}, bf16[5120]{0:T(1024)(128)(2,1)S(1)}) fusion(bf16[2,5120]{0,1:T(8,128)(2,1)S(1)} %scatter_custom_fusion), kind=kLoop, calls=%fused_computation.58 | loop fusion | bytes 40960 | tf_op jit(solution)/shard_map/slice | solution.py:114
  112.3 0.1 squeeze.68
  112.4 0.1 fusion.111
  112.5 0.1 squeeze.70
  112.6 0.1 fusion.110
  112.7 0.2 fusion.89
  113.0 0.2 fusion.85
  113.2 0.2 fusion.66
  113.4 0.2 fusion.83
  113.7 0.2 fusion.79
  113.9 0.1 fusion.58
  114.0 0.2 fusion.99
  114.2 0.1 fusion.59
  114.3 0.2 fusion.95
  114.5 0.2 convolution_subtract_fusion.1
  114.7 0.2 fusion.67
  114.9 0.2 convolution_add_fusion
  115.1 0.2 fusion.57
  115.3 0.2 fusion.55
  115.6 0.7 copy.67
  (34 shorter events, 0.6 us)
Async XLA Ops:
  0.0 17.2 %collective-permute-start = (f32[1,1,2,2,2048]{4,3,2,1,0:T(2,128)}, f32[1,1,2,2,2048]{4,3,2,1,0:T(2,128)S(1)}, u32[]{:S(2)}, u32[]{:S(2)}) collective-permute-start(f32[1,1,2,2,2048]{4,3,2,1,0:T(2,128)} %param.7), channel_id=1, source_target_pairs={{0,1},{1,2},{2,3},{3,4},{4,5},{5,6},{6,7},{8,9},{9,10},{10,11},{11... | collective-permute-start | bytes 98312 | tf_op jit(solution)/shard_map/ppermute | solution.py:19
  10.5 10.9 %collective-permute-start.1 = (f32[1,1,2,2,2048]{4,3,2,1,0:T(2,128)}, f32[1,1,2,2,2048]{4,3,2,1,0:T(2,128)S(1)}, u32[]{:S(2)}, u32[]{:S(2)}) collective-permute-start(f32[1,1,2,2,2048]{4,3,2,1,0:T(2,128)} %param.7), channel_id=1, source_target_pairs={{1,0},{2,1},{3,2},{4,3},{5,4},{6,5},{7,6},{9,8},{10,9},{11,10},{12... | collective-permute-start | bytes 98312 | tf_op jit(solution)/shard_map/ppermute | solution.py:21
  13.5 3.7 %copy-start.4 = (s32[1,2560]{1,0:T(1,128)S(1)}, s32[1,2560]{1,0:T(1,128)}, u32[]{:S(2)}) copy-start(s32[1,2560]{1,0:T(1,128)} %param.8) | copy-start | bytes 30724
  13.5 8.0 %copy-start.6 = (f32[1,1,2,2,2048]{4,3,2,1,0:T(2,128)S(1)}, f32[1,1,2,2,2048]{4,3,2,1,0:T(2,128)}, u32[]{:S(2)}) copy-start(f32[1,1,2,2,2048]{4,3,2,1,0:T(2,128)} %param.7) | copy-start | bytes 98308
  13.5 14.9 %collective-permute-start.2 = (bf16[2,2,16,2048]{3,2,1,0:T(8,128)(2,1)S(1)}, bf16[2,2,16,2048]{3,2,1,0:T(8,128)(2,1)}, u32[]{:S(2)}, u32[]{:S(2)}) collective-permute-start(bf16[2,2,16,2048]{3,2,1,0:T(8,128)(2,1)S(1)} %slice_bitcast_fusion.1), channel_id=1, source_target_pairs={{1,0},{2,1},{3,2},{4,3},{5,4},{6,5},{7,6},{9,8},{10,9},{11,10},{12... | collective-permute-start | bytes 786440 | tf_op jit(solution)/shard_map/ppermute | solution.py:31
  21.8 1.9 %copy-start = (bf16[1,1,2,3,64,2048]{5,4,3,2,1,0:T(8,128)(2,1)S(1)}, bf16[1,1,2,3,64,2048]{5,4,3,2,1,0:T(8,128)(2,1)}, u32[]{:S(2)}) copy-start(bf16[1,1,2,3,64,2048]{5,4,3,2,1,0:T(8,128)(2,1)} %param.6) | copy-start | bytes 4718596
  29.8 1.6 %copy-start.3 = (bf16[2,64,64]{2,1,0:T(8,128)(2,1)S(1)}, bf16[2,64,64]{2,1,0:T(8,128)(2,1)}, u32[]{:S(2)}) copy-start(bf16[2,64,64]{2,1,0:T(8,128)(2,1)} %fusion.51) | copy-start | bytes 49156
  34.5 1.6 %copy-start.2 = (bf16[2,64,64]{2,1,0:T(8,128)(2,1)S(1)}, bf16[2,64,64]{2,1,0:T(8,128)(2,1)}, u32[]{:S(2)}) copy-start(bf16[2,64,64]{2,1,0:T(8,128)(2,1)} %fusion.49) | copy-start | bytes 49156
  47.6 20.8 %copy-start.1 = (bf16[1,1,2,64,80]{4,3,2,1,0:T(8,128)(2,1)S(1)}, bf16[1,1,2,64,80]{4,3,2,1,0:T(8,128)(2,1)}, u32[]{:S(2)}) copy-start(bf16[1,1,2,64,80]{4,3,2,1,0:T(8,128)(2,1)} %param.9) | copy-start | bytes 61444
  51.5 27.1 %all-to-all-start = ((bf16[64,2,2,40]{3,2,1,0:T(2,128)(2,1)}), bf16[64,2,2,40]{3,2,1,0:T(2,128)(2,1)S(1)}, u32[]{:S(2)}, u32[]{:S(2)}) async-start(bf16[64,2,2,40]{3,2,1,0:T(2,128)(2,1)} %maximum_bitcast_fusion.1), calls=%async_computation | async-start | bytes 131072 | tf_op jit(solution)/shard_map/all_to_all | solution.py:139
  87.9 5.5 %copy-start.5 = (s32[1,2560]{1,0:T(1,128)S(1)}, s32[1,2560]{1,0:T(1,128)}, u32[]{:S(2)}) copy-start(s32[1,2560]{1,0:T(1,128)} %param.8) | copy-start | bytes 30724
  88.9 14.1 %all-to-all-start.1 = ((bf16[64,2,40]{2,1,0:T(2,128)(2,1)}), bf16[64,2,40]{2,1,0:T(2,128)(2,1)S(1)}, u32[]{:S(2)}, u32[]{:S(2)}) async-start(bf16[64,2,40]{2,1,0:T(2,128)(2,1)} %copy.64), calls=%async_computation.1 | async-start | bytes 65536 | tf_op jit(solution)/shard_map/all_to_all | solution.py:141

commit v3 on v2

--- a/solution.py
+++ b/solution.py
@@ -76,9 +76,8 @@
     )
     joined_real = jnp.concatenate([near_real, edge_real], axis=2).reshape(2, -1)
     joined_imag = jnp.concatenate([near_imag, edge_imag], axis=2).reshape(2, -1)
-    picked_real = jnp.take(joined_real, pattern_row, axis=1)
-    picked_imag = jnp.take(joined_imag, pattern_row, axis=1)
-    return jnp.stack([picked_real, picked_imag], axis=1).astype(jnp.bfloat16)
+    joined = jnp.stack([joined_real, joined_imag], axis=1).astype(jnp.bfloat16)
+    return jnp.take(joined.reshape(4, -1), pattern_row, axis=1).reshape(2, 2, -1)
 
 
 def lagged_sums(by_element):

time: 117 us -> 106 us (0.906)
  blocking collectives: 0 us -> 26.9 us
  starting transfers between devices: 35.7 us -> 18.8 us
  waiting for transfers between devices: 25.3 us -> 13.8 us
  local copies, waits for them, and re-layouts: 32.5 us -> 24.4 us
    all_to_all x0 -> x1, blocking collectives: none -> 26.9 us  [body(): lax.all_to_all(values, 'energy', split_axis=0, concat_axis=0, tiled=True)]
    all_to_all x1 -> x0, starting transfers between devices: 16.9 us -> none  [body(): lax.all_to_all(values, 'energy', split_axis=0, concat_axis=0, tiled=True)]
    all_to_all x1 -> x0, waiting for transfers between devices: 10.1 us -> none  [body(): lax.all_to_all(values, 'energy', split_axis=0, concat_axis=0, tiled=True)]
    gather x2 -> x3, local copies, waits for them, and re-layouts: 10.8 us -> 5.47 us  [element_values(): jnp.take(joined.reshape(4, -1), pattern_row, axis=1).reshape(2, 2, -1)]
    reshape x2 -> x0, local copies, waits for them, and re-layouts: 2.23 us -> none  [the longest x1 1.62 us: element_values(): joined_imag = jnp.concatenate([near_imag, edge_imag], axis=2).reshape(2, -1)]
    another operation x1, other arithmetic: 1.36 us -> 0.1 us  [element_values(): joined = jnp.stack([joined_real, joined_imag], axis=1).astype(jnp.bfloat16)]
    another operation x2 -> x4, local copies, waits for them, and re-layouts: 1.67 us -> 0.43 us  [element_values(): return jnp.stack([picked_real, picked_imag], axis=1).astype(jnp.bfloat16)]
    dot_general x2, matrix products: 2.13 us -> 3.34 us  [slab_adjoint(): jnp.einsum('qjrb,jsb->qrs', left_real, right_real, preferred_element_type...]
  transfers between devices with their start and end apart: 5 -> 4, of which waited for: 4 -> 3; matrix products, arithmetic and copies ran while one was open for 7% -> 9% of each run, Pallas kernels for 0% -> 0%
where the time goes in v3:
time: 106 us
  blocking collectives  26.9 us (25%)
  local copies, waits for them, and re-layouts  24.4 us (23%)
  starting transfers between devices  18.8 us (18%)
  matrix products  14 us (13%)
  waiting for transfers between devices  13.8 us (13%)
  other arithmetic  7.59 us (7%)
    all_to_all x1, blocking collectives, body(): lax.all_to_all(values, 'energy', split_axis=0, concat_axis=0, tiled=True)  26.9 us
    ppermute x1, starting transfers between devices, padded_2(): lax.ppermute(tail, axis, [(i, (i + 1) % count) for i in range(ends)])  10.5 us
    all_to_all x1, waiting for transfers between devices, body(): lax.all_to_all(polarization, 'energy', split_axis=0, concat_axis=2, tiled...  9.64 us
    scatter x1, local copies, waits for them, and re-layouts, screen(): jnp.zeros((2, row_count * col_count), jnp.bfloat16).at[:, pattern_row]  7.59 us
    gather x3, local copies, waits for them, and re-layouts, element_values(): jnp.take(joined.reshape(4, -1), pattern_row, axis=1).reshape(2, 2, -1)  5.47 us
    reshape x1, local copies, waits for them, and re-layouts, lagged_sums(): padded.reshape(energy_count * (2 * energy_count + 1), 2 * column_count)  4.5 us
    all_to_all x1, starting transfers between devices, body(): lax.all_to_all(polarization, 'energy', split_axis=0, concat_axis=2, tiled...  4.42 us
    ppermute x1, waiting for transfers between devices, padded_2(): lax.ppermute(head, axis, [((i + 1) % count, i) for i in range(ends)])  3.61 us
  transfers between devices with their start and end apart: 4, of which 3 were waited for; matrix products, arithmetic and copies ran while one was open for 9% of the time, Pallas kernels for 0%

profile of v3, /device:TPU:7, one launch (start us, length us, event | category | flops | bytes accessed | tf_op | source)
XLA Modules:
  0.0 105.8 jit_solution(14136347256064258232)
XLA Ops:
  0.0 10.5 %collective-permute-start = (f32[1,1,2,2,2048]{4,3,2,1,0:T(2,128)}, f32[1,1,2,2,2048]{4,3,2,1,0:T(2,128)S(1)}, u32[]{:S(2)}, u32[]{:S(2)}) collective-permute-start(f32[1,1,2,2,2048]{4,3,2,1,0:T(2,128)} %param.5), channel_id=1, source_target_pairs={{0,1},{1,2},{2,3},{3,4},{4,5},{5,6},{6,7},{8,9},{9,10},{10,11},{11... | collective-permute-start | bytes 98312 | tf_op jit(solution)/shard_map/ppermute | solution.py:19
  10.5 1.9 %collective-permute-start.1 = (f32[1,1,2,2,2048]{4,3,2,1,0:T(2,128)}, f32[1,1,2,2,2048]{4,3,2,1,0:T(2,128)}, u32[]{:S(2)}, u32[]{:S(2)}) collective-permute-start(f32[1,1,2,2,2048]{4,3,2,1,0:T(2,128)} %param.5), channel_id=1, source_target_pairs={{1,0},{2,1},{3,2},{4,3},{5,4},{6,5},{7,6},{9,8},{10,9},{11,10},{12... | collective-permute-start | bytes 98312 | tf_op jit(solution)/shard_map/ppermute | solution.py:21
  12.5 1.0 slice_bitcast_fusion.1
  13.5 1.9 %collective-permute-start.2 = (bf16[2,2,16,2048]{3,2,1,0:T(8,128)(2,1)S(1)}, bf16[2,2,16,2048]{3,2,1,0:T(8,128)(2,1)}, u32[]{:S(2)}, u32[]{:S(2)}) collective-permute-start(bf16[2,2,16,2048]{3,2,1,0:T(8,128)(2,1)S(1)} %slice_bitcast_fusion.1), channel_id=1, source_target_pairs={{1,0},{2,1},{3,2},{4,3},{5,4},{6,5},{7,6},{9,8},{10,9},{11,10},{12... | collective-permute-start | bytes 786440 | tf_op jit(solution)/shard_map/ppermute | solution.py:31
  15.4 1.7 %bitcast_convert_fusion.1 = (f32[3,64,2048]{2,1,0:T(8,128)S(1)}, f32[3,64,2048]{2,1,0:T(8,128)S(1)}) fusion(bf16[1,1,2,3,64,2048]{5,4,3,2,1,0:T(8,128)(2,1)} %param.4), kind=kLoop, calls=%fused_computation.97 | loop fusion | flops 786432 | bytes 4718592 | tf_op jit(solution)/shard_map/convert_element_type | solution.py:69
  17.3 0.6 compare_and_fusion
  18.0 3.6 %collective-permute-done.1 = f32[1,1,2,2,2048]{4,3,2,1,0:T(2,128)} collective-permute-done((f32[1,1,2,2,2048]{4,3,2,1,0:T(2,128)}, f32[1,1,2,2,2048]{4,3,2,1,0:T(2,128)}, u32[]{:S(2)}, u32[]{:S(2)}) %collective-permute-start.1) | collective-permute-done | bytes 32800 | tf_op jit(solution)/shard_map/ppermute | solution.py:21
  21.6 0.8 maximum_bitcast_fusion
  22.6 1.9 %fusion.52 = f32[2,64,64]{2,1,0:T(8,128)S(1)} fusion(f32[2,3,2048]{2,1,0:T(4,128)S(1)} %copy.63, f32[3,64,2048]{2,1,0:T(8,128)S(1)} %get-tuple-element.8, f32[2,3,2048]{2,1,0:T(4,128)S(1)} %copy.62, f32[3,64,2048]{2,1,0:T(8,128)S(1)} %get-tuple-element.7, bf16[1,1,2,3,64,2048]{5,4,3,2,1,0:T(8,128)(2,1)} %param.4), kind=kOutput, calls=%fused_computation.64 | convolution fusion | flops 104595456 | bytes 4063232 | tf_op jit(solution)/shard_map/qjrb,jsb->qrs/dot_general | solution.py:35
  24.5 0.7 fusion.53
  25.2 1.3 %fusion.55 = bf16[2,64,64]{2,1,0:T(8,128)(2,1)} fusion(f32[2,64,64]{2,1,0:T(8,128)S(1)} %fusion.52, f32[2,3,2048]{2,1,0:T(4,128)S(1)} %copy.63, f32[3,64,2048]{2,1,0:T(8,128)S(1)} %get-tuple-element.8, f32[2,3,2048]{2,1,0:T(4,128)S(1)} %copy.62, f32[3,64,2048]{2,1,0:T(8,128)S(1)} %get-tuple-element.7, bf16[1,1,2,3,64,2048]{5,4,3,2,1,0:T(8,128)(2,1)S(1)} %copy-done), kind=kOutput, calls=%fused_computation.67 | convolution fusion | flops 104611840 | bytes 4145152 | tf_op jit(solution)/shard_map/qjrb,jsb->qrs/dot_general | solution.py:37
  26.5 1.3 %fusion.54 = bf16[2,64,64]{2,1,0:T(8,128)(2,1)} fusion(f32[2,64,64]{2,1,0:T(8,128)S(1)} %fusion.53, f32[2,3,2048]{2,1,0:T(4,128)S(1)} %copy.63, f32[3,64,2048]{2,1,0:T(8,128)S(1)} %get-tuple-element.8, f32[2,3,2048]{2,1,0:T(4,128)S(1)} %copy.62, f32[3,64,2048]{2,1,0:T(8,128)S(1)} %get-tuple-element.7, bf16[1,1,2,3,64,2048]{5,4,3,2,1,0:T(8,128)(2,1)S(1)} %copy-done), kind=kOutput, calls=%fused_computation.66 | convolution fusion | flops 104611840 | bytes 4145152 | tf_op jit(solution)/shard_map/qjrb,jsb->qrs/dot_general | solution.py:38
  27.8 0.5 collective-permute-done.2
  28.4 1.4 %fusion.64 = f32[2,64,16]{1,2,0:T(8,128)S(1)} fusion(f32[2,3,2048]{2,1,0:T(4,128)S(1)} %copy.63, f32[3,64,2048]{2,1,0:T(8,128)S(1)} %get-tuple-element.8, f32[2,3,2048]{2,1,0:T(4,128)S(1)} %copy.62, f32[3,64,2048]{2,1,0:T(8,128)S(1)} %get-tuple-element.7, bf16[2,2,16,2048]{3,2,1,0:T(8,128)(2,1)} %collective-permute-done.2), kind=kOutput, calls=%fused_computation.82 | convolution fusion | flops 20709376 | bytes 3383296 | tf_op jit(solution)/shard_map/qjrb,jsb->qrs/dot_general | solution.py:37
  29.8 1.5 %fusion.68 = bf16[2,64,16]{1,2,0:T(8,128)(2,1)S(1)} fusion(f32[2,64,16]{1,2,0:T(8,128)S(1)} %fusion.64, f32[2,3,2048]{2,1,0:T(4,128)S(1)} %copy.63, f32[3,64,2048]{2,1,0:T(8,128)S(1)} %get-tuple-element.8, f32[2,3,2048]{2,1,0:T(4,128)S(1)} %copy.62, f32[3,64,2048]{2,1,0:T(8,128)S(1)} %get-tuple-element.7, bf16[2,2,16,2048]{3,2,1,0:T(8,128)(2,1)} %collective-permute-done.2), kind=kOutput, calls=%fused_computation.86 | convolution fusion | flops 20713472 | bytes 3387392 | tf_op jit(solution)/shard_map/qjrb,jsb->qrs/dot_general | solution.py:35
  31.2 0.1 copy.64
  31.4 0.1 pad_maximum_fusion.1
  31.5 0.1 stack_reshape.10
  31.6 1.4 %fusion.65 = f32[2,64,16]{1,2,0:T(8,128)S(1)} fusion(f32[2,3,2048]{2,1,0:T(4,128)S(1)} %copy.63, f32[3,64,2048]{2,1,0:T(8,128)S(1)} %get-tuple-element.8, f32[2,3,2048]{2,1,0:T(4,128)S(1)} %copy.62, f32[3,64,2048]{2,1,0:T(8,128)S(1)} %get-tuple-element.7, bf16[2,2,16,2048]{3,2,1,0:T(8,128)(2,1)} %collective-permute-done.2), kind=kOutput, calls=%fused_computation.83 | convolution fusion | flops 20709376 | bytes 3383296 | tf_op jit(solution)/shard_map/qjrb,jsb->qrs/dot_general | solution.py:40
  33.0 1.5 %fusion.69 = bf16[2,64,16]{1,2,0:T(8,128)(2,1)S(1)} fusion(f32[2,64,16]{1,2,0:T(8,128)S(1)} %fusion.65, f32[2,3,2048]{2,1,0:T(4,128)S(1)} %copy.63, f32[3,64,2048]{2,1,0:T(8,128)S(1)} %get-tuple-element.8, f32[2,3,2048]{2,1,0:T(4,128)S(1)} %copy.62, f32[3,64,2048]{2,1,0:T(8,128)S(1)} %get-tuple-element.7, bf16[2,2,16,2048]{3,2,1,0:T(8,128)(2,1)} %collective-permute-done.2), kind=kOutput, calls=%fused_computation.87 | convolution fusion | flops 20713472 | bytes 3387392 | tf_op jit(solution)/shard_map/qjrb,jsb->qrs/dot_general | solution.py:38
  34.5 0.1 copy.65
  34.6 0.1 pad_maximum_fusion.2
  34.7 0.1 stack_reshape.11
  34.8 0.1 pad_maximum_fusion
  34.9 0.6 copy.68
  35.5 5.1 %gather_fusion = bf16[2560,4]{1,0:T(8,128)(2,1)S(1)} fusion(bf16[4,5120]{0,1:T(8,128)(2,1)S(1)} %copy.68, s32[3072]{0:T(1024)S(1)} %pad_clamp_fusion), kind=kCustom, calls=%fused_computation | custom fusion | bytes 51200 | tf_op jit(solution)/shard_map/jit(_take)/gather | solution.py:80
  40.6 0.3 copy.69
  40.9 0.1 gather.7
  41.1 26.9 %all_to_all.20 = bf16[64,2,2,40]{3,2,1,0:T(2,128)(2,1)S(1)} all-to-all(bf16[64,2,2,40]{3,2,1,0:T(2,128)(2,1)S(1)} %copy.70), channel_id=1, replica_groups=mesh['energy'=64,'domain'=8] {'energy'}, dimensions={0} | all-to-all | bytes 40960 | tf_op jit(solution)/shard_map/all_to_all | solution.py:138
  68.0 0.1 copy.88
  68.1 0.1 rev.3
  68.3 0.1 copy.87
  68.4 0.7 multiply_subtract_fusion
  69.1 3.0 %select_maximum_fusion = f32[64,129,80]{1,0,2:T(8,128)} fusion(f32[64,64,40]{1,0,2:T(8,128)S(1)} %get-tuple-element.12, f32[64,64,40]{1,0,2:T(8,128)S(1)} %get-tuple-element.11), kind=kLoop, calls=%fused_computation.2 | loop fusion | flops 2641920 | bytes 3952640 | tf_op jit(solution)/shard_map/concatenate | solution.py:94
  72.1 4.5 %reshape.85 = f32[8256,80]{0,1:T(8,128)S(1)} reshape(f32[64,129,80]{1,0,2:T(8,128)} %select_maximum_fusion) | data formatting | bytes 5283840 | tf_op jit(solution)/shard_map/reshape | solution.py:96
  76.6 0.2 slice_bitcast_fusion
  76.8 0.5 copy.89
  77.3 0.3 bitcast_reduce_fusion
  77.6 0.7 copy.73
  78.4 4.4 %all-to-all-start.1 = ((bf16[64,2,40]{2,1,0:T(2,128)(2,1)}), bf16[64,2,40]{2,1,0:T(2,128)(2,1)S(1)}, u32[]{:S(2)}, u32[]{:S(2)}) async-start(bf16[64,2,40]{2,1,0:T(2,128)(2,1)} %copy.73), calls=%async_computation.1 | async-start | bytes 65536 | tf_op jit(solution)/shard_map/all_to_all | solution.py:140
  82.8 9.6 %all-to-all-done.1 = bf16[64,2,40]{2,1,0:T(2,128)(2,1)S(1)} async-done(((bf16[64,2,40]{2,1,0:T(2,128)(2,1)}), bf16[64,2,40]{2,1,0:T(2,128)(2,1)S(1)}, u32[]{:S(2)}, u32[]{:S(2)}) %all-to-all-start.1) | async-done | bytes 10272 | tf_op jit(solution)/shard_map/all_to_all | solution.py:140
  92.5 0.1 reshape.98
  92.6 0.4 copy.75
  93.0 7.6 %scatter_custom_fusion = bf16[2,5120]{0,1:T(8,128)(2,1)S(1)} fusion(s32[2560]{0:T(1024)} %copy-done.4, bf16[2560,2]{1,0:T(8,128)(2,1)S(1)} %copy.75, bf16[]{:T(256)} %constant.8.clone.1), kind=kCustom, calls=%fused_computation.98 | custom fusion | bytes 20992 | tf_op jit(solution)/shard_map/scatter | solution.py:109
  100.6 1.2 %slice_reduce_fusion.1 = (bf16[5120]{0:T(1024)(128)(2,1)S(1)}, bf16[5120]{0:T(1024)(128)(2,1)S(1)}) fusion(bf16[2,5120]{0,1:T(8,128)(2,1)S(1)} %scatter_custom_fusion), kind=kLoop, calls=%fused_computation.57 | loop fusion | bytes 40960 | tf_op jit(solution)/shard_map/slice | solution.py:113
  101.8 0.1 squeeze.68
  101.9 0.1 fusion.115
  102.0 0.1 squeeze.70
  102.1 0.1 fusion.114
  102.3 0.2 fusion.93
  102.5 0.2 fusion.89
  102.8 0.2 fusion.70
  103.0 0.2 fusion.87
  103.2 0.2 fusion.83
  103.4 0.1 fusion.60
  103.6 0.2 fusion.103
  103.7 0.1 fusion.61
  103.9 0.2 fusion.99
  104.1 0.2 convolution_subtract_fusion.1
  104.2 0.2 fusion.71
  104.5 0.2 convolution_add_fusion
  104.7 0.2 fusion.59
  104.9 0.2 fusion.57
  105.1 0.7 copy.76
  (37 shorter events, 0.7 us)
Async XLA Ops:
  0.0 18.0 %collective-permute-start = (f32[1,1,2,2,2048]{4,3,2,1,0:T(2,128)}, f32[1,1,2,2,2048]{4,3,2,1,0:T(2,128)S(1)}, u32[]{:S(2)}, u32[]{:S(2)}) collective-permute-start(f32[1,1,2,2,2048]{4,3,2,1,0:T(2,128)} %param.5), channel_id=1, source_target_pairs={{0,1},{1,2},{2,3},{3,4},{4,5},{5,6},{6,7},{8,9},{9,10},{10,11},{11... | collective-permute-start | bytes 98312 | tf_op jit(solution)/shard_map/ppermute | solution.py:19
  10.5 11.0 %collective-permute-start.1 = (f32[1,1,2,2,2048]{4,3,2,1,0:T(2,128)}, f32[1,1,2,2,2048]{4,3,2,1,0:T(2,128)}, u32[]{:S(2)}, u32[]{:S(2)}) collective-permute-start(f32[1,1,2,2,2048]{4,3,2,1,0:T(2,128)} %param.5), channel_id=1, source_target_pairs={{1,0},{2,1},{3,2},{4,3},{5,4},{6,5},{7,6},{9,8},{10,9},{11,10},{12... | collective-permute-start | bytes 98312 | tf_op jit(solution)/shard_map/ppermute | solution.py:21
  13.5 3.7 %copy-start.5 = (s32[1,2560]{1,0:T(1,128)S(1)}, s32[1,2560]{1,0:T(1,128)}, u32[]{:S(2)}) copy-start(s32[1,2560]{1,0:T(1,128)} %param.6) | copy-start | bytes 30724
  13.5 8.1 %copy-start.7 = (f32[1,1,2,2,2048]{4,3,2,1,0:T(2,128)S(1)}, f32[1,1,2,2,2048]{4,3,2,1,0:T(2,128)}, u32[]{:S(2)}) copy-start(f32[1,1,2,2,2048]{4,3,2,1,0:T(2,128)} %param.5) | copy-start | bytes 98308
  13.5 14.9 %collective-permute-start.2 = (bf16[2,2,16,2048]{3,2,1,0:T(8,128)(2,1)S(1)}, bf16[2,2,16,2048]{3,2,1,0:T(8,128)(2,1)}, u32[]{:S(2)}, u32[]{:S(2)}) collective-permute-start(bf16[2,2,16,2048]{3,2,1,0:T(8,128)(2,1)S(1)} %slice_bitcast_fusion.1), channel_id=1, source_target_pairs={{1,0},{2,1},{3,2},{4,3},{5,4},{6,5},{7,6},{9,8},{10,9},{11,10},{12... | collective-permute-start | bytes 786440 | tf_op jit(solution)/shard_map/ppermute | solution.py:31
  17.2 4.4 %copy-start.4 = (s32[2560]{0:T(1024)}, s32[2560]{0:T(1024)S(1)}, u32[]{:S(2)}) copy-start(s32[2560]{0:T(1024)S(1)} %fusion.105) | copy-start | bytes 30724
  22.6 1.9 %copy-start = (bf16[1,1,2,3,64,2048]{5,4,3,2,1,0:T(8,128)(2,1)S(1)}, bf16[1,1,2,3,64,2048]{5,4,3,2,1,0:T(8,128)(2,1)}, u32[]{:S(2)}) copy-start(bf16[1,1,2,3,64,2048]{5,4,3,2,1,0:T(8,128)(2,1)} %param.4) | copy-start | bytes 4718596
  29.8 1.6 %copy-start.3 = (bf16[2,64,64]{2,1,0:T(8,128)(2,1)S(1)}, bf16[2,64,64]{2,1,0:T(8,128)(2,1)}, u32[]{:S(2)}) copy-start(bf16[2,64,64]{2,1,0:T(8,128)(2,1)} %fusion.55) | copy-start | bytes 49156
  33.0 1.6 %copy-start.2 = (bf16[2,64,64]{2,1,0:T(8,128)(2,1)S(1)}, bf16[2,64,64]{2,1,0:T(8,128)(2,1)}, u32[]{:S(2)}) copy-start(bf16[2,64,64]{2,1,0:T(8,128)(2,1)} %fusion.54) | copy-start | bytes 49156
  34.5 6.6 %copy-start.6 = (pred[64,40]{1,0:T(8,128)(4,1)S(1)}, pred[64,40]{1,0:T(8,128)(4,1)}, u32[]{:S(2)}) copy-start(pred[64,40]{1,0:T(8,128)(4,1)} %compare_and_fusion) | copy-start | bytes 7684
  77.3 5.5 %copy-start.1 = (bf16[1,1,2,64,80]{4,3,2,1,0:T(8,128)(2,1)S(1)}, bf16[1,1,2,64,80]{4,3,2,1,0:T(8,128)(2,1)}, u32[]{:S(2)}) copy-start(bf16[1,1,2,64,80]{4,3,2,1,0:T(8,128)(2,1)} %param.7) | copy-start | bytes 61444
  78.4 14.1 %all-to-all-start.1 = ((bf16[64,2,40]{2,1,0:T(2,128)(2,1)}), bf16[64,2,40]{2,1,0:T(2,128)(2,1)S(1)}, u32[]{:S(2)}, u32[]{:S(2)}) async-start(bf16[64,2,40]{2,1,0:T(2,128)(2,1)} %copy.73), calls=%async_computation.1 | async-start | bytes 65536 | tf_op jit(solution)/shard_map/all_to_all | solution.py:140

commit v4 on v3

--- a/solution.py
+++ b/solution.py
@@ -1,8 +1,10 @@
+import functools
 import math
 
 import jax
 import jax.numpy as jnp
 from jax import lax
+from jax.experimental import pallas as pl
 from jax.sharding import PartitionSpec as P
 
 EDGE = 16
@@ -31,16 +33,6 @@
     return lax.ppermute(x, axis, pairs)
 
 
-def slab_adjoint(left_real, left_imag, right_real, right_imag):
-    real_sum = jnp.einsum(
-        "qjrb,jsb->qrs", left_real, right_real, preferred_element_type=jnp.float32
-    ) + jnp.einsum("qjrb,jsb->qrs", left_imag, right_imag, preferred_element_type=jnp.float32)
-    imag_sum = jnp.einsum(
-        "qjrb,jsb->qrs", left_imag, right_real, preferred_element_type=jnp.float32
-    ) - jnp.einsum("qjrb,jsb->qrs", left_real, right_imag, preferred_element_type=jnp.float32)
-    return (real_sum, imag_sum)
-
-
 def times_adjoint(left_real, left_imag, right_real, right_imag):
     real_sum = jnp.dot(left_real, right_real.T, preferred_element_type=jnp.float32) + jnp.dot(
         left_imag, right_imag.T, preferred_element_type=jnp.float32
@@ -61,22 +53,59 @@
     return (real_sum, imag_sum)
 
 
+def _weigh_kernel(slab_ref, edge_ref, rate_ref, out_ref, *, factor, rows, edge):
+    step = pl.program_id(0)
+
+    @pl.when(step == 0)
+    def _():
+        out_ref[...] = jnp.zeros_like(out_ref)
+
+    slab_real = slab_ref[0, 0]
+    slab_imag = slab_ref[1, 0]
+    real_f = slab_real.astype(jnp.float32)
+    imag_f = slab_imag.astype(jnp.float32)
+    pieces = []
+    for q in range(2):
+        rate_real = rate_ref[0, q, 0:1, :]
+        rate_imag = rate_ref[0, q, 1:2, :]
+        pieces.append(((real_f * rate_real - imag_f * rate_imag) * factor).astype(jnp.bfloat16))
+        pieces.append(((real_f * rate_imag + imag_f * rate_real) * factor).astype(jnp.bfloat16))
+    left = jnp.concatenate(pieces, axis=0)
+    right = jnp.concatenate([slab_real, slab_imag, edge_ref[0, 0], edge_ref[1, 0]], axis=0)
+    prod = lax.dot_general(left, right, (((1,), (1,)), ((), ())), preferred_element_type=jnp.float32)
+    for q in range(2):
+        wr = prod[2 * q * rows:(2 * q + 1) * rows]
+        wi = prod[(2 * q + 1) * rows:(2 * q + 2) * rows]
+        out_ref[q, 0, :, 0:rows] += wr[:, 0:rows] + wi[:, rows:2 * rows]
+        out_ref[q, 1, :, 0:rows] += wi[:, 0:rows] - wr[:, rows:2 * rows]
+
+        @pl.when(step > 0)
+        def _():
+            e0 = 2 * rows
+            out_ref[q, 0, :, rows:rows + edge] += wr[:, e0:e0 + edge] + wi[:, e0 + edge:e0 + 2 * edge]
+            out_ref[q, 1, :, rows:rows + edge] += wi[:, e0:e0 + edge] - wr[:, e0 + edge:e0 + 2 * edge]
+
+
+def weighed_products(own_slab, next_edge, diag_rates):
+    _, blocks, rows, block_order = own_slab.shape
+    edge = next_edge.shape[2]
+    factor = 1.0 / math.sqrt(3.0 * block_order)
+    kernel = functools.partial(_weigh_kernel, factor=factor, rows=rows, edge=edge)
+    return pl.pallas_call(
+        kernel,
+        grid=(blocks,),
+        in_specs=[
+            pl.BlockSpec((2, 1, rows, block_order), lambda j: (0, j, 0, 0)),
+            pl.BlockSpec((2, 1, edge, block_order), lambda j: (0, jnp.maximum(j - 1, 0), 0, 0)),
+            pl.BlockSpec((1, 2, 2, block_order), lambda j: (j, 0, 0, 0)),
+        ],
+        out_specs=pl.BlockSpec((2, 2, rows, rows + edge), lambda j: (0, 0, 0, 0)),
+        out_shape=jax.ShapeDtypeStruct((2, 2, rows, rows + edge), jnp.float32),
+    )(own_slab, next_edge, diag_rates)
+
+
 def element_values(own_slab, next_edge, diag_rates, pattern_row):
-    block_order = own_slab.shape[3]
-    factor = 1.0 / math.sqrt(3.0 * block_order)
-    rate_real = jnp.transpose(diag_rates[:, :, 0], (1, 0, 2))[:, :, None, :]
-    rate_imag = jnp.transpose(diag_rates[:, :, 1], (1, 0, 2))[:, :, None, :]
-    slab_real = own_slab[0].astype(jnp.float32)[None]
-    slab_imag = own_slab[1].astype(jnp.float32)[None]
-    weighted_real = ((slab_real * rate_real - slab_imag * rate_imag) * factor).astype(jnp.bfloat16)
-    weighted_imag = ((slab_real * rate_imag + slab_imag * rate_real) * factor).astype(jnp.bfloat16)
-    near_real, near_imag = slab_adjoint(weighted_real, weighted_imag, own_slab[0], own_slab[1])
-    edge_real, edge_imag = slab_adjoint(
-        weighted_real[:, 1:3], weighted_imag[:, 1:3], next_edge[0], next_edge[1]
-    )
-    joined_real = jnp.concatenate([near_real, edge_real], axis=2).reshape(2, -1)
-    joined_imag = jnp.concatenate([near_imag, edge_imag], axis=2).reshape(2, -1)
-    joined = jnp.stack([joined_real, joined_imag], axis=1).astype(jnp.bfloat16)
+    joined = weighed_products(own_slab, next_edge, diag_rates).astype(jnp.bfloat16)
     return jnp.take(joined.reshape(4, -1), pattern_row, axis=1).reshape(2, 2, -1)
 
 

time: 106 us -> 106 us (level)
  matrix products: 14 us -> 3.05 us
  waiting for transfers between devices: 13.8 us -> 19.4 us
  Pallas kernels: 0 us -> 4.34 us
    dot_general x8 -> x0, matrix products: 10.9 us -> none  [the longest x2 3.34 us: slab_adjoint(): jnp.einsum('qjrb,jsb->qrs', left_real, right_real, preferred_element_type...]
    ppermute x1, waiting for transfers between devices: 0.53 us -> 5.32 us  [passed_along(): return lax.ppermute(x, axis, pairs)]
    pallas_call x0 -> x1, Pallas kernels: none -> 4.34 us  [weighed_products(): pl.pallas_call(kernel, grid=(blocks,), in_specs=[pl.BlockSpec((2, 1, rows...]
  transfers between devices with their start and end apart: 4 -> 4, of which waited for: 3 -> 3; matrix products, arithmetic and copies ran while one was open for 9% -> 4% of each run, Pallas kernels for 0% -> 0%
where the time goes in v4:
time: 106 us; the launch traced here: 105 us
  blocking collectives  26.9 us (25%)
  local copies, waits for them, and re-layouts  24.4 us (23%)
  waiting for transfers between devices  19.4 us (18%)
  starting transfers between devices  18.8 us (18%)
  other arithmetic  7.95 us (8%)
  Pallas kernels  4.34 us (4%)
  matrix products  3.05 us (3%)
    all_to_all x1, blocking collectives, body(): lax.all_to_all(values, 'energy', split_axis=0, concat_axis=0, tiled=True)  26.9 us
    ppermute x1, starting transfers between devices, padded_2(): lax.ppermute(tail, axis, [(i, (i + 1) % count) for i in range(ends)])  10.5 us
    all_to_all x1, waiting for transfers between devices, body(): lax.all_to_all(polarization, 'energy', split_axis=0, concat_axis=2, tiled...  9.64 us
    scatter x1, local copies, waits for them, and re-layouts, screen(): jnp.zeros((2, row_count * col_count), jnp.bfloat16).at[:, pattern_row]  7.46 us
    gather x3, local copies, waits for them, and re-layouts, element_values(): jnp.take(joined.reshape(4, -1), pattern_row, axis=1).reshape(2, 2, -1)  5.47 us
    ppermute x1, waiting for transfers between devices, passed_along(): return lax.ppermute(x, axis, pairs)  5.32 us
    reshape x1, local copies, waits for them, and re-layouts, lagged_sums(): padded.reshape(energy_count * (2 * energy_count + 1), 2 * column_count)  4.5 us
    ppermute x1, waiting for transfers between devices, padded_2(): lax.ppermute(head, axis, [((i + 1) % count, i) for i in range(ends)])  4.47 us
  transfers between devices with their start and end apart: 4, of which 3 were waited for; matrix products, arithmetic and copies ran while one was open for 4% of the time, Pallas kernels for 0%

profile of v4, /device:TPU:7, one launch (start us, length us, event | category | flops | bytes accessed | tf_op | source)
XLA Modules:
  0.0 105.1 jit_solution(8471215302989441700)
XLA Ops:
  0.0 10.5 %collective-permute-start.1 = (f32[1,1,2,2,2048]{4,3,2,1,0:T(2,128)}, f32[1,1,2,2,2048]{4,3,2,1,0:T(2,128)S(1)}, u32[]{:S(2)}, u32[]{:S(2)}) collective-permute-start(f32[1,1,2,2,2048]{4,3,2,1,0:T(2,128)} %param.5), channel_id=1, source_target_pairs={{0,1},{1,2},{2,3},{3,4},{4,5},{5,6},{6,7},{8,9},{9,10},{10,11},{11... | collective-permute-start | bytes 98312 | tf_op jit(solution)/shard_map/ppermute | solution.py:21
  10.5 1.9 %collective-permute-start.2 = (f32[1,1,2,2,2048]{4,3,2,1,0:T(2,128)}, f32[1,1,2,2,2048]{4,3,2,1,0:T(2,128)S(1)}, u32[]{:S(2)}, u32[]{:S(2)}) collective-permute-start(f32[1,1,2,2,2048]{4,3,2,1,0:T(2,128)} %param.5), channel_id=1, source_target_pairs={{1,0},{2,1},{3,2},{4,3},{5,4},{6,5},{7,6},{9,8},{10,9},{11,10},{12... | collective-permute-start | bytes 98312 | tf_op jit(solution)/shard_map/ppermute | solution.py:23
  12.5 1.0 slice_bitcast_fusion.1
  13.5 1.9 %collective-permute-start = (bf16[2,2,16,2048]{3,2,1,0:T(8,128)(2,1)S(1)}, bf16[2,2,16,2048]{3,2,1,0:T(8,128)(2,1)S(1)}, u32[]{:S(2)}, u32[]{:S(2)}) collective-permute-start(bf16[2,2,16,2048]{3,2,1,0:T(8,128)(2,1)S(1)} %slice_bitcast_fusion.1), channel_id=1, source_target_pairs={{1,0},{2,1},{3,2},{4,3},{5,4},{6,5},{7,6},{9,8},{10,9},{11,10},{12... | collective-permute-start | bytes 786440 | tf_op jit(solution)/shard_map/ppermute | solution.py:33
  15.4 0.7 fusion.33
  16.1 0.7 reduce.1
  16.9 0.1 squeeze.40
  17.0 0.0 collective-permute-done.1
  17.0 4.5 %collective-permute-done.2 = f32[1,1,2,2,2048]{4,3,2,1,0:T(2,128)S(1)} collective-permute-done((f32[1,1,2,2,2048]{4,3,2,1,0:T(2,128)}, f32[1,1,2,2,2048]{4,3,2,1,0:T(2,128)S(1)}, u32[]{:S(2)}, u32[]{:S(2)}) %collective-permute-start.2) | collective-permute-done | bytes 32800 | tf_op jit(solution)/shard_map/ppermute | solution.py:23
  21.5 1.4 %maximum_bitcast_fusion.rate_ref = f32[3,2,2,2048]{3,2,1,0:T(2,128)} fusion(f32[1,1,2,2,2048]{4,3,2,1,0:T(2,128)S(1)} %collective-permute-done.2, f32[1,1,2,2,2048]{4,3,2,1,0:T(2,128)} %param.5, f32[1,1,2,2,2048]{4,3,2,1,0:T(2,128)S(1)} %collective-permute-done.1), kind=kLoop, calls=%fused_computation.29 | loop fusion | flops 49152 | bytes 196608 | tf_op jit(solution)/shard_map/squeeze | solution.py:164
  22.9 5.3 %collective-permute-done.edge_ref = bf16[2,2,16,2048]{3,2,1,0:T(8,128)(2,1)S(1)} collective-permute-done((bf16[2,2,16,2048]{3,2,1,0:T(8,128)(2,1)S(1)}, bf16[2,2,16,2048]{3,2,1,0:T(8,128)(2,1)S(1)}, u32[]{:S(2)}, u32[]{:S(2)}) %collective-permute-start) | collective-permute-done | bytes 262176 | tf_op jit(solution)/shard_map/ppermute | solution.py:33
  28.2 0.0 copy-start.1
  28.2 0.7 copy-done.1
  28.9 4.3 %shard_map.46 = f32[2,2,64,80]{3,2,1,0:T(8,128)} custom-call(bf16[2,3,64,2048]{3,2,1,0:T(8,128)(2,1)} %bitcast.71, bf16[2,2,16,2048]{3,2,1,0:T(8,128)(2,1)} %copy-done.1, f32[3,2,2,2048]{3,2,1,0:T(2,128)} %maximum_bitcast_fusion.rate_ref), custom_call_target="tpu_custom_call" | custom-call | tf_op jit(solution)/shard_map/pallas_call | solution.py:94
  33.3 0.9 convert_element_type.37
  34.2 0.2 reshape.69
  34.3 0.6 copy.23
  34.9 5.1 %gather_fusion = bf16[2560,4]{1,0:T(8,128)(2,1)S(1)} fusion(bf16[4,5120]{0,1:T(8,128)(2,1)S(1)} %copy.23, s32[3072]{0:T(1024)S(1)} %pad_clamp_fusion), kind=kCustom, calls=%fused_computation | custom fusion | bytes 51200 | tf_op jit(solution)/shard_map/jit(_take)/gather | solution.py:109
  40.0 0.3 copy.24
  40.3 0.1 gather.7
  40.4 0.1 copy.25
  40.5 26.9 %all_to_all.20 = bf16[64,2,2,40]{3,2,1,0:T(2,128)(2,1)S(1)} all-to-all(bf16[64,2,2,40]{3,2,1,0:T(2,128)(2,1)S(1)} %copy.25), channel_id=1, replica_groups=mesh['energy'=64,'domain'=8] {'energy'}, dimensions={0} | all-to-all | bytes 40960 | tf_op jit(solution)/shard_map/all_to_all | solution.py:167
  67.4 0.1 copy.33
  67.5 0.1 rev.3
  67.6 0.1 copy.32
  67.8 0.7 multiply_subtract_fusion
  68.5 3.0 %select_maximum_fusion = f32[64,129,80]{1,0,2:T(8,128)} fusion(f32[64,64,40]{1,0,2:T(8,128)S(1)} %get-tuple-element.8, f32[64,64,40]{1,0,2:T(8,128)S(1)} %get-tuple-element.7), kind=kLoop, calls=%fused_computation.2 | loop fusion | flops 2641920 | bytes 3952640 | tf_op jit(solution)/shard_map/concatenate | solution.py:123
  71.5 4.5 %reshape.70 = f32[8256,80]{0,1:T(8,128)S(1)} reshape(f32[64,129,80]{1,0,2:T(8,128)} %select_maximum_fusion) | data formatting | bytes 5283840 | tf_op jit(solution)/shard_map/reshape | solution.py:125
  76.0 0.2 slice_bitcast_fusion
  76.2 0.5 copy.34
  76.7 0.0 copy-start
  76.7 0.3 bitcast_reduce_fusion
  77.0 0.1 fusion.10
  77.0 0.7 copy.28
  77.8 4.4 %all-to-all-start.1 = ((bf16[64,2,40]{2,1,0:T(2,128)(2,1)}), bf16[64,2,40]{2,1,0:T(2,128)(2,1)S(1)}, u32[]{:S(2)}, u32[]{:S(2)}) async-start(bf16[64,2,40]{2,1,0:T(2,128)(2,1)} %copy.28), calls=%async_computation.1 | async-start | bytes 65536 | tf_op jit(solution)/shard_map/all_to_all | solution.py:169
  82.2 0.0 copy-done
  82.2 9.6 %all-to-all-done.1 = bf16[64,2,40]{2,1,0:T(2,128)(2,1)S(1)} async-done(((bf16[64,2,40]{2,1,0:T(2,128)(2,1)}), bf16[64,2,40]{2,1,0:T(2,128)(2,1)S(1)}, u32[]{:S(2)}, u32[]{:S(2)}) %all-to-all-start.1) | async-done | bytes 10272 | tf_op jit(solution)/shard_map/all_to_all | solution.py:169
  91.9 0.1 reshape.83
  92.0 0.4 copy.30
  92.4 7.5 %scatter_custom_fusion = bf16[2,5120]{0,1:T(8,128)(2,1)S(1)} fusion(s32[2560]{0:T(1024)S(1)} %fusion.33, bf16[2560,2]{1,0:T(8,128)(2,1)S(1)} %copy.30, bf16[]{:T(256)} %constant.7.clone.1), kind=kCustom, calls=%fused_computation.26 | custom fusion | bytes 20482 | tf_op jit(solution)/shard_map/scatter | solution.py:138
  99.9 1.2 %slice_reduce_fusion.1 = (bf16[5120]{0:T(1024)(128)(2,1)S(1)}, bf16[5120]{0:T(1024)(128)(2,1)S(1)}) fusion(bf16[2,5120]{0,1:T(8,128)(2,1)S(1)} %scatter_custom_fusion), kind=kLoop, calls=%fused_computation.7 | loop fusion | bytes 40960 | tf_op jit(solution)/shard_map/slice | solution.py:142
  101.1 0.1 squeeze.45
  101.2 0.1 fusion.35
  101.3 0.1 squeeze.47
  101.4 0.1 fusion.34
  101.6 0.2 fusion.21
  101.8 0.2 fusion.17
  102.0 0.2 fusion.6
  102.3 0.2 fusion.15
  102.5 0.2 fusion.11
  102.7 0.1 fusion.4
  102.8 0.2 fusion.31
  103.0 0.1 fusion.5
  103.2 0.2 fusion.27
  103.3 0.2 convolution_subtract_fusion.1
  103.5 0.2 fusion.7
  103.8 0.2 convolution_add_fusion
  103.9 0.2 fusion.3
  104.2 0.2 fusion.1
  104.4 0.7 copy.31
  (10 shorter events, 0.1 us)
Async XLA Ops:
  0.0 17.0 %collective-permute-start.1 = (f32[1,1,2,2,2048]{4,3,2,1,0:T(2,128)}, f32[1,1,2,2,2048]{4,3,2,1,0:T(2,128)S(1)}, u32[]{:S(2)}, u32[]{:S(2)}) collective-permute-start(f32[1,1,2,2,2048]{4,3,2,1,0:T(2,128)} %param.5), channel_id=1, source_target_pairs={{0,1},{1,2},{2,3},{3,4},{4,5},{5,6},{6,7},{8,9},{9,10},{10,11},{11... | collective-permute-start | bytes 98312 | tf_op jit(solution)/shard_map/ppermute | solution.py:21
  10.5 10.9 %collective-permute-start.2 = (f32[1,1,2,2,2048]{4,3,2,1,0:T(2,128)}, f32[1,1,2,2,2048]{4,3,2,1,0:T(2,128)S(1)}, u32[]{:S(2)}, u32[]{:S(2)}) collective-permute-start(f32[1,1,2,2,2048]{4,3,2,1,0:T(2,128)} %param.5), channel_id=1, source_target_pairs={{1,0},{2,1},{3,2},{4,3},{5,4},{6,5},{7,6},{9,8},{10,9},{11,10},{12... | collective-permute-start | bytes 98312 | tf_op jit(solution)/shard_map/ppermute | solution.py:23
  13.5 14.8 %collective-permute-start = (bf16[2,2,16,2048]{3,2,1,0:T(8,128)(2,1)S(1)}, bf16[2,2,16,2048]{3,2,1,0:T(8,128)(2,1)S(1)}, u32[]{:S(2)}, u32[]{:S(2)}) collective-permute-start(bf16[2,2,16,2048]{3,2,1,0:T(8,128)(2,1)S(1)} %slice_bitcast_fusion.1), channel_id=1, source_target_pairs={{1,0},{2,1},{3,2},{4,3},{5,4},{6,5},{7,6},{9,8},{10,9},{11,10},{12... | collective-permute-start | bytes 786440 | tf_op jit(solution)/shard_map/ppermute | solution.py:33
  28.2 0.7 copy-start.1
  76.7 5.5 %copy-start = (bf16[1,1,2,64,80]{4,3,2,1,0:T(8,128)(2,1)S(1)}, bf16[1,1,2,64,80]{4,3,2,1,0:T(8,128)(2,1)}, u32[]{:S(2)}) copy-start(bf16[1,1,2,64,80]{4,3,2,1,0:T(8,128)(2,1)} %param.7) | copy-start | bytes 61444
  77.8 14.1 %all-to-all-start.1 = ((bf16[64,2,40]{2,1,0:T(2,128)(2,1)}), bf16[64,2,40]{2,1,0:T(2,128)(2,1)S(1)}, u32[]{:S(2)}, u32[]{:S(2)}) async-start(bf16[64,2,40]{2,1,0:T(2,128)(2,1)} %copy.28), calls=%async_computation.1 | async-start | bytes 65536 | tf_op jit(solution)/shard_map/all_to_all | solution.py:169

commit v5 on v4

--- a/solution.py
+++ b/solution.py
@@ -109,26 +109,29 @@
     return jnp.take(joined.reshape(4, -1), pattern_row, axis=1).reshape(2, 2, -1)
 
 
-def lagged_sums(by_element):
-    energy_count = by_element.shape[0]
-    column_count = by_element.shape[3]
-    lesser = by_element[:, 0].astype(jnp.float32)
-    backward = by_element[::-1, 1].astype(jnp.float32)
-    real_part = (
-        lesser[:, None, 0] * backward[None, :, 0] - lesser[:, None, 1] * backward[None, :, 1]
-    )
-    imag_part = (
-        lesser[:, None, 0] * backward[None, :, 1] + lesser[:, None, 1] * backward[None, :, 0]
-    )
-    joined = jnp.concatenate([real_part, imag_part], axis=2)
-    padded = jnp.pad(joined, ((0, 0), (0, energy_count + 1), (0, 0)))
-    flat_rows = padded.reshape(energy_count * (2 * energy_count + 1), 2 * column_count)
-    skewed = flat_rows[: energy_count * 2 * energy_count].reshape(
-        energy_count, 2 * energy_count, 2 * column_count
-    )
-    totals = jnp.sum(skewed, axis=0)[energy_count - 1 : 2 * energy_count - 1]
-    factor = 1.0 / math.sqrt(energy_count)
-    return (totals.reshape(energy_count, 2, column_count) * factor).astype(jnp.bfloat16)
+def _lag_kernel(in_ref, out_ref, *, width, factor):
+    values = in_ref[...].astype(jnp.float32)
+    energy_count = values.shape[0]
+    lesser = values[:, 0:2 * width]
+    greater = values[:, 2 * width:4 * width]
+    swapped = jnp.concatenate([greater[:, width:], greater[:, :width]], axis=1)
+    rows = []
+    for lag in range(energy_count):
+        head = lesser[lag:]
+        straight = jnp.sum(head * greater[:energy_count - lag], axis=0, keepdims=True)
+        crossed = jnp.sum(head * swapped[:energy_count - lag], axis=0, keepdims=True)
+        rows.append(jnp.concatenate([straight[:, :width] - straight[:, width:], crossed[:, :width] + crossed[:, width:]], axis=1))
+    out_ref[...] = (jnp.concatenate(rows, axis=0) * factor).astype(out_ref.dtype)
+
+
+def lag_sums(by_element):
+    energy_count, joined = by_element.shape
+    width = joined // 4
+    kernel = functools.partial(_lag_kernel, width=width, factor=1.0 / math.sqrt(energy_count))
+    return pl.pallas_call(
+        kernel,
+        out_shape=jax.ShapeDtypeStruct((energy_count, 2 * width), jnp.bfloat16),
+    )(by_element)
 
 
 def screen(polar_row, pattern_row, screen_block):
@@ -163,11 +166,12 @@
     following = passed_along(edge_block, "domain", -1)
     values = element_values(green_slab[0, 0], following, nearby[0], pattern[0])
     chunks = lax.axis_size("energy")
-    values = values.reshape(2, 2, chunks, -1).transpose(2, 0, 1, 3)
+    values = values.reshape(4, chunks, -1).transpose(1, 0, 2).reshape(chunks, -1)
     by_element = lax.all_to_all(values, "energy", split_axis=0, concat_axis=0, tiled=True)
-    polarization = lagged_sums(by_element)
-    per_energy = lax.all_to_all(polarization, "energy", split_axis=0, concat_axis=2, tiled=True)
-    result = screen(per_energy[0], pattern[0], screened[0, 0])
+    polarization = lag_sums(by_element)
+    per_energy = lax.all_to_all(polarization, "energy", split_axis=0, concat_axis=0, tiled=True)
+    per_energy = per_energy.reshape(chunks, 2, -1).transpose(1, 0, 2).reshape(2, -1)
+    result = screen(per_energy, pattern[0], screened[0, 0])
     return result[None, None]
 
 

time: 106 us -> 101 us (0.953)
  other arithmetic: 7.95 us -> 3.87 us
  local copies, waits for them, and re-layouts: 24.4 us -> 20.6 us
  Pallas kernels: 4.34 us -> 7.22 us
    reshape x1 -> x2, local copies, waits for them, and re-layouts: 4.5 us -> 0.53 us  [body(): per_energy.reshape(chunks, 2, -1).transpose(1, 0, 2).reshape(2, -1)]
    concatenate x1 -> x0, other arithmetic: 3 us -> none  [lagged_sums(): joined = jnp.concatenate([real_part, imag_part], axis=2)]
    pallas_call x0 -> x1, Pallas kernels: none -> 2.89 us  [lag_sums(): pl.pallas_call(kernel, out_shape=jax.ShapeDtypeStruct((energy_count, 2 *...]
    all_to_all x1 -> x3, local copies, waits for them, and re-layouts: 0.01 us -> 1.57 us  [the longest x2 1.46 us: body(): lax.all_to_all(polarization, 'energy', split_axis=0, concat_axis=0, tiled...]
    gather x3 -> x2, local copies, waits for them, and re-layouts: 5.47 us -> 5.53 us  [element_values(): jnp.take(joined.reshape(4, -1), pattern_row, axis=1).reshape(2, 2, -1)]
where the time goes in v5:
time: 101 us; the launch traced here: 99.9 us
  blocking collectives  26.9 us (27%)
  local copies, waits for them, and re-layouts  20.6 us (20%)
  waiting for transfers between devices  19.3 us (19%)
  starting transfers between devices  18.8 us (19%)
  Pallas kernels  7.22 us (7%)
  other arithmetic  3.87 us (4%)
  matrix products  3.05 us (3%)
    all_to_all x1, blocking collectives, body(): lax.all_to_all(values, 'energy', split_axis=0, concat_axis=0, tiled=True)  26.9 us
    ppermute x1, starting transfers between devices, padded_2(): lax.ppermute(tail, axis, [(i, (i + 1) % count) for i in range(ends)])  10.5 us
    all_to_all x1, waiting for transfers between devices, body(): lax.all_to_all(polarization, 'energy', split_axis=0, concat_axis=0, tiled...  9.64 us
    scatter x1, local copies, waits for them, and re-layouts, screen(): jnp.zeros((2, row_count * col_count), jnp.bfloat16).at[:, pattern_row]  7.46 us
    gather x2, local copies, waits for them, and re-layouts, element_values(): jnp.take(joined.reshape(4, -1), pattern_row, axis=1).reshape(2, 2, -1)  5.53 us
    ppermute x1, waiting for transfers between devices, passed_along(): return lax.ppermute(x, axis, pairs)  5.32 us
    all_to_all x1, starting transfers between devices, body(): lax.all_to_all(polarization, 'energy', split_axis=0, concat_axis=0, tiled...  4.42 us
    ppermute x1, waiting for transfers between devices, padded_2(): lax.ppermute(head, axis, [((i + 1) % count, i) for i in range(ends)])  4.38 us
  transfers between devices with their start and end apart: 4, of which 3 were waited for; matrix products, arithmetic and copies ran while one was open for 4% of the time, Pallas kernels for 0%

profile of v5, /device:TPU:7, one launch (start us, length us, event | category | flops | bytes accessed | tf_op | source)
XLA Modules:
  0.0 99.9 jit_solution(16040731879390229530)
XLA Ops:
  0.0 10.5 %collective-permute-start.1 = (f32[1,1,2,2,2048]{4,3,2,1,0:T(2,128)}, f32[1,1,2,2,2048]{4,3,2,1,0:T(2,128)S(1)}, u32[]{:S(2)}, u32[]{:S(2)}) collective-permute-start(f32[1,1,2,2,2048]{4,3,2,1,0:T(2,128)} %param.5), channel_id=1, source_target_pairs={{0,1},{1,2},{2,3},{3,4},{4,5},{5,6},{6,7},{8,9},{9,10},{10,11},{11... | collective-permute-start | bytes 98312 | tf_op jit(solution)/shard_map/ppermute | solution.py:21
  10.5 1.9 %collective-permute-start.2 = (f32[1,1,2,2,2048]{4,3,2,1,0:T(2,128)}, f32[1,1,2,2,2048]{4,3,2,1,0:T(2,128)S(1)}, u32[]{:S(2)}, u32[]{:S(2)}) collective-permute-start(f32[1,1,2,2,2048]{4,3,2,1,0:T(2,128)} %param.5), channel_id=1, source_target_pairs={{1,0},{2,1},{3,2},{4,3},{5,4},{6,5},{7,6},{9,8},{10,9},{11,10},{12... | collective-permute-start | bytes 98312 | tf_op jit(solution)/shard_map/ppermute | solution.py:23
  12.5 1.0 slice_bitcast_fusion
  13.5 1.9 %collective-permute-start = (bf16[2,2,16,2048]{3,2,1,0:T(8,128)(2,1)S(1)}, bf16[2,2,16,2048]{3,2,1,0:T(8,128)(2,1)S(1)}, u32[]{:S(2)}, u32[]{:S(2)}) collective-permute-start(bf16[2,2,16,2048]{3,2,1,0:T(8,128)(2,1)S(1)} %slice_bitcast_fusion), channel_id=1, source_target_pairs={{1,0},{2,1},{3,2},{4,3},{5,4},{6,5},{7,6},{9,8},{10,9},{11,10},{12... | collective-permute-start | bytes 786440 | tf_op jit(solution)/shard_map/ppermute | solution.py:33
  15.4 0.7 fusion.32
  16.1 0.7 reduce.1
  16.9 0.1 squeeze.35
  17.0 0.1 copy.32
  17.1 0.0 collective-permute-done.1
  17.1 4.4 %collective-permute-done.2 = f32[1,1,2,2,2048]{4,3,2,1,0:T(2,128)S(1)} collective-permute-done((f32[1,1,2,2,2048]{4,3,2,1,0:T(2,128)}, f32[1,1,2,2,2048]{4,3,2,1,0:T(2,128)S(1)}, u32[]{:S(2)}, u32[]{:S(2)}) %collective-permute-start.2) | collective-permute-done | bytes 32800 | tf_op jit(solution)/shard_map/ppermute | solution.py:23
  21.5 1.4 %maximum_bitcast_fusion.rate_ref = f32[3,2,2,2048]{3,2,1,0:T(2,128)} fusion(f32[1,1,2,2,2048]{4,3,2,1,0:T(2,128)S(1)} %collective-permute-done.2, f32[1,1,2,2,2048]{4,3,2,1,0:T(2,128)} %param.5, f32[1,1,2,2,2048]{4,3,2,1,0:T(2,128)S(1)} %collective-permute-done.1), kind=kLoop, calls=%fused_computation.23 | loop fusion | flops 49152 | bytes 196608 | tf_op jit(solution)/shard_map/squeeze | solution.py:167
  22.9 5.3 %collective-permute-done.edge_ref = bf16[2,2,16,2048]{3,2,1,0:T(8,128)(2,1)S(1)} collective-permute-done((bf16[2,2,16,2048]{3,2,1,0:T(8,128)(2,1)S(1)}, bf16[2,2,16,2048]{3,2,1,0:T(8,128)(2,1)S(1)}, u32[]{:S(2)}, u32[]{:S(2)}) %collective-permute-start) | collective-permute-done | bytes 262176 | tf_op jit(solution)/shard_map/ppermute | solution.py:33
  28.2 0.0 copy-start.1
  28.2 0.7 copy-done.1
  28.9 4.3 %shard_map.46 = f32[2,2,64,80]{3,2,1,0:T(8,128)} custom-call(bf16[2,3,64,2048]{3,2,1,0:T(8,128)(2,1)} %bitcast.53, bf16[2,2,16,2048]{3,2,1,0:T(8,128)(2,1)} %copy-done.1, f32[3,2,2,2048]{3,2,1,0:T(2,128)} %maximum_bitcast_fusion.rate_ref), custom_call_target="tpu_custom_call" | custom-call | tf_op jit(solution)/shard_map/pallas_call | solution.py:94
  33.3 0.9 convert_element_type.17
  34.2 0.2 reshape.65
  34.3 0.0 copy-start
  34.3 0.6 copy.33
  34.9 5.1 %gather_fusion = bf16[2560,4]{1,0:T(8,128)(2,1)S(1)} fusion(bf16[4,5120]{0,1:T(8,128)(2,1)S(1)} %copy.33, s32[3072]{0:T(1024)S(1)} %pad_clamp_fusion), kind=kCustom, calls=%fused_computation | custom fusion | bytes 51200 | tf_op jit(solution)/shard_map/jit(_take)/gather | solution.py:109
  40.0 0.5 copy.34
  40.5 0.1 copy.35
  40.6 26.9 %all_to_all.20 = bf16[64,1,160]{2,1,0:T(2,128)(2,1)S(1)} all-to-all(bf16[64,1,160]{2,1,0:T(2,128)(2,1)S(1)} %copy.35), channel_id=1, replica_groups=mesh['energy'=64,'domain'=8] {'energy'}, dimensions={0} | all-to-all | bytes 40960 | tf_op jit(solution)/shard_map/all_to_all | solution.py:170
  67.5 0.6 copy.43
  68.1 2.9 %shard_map.47 = bf16[64,80]{1,0:T(8,128)(2,1)} custom-call(bf16[64,160]{1,0:T(8,128)(2,1)} %bitcast.56), custom_call_target="tpu_custom_call" | custom-call | tf_op jit(solution)/shard_map/pallas_call | solution.py:131
  71.0 1.4 %copy.36 = bf16[64,1,80]{2,1,0:T(2,128)(2,1)} copy(bf16[64,1,80]{2,0,1:T(8,128)(2,1)} %bitcast.58) | data formatting | bytes 20480 | tf_op jit(solution)/shard_map/all_to_all | solution.py:172
  72.4 4.4 %all-to-all-start.1 = ((bf16[64,1,80]{2,1,0:T(2,128)(2,1)}), bf16[64,1,80]{2,1,0:T(2,128)(2,1)S(1)}, u32[]{:S(2)}, u32[]{:S(2)}) async-start(bf16[64,1,80]{2,1,0:T(2,128)(2,1)} %copy.36), calls=%async_computation.1 | async-start | bytes 65536 | tf_op jit(solution)/shard_map/all_to_all | solution.py:172
  76.8 0.0 copy-done
  76.8 9.6 %all-to-all-done.1 = bf16[64,1,80]{2,1,0:T(2,128)(2,1)S(1)} async-done(((bf16[64,1,80]{2,1,0:T(2,128)(2,1)}), bf16[64,1,80]{2,1,0:T(2,128)(2,1)S(1)}, u32[]{:S(2)}, u32[]{:S(2)}) %all-to-all-start.1) | async-done | bytes 10272 | tf_op jit(solution)/shard_map/all_to_all | solution.py:172
  86.5 0.1 copy.37
  86.6 0.1 copy.38
  86.7 0.1 reshape.77
  86.8 0.4 copy.39
  87.2 7.5 %scatter_custom_fusion = bf16[2,5120]{0,1:T(8,128)(2,1)S(1)} fusion(s32[2560]{0:T(1024)S(1)} %fusion.32, bf16[2560,2]{1,0:T(8,128)(2,1)S(1)} %copy.39, bf16[]{:T(256)} %constant.6.clone.1), kind=kCustom, calls=%fused_computation.20 | custom fusion | bytes 20482 | tf_op jit(solution)/shard_map/scatter | solution.py:141
  94.7 1.2 %slice_reduce_fusion.1 = (bf16[5120]{0:T(1024)(128)(2,1)S(1)}, bf16[5120]{0:T(1024)(128)(2,1)S(1)}) fusion(bf16[2,5120]{0,1:T(8,128)(2,1)S(1)} %scatter_custom_fusion), kind=kLoop, calls=%fused_computation.3 | loop fusion | bytes 40960 | tf_op jit(solution)/shard_map/slice | solution.py:145
  95.9 0.1 squeeze.39
  96.0 0.1 fusion.34
  96.1 0.1 squeeze.41
  96.2 0.1 fusion.33
  96.4 0.2 fusion.20
  96.6 0.2 fusion.16
  96.8 0.2 fusion.6
  97.1 0.2 fusion.14
  97.3 0.2 fusion.10
  97.5 0.1 fusion.4
  97.6 0.2 fusion.30
  97.8 0.1 fusion.5
  98.0 0.2 fusion.26
  98.2 0.2 convolution_subtract_fusion.1
  98.3 0.2 fusion.7
  98.6 0.2 convolution_add_fusion
  98.8 0.2 fusion.3
  99.0 0.2 fusion.1
  99.2 0.7 copy.40
  (5 shorter events, 0.1 us)
Async XLA Ops:
  0.0 17.1 %collective-permute-start.1 = (f32[1,1,2,2,2048]{4,3,2,1,0:T(2,128)}, f32[1,1,2,2,2048]{4,3,2,1,0:T(2,128)S(1)}, u32[]{:S(2)}, u32[]{:S(2)}) collective-permute-start(f32[1,1,2,2,2048]{4,3,2,1,0:T(2,128)} %param.5), channel_id=1, source_target_pairs={{0,1},{1,2},{2,3},{3,4},{4,5},{5,6},{6,7},{8,9},{9,10},{10,11},{11... | collective-permute-start | bytes 98312 | tf_op jit(solution)/shard_map/ppermute | solution.py:21
  10.5 10.9 %collective-permute-start.2 = (f32[1,1,2,2,2048]{4,3,2,1,0:T(2,128)}, f32[1,1,2,2,2048]{4,3,2,1,0:T(2,128)S(1)}, u32[]{:S(2)}, u32[]{:S(2)}) collective-permute-start(f32[1,1,2,2,2048]{4,3,2,1,0:T(2,128)} %param.5), channel_id=1, source_target_pairs={{1,0},{2,1},{3,2},{4,3},{5,4},{6,5},{7,6},{9,8},{10,9},{11,10},{12... | collective-permute-start | bytes 98312 | tf_op jit(solution)/shard_map/ppermute | solution.py:23
  13.5 14.8 %collective-permute-start = (bf16[2,2,16,2048]{3,2,1,0:T(8,128)(2,1)S(1)}, bf16[2,2,16,2048]{3,2,1,0:T(8,128)(2,1)S(1)}, u32[]{:S(2)}, u32[]{:S(2)}) collective-permute-start(bf16[2,2,16,2048]{3,2,1,0:T(8,128)(2,1)S(1)} %slice_bitcast_fusion), channel_id=1, source_target_pairs={{1,0},{2,1},{3,2},{4,3},{5,4},{6,5},{7,6},{9,8},{10,9},{11,10},{12... | collective-permute-start | bytes 786440 | tf_op jit(solution)/shard_map/ppermute | solution.py:33
  28.2 0.7 copy-start.1
  34.3 42.5 %copy-start = (bf16[1,1,2,64,80]{4,3,2,1,0:T(8,128)(2,1)S(1)}, bf16[1,1,2,64,80]{4,3,2,1,0:T(8,128)(2,1)}, u32[]{:S(2)}) copy-start(bf16[1,1,2,64,80]{4,3,2,1,0:T(8,128)(2,1)} %param.7) | copy-start | bytes 61444
  72.4 14.1 %all-to-all-start.1 = ((bf16[64,1,80]{2,1,0:T(2,128)(2,1)}), bf16[64,1,80]{2,1,0:T(2,128)(2,1)S(1)}, u32[]{:S(2)}, u32[]{:S(2)}) async-start(bf16[64,1,80]{2,1,0:T(2,128)(2,1)} %copy.36), calls=%async_computation.1 | async-start | bytes 65536 | tf_op jit(solution)/shard_map/all_to_all | solution.py:172

commit v6 on v5

--- a/solution.py
+++ b/solution.py
@@ -5,9 +5,10 @@
 import jax.numpy as jnp
 from jax import lax
 from jax.experimental import pallas as pl
-from jax.sharding import PartitionSpec as P
+from jax.sharding import Mesh, PartitionSpec as P
 
 EDGE = 16
+ENERGY = ("energy_outer", "energy_inner")
 
 
 def padded_2(cells, sides, width):
@@ -160,32 +161,50 @@
     return jnp.stack([first_real + second_real, first_imag + second_imag], axis=0)
 
 
+def staged_all_to_all(chunked):
+    outer = lax.axis_size(ENERGY[0])
+    inner = lax.axis_size(ENERGY[1])
+    rest = chunked.shape[1:]
+    grid = chunked.reshape(outer, inner, *rest)
+    grid = lax.all_to_all(grid, ENERGY[1], split_axis=1, concat_axis=1, tiled=True)
+    grid = lax.all_to_all(grid, ENERGY[0], split_axis=0, concat_axis=0, tiled=True)
+    return grid.reshape(outer * inner, *rest)
+
+
 def body(green_slab, self_energy, pattern, screened):
     nearby = padded_2(self_energy, (("domain", 1),), 1)
     edge_block = green_slab[0, 0, :, 0:2, :EDGE, :]
     following = passed_along(edge_block, "domain", -1)
     values = element_values(green_slab[0, 0], following, nearby[0], pattern[0])
-    chunks = lax.axis_size("energy")
+    chunks = lax.axis_size(ENERGY)
     values = values.reshape(4, chunks, -1).transpose(1, 0, 2).reshape(chunks, -1)
-    by_element = lax.all_to_all(values, "energy", split_axis=0, concat_axis=0, tiled=True)
+    by_element = staged_all_to_all(values)
     polarization = lag_sums(by_element)
-    per_energy = lax.all_to_all(polarization, "energy", split_axis=0, concat_axis=0, tiled=True)
+    per_energy = staged_all_to_all(polarization)
     per_energy = per_energy.reshape(chunks, 2, -1).transpose(1, 0, 2).reshape(2, -1)
     result = screen(per_energy, pattern[0], screened[0, 0])
     return result[None, None]
 
 
 def solution(mesh):
+    energy_count = mesh.shape["energy"]
+    outer = 1
+    while outer * outer < energy_count:
+        outer *= 2
+    staged = Mesh(
+        mesh.devices.reshape(outer, energy_count // outer, mesh.shape["domain"]),
+        (*ENERGY, "domain"),
+    )
     placed = (
-        P("energy", "domain", None, None, None, None),
-        P("energy", "domain", None, None, None),
+        P(ENERGY, "domain", None, None, None, None),
+        P(ENERGY, "domain", None, None, None),
         P("domain", None),
-        P("energy", "domain", None, None, None),
+        P(ENERGY, "domain", None, None, None),
     )
     return jax.shard_map(
         body,
-        mesh=mesh,
+        mesh=staged,
         in_specs=placed,
-        out_specs=P("energy", "domain", None, None, None),
+        out_specs=P(ENERGY, "domain", None, None, None),
         check_vma=False,
     )

time: 101 us -> 109 us (1.079)
  blocking collectives: 26.9 us -> 39 us
  waiting for transfers between devices: 19.3 us -> 16.3 us
  starting transfers between devices: 18.8 us -> 17.7 us
    all_to_all x1 -> x3, blocking collectives: 26.9 us -> 39 us  [the longest x2 25.4 us: staged_all_to_all(): lax.all_to_all(grid, ENERGY[1], split_axis=1, concat_axis=1, tiled=True)]
    all_to_all x1, waiting for transfers between devices: 9.64 us -> 6.52 us  [staged_all_to_all(): lax.all_to_all(grid, ENERGY[0], split_axis=0, concat_axis=0, tiled=True)]
where the time goes in v6:
time: 109 us; the launch traced here: 107 us
  blocking collectives  39 us (36%)
  local copies, waits for them, and re-layouts  19.7 us (18%)
  starting transfers between devices  17.7 us (16%)
  waiting for transfers between devices  16.3 us (15%)
  Pallas kernels  7.23 us (7%)
  other arithmetic  3.92 us (4%)
  matrix products  3.05 us (3%)
    all_to_all x2, blocking collectives, staged_all_to_all(): lax.all_to_all(grid, ENERGY[1], split_axis=1, concat_axis=1, tiled=True)  25.4 us
    all_to_all x1, blocking collectives, staged_all_to_all(): lax.all_to_all(grid, ENERGY[0], split_axis=0, concat_axis=0, tiled=True)  13.6 us
    ppermute x1, starting transfers between devices, padded_2(): lax.ppermute(tail, axis, [(i, (i + 1) % count) for i in range(ends)])  10.5 us
    scatter x1, local copies, waits for them, and re-layouts, screen(): jnp.zeros((2, row_count * col_count), jnp.bfloat16).at[:, pattern_row]  7.46 us
    all_to_all x1, waiting for transfers between devices, staged_all_to_all(): lax.all_to_all(grid, ENERGY[0], split_axis=0, concat_axis=0, tiled=True)  6.52 us
    gather x2, local copies, waits for them, and re-layouts, element_values(): jnp.take(joined.reshape(4, -1), pattern_row, axis=1).reshape(2, 2, -1)  5.54 us
    ppermute x1, waiting for transfers between devices, passed_along(): return lax.ppermute(x, axis, pairs)  5.32 us
    ppermute x1, waiting for transfers between devices, padded_2(): lax.ppermute(head, axis, [((i + 1) % count, i) for i in range(ends)])  4.47 us
  transfers between devices with their start and end apart: 4, of which 3 were waited for; matrix products, arithmetic and copies ran while one was open for 4% of the time, Pallas kernels for 0%

profile of v6, /device:TPU:7, one launch (start us, length us, event | category | flops | bytes accessed | tf_op | source)
XLA Modules:
  0.0 107.1 jit_solution(9074865183139737936)
XLA Ops:
  0.0 10.5 %collective-permute-start.1 = (f32[1,1,2,2,2048]{4,3,2,1,0:T(2,128)}, f32[1,1,2,2,2048]{4,3,2,1,0:T(2,128)S(1)}, u32[]{:S(2)}, u32[]{:S(2)}) collective-permute-start(f32[1,1,2,2,2048]{4,3,2,1,0:T(2,128)} %param.5), channel_id=1, source_target_pairs={{0,1},{1,2},{2,3},{3,4},{4,5},{5,6},{6,7},{8,9},{9,10},{10,11},{11... | collective-permute-start | bytes 98312 | tf_op jit(solution)/shard_map/ppermute | solution.py:22
  10.5 1.9 %collective-permute-start.2 = (f32[1,1,2,2,2048]{4,3,2,1,0:T(2,128)}, f32[1,1,2,2,2048]{4,3,2,1,0:T(2,128)S(1)}, u32[]{:S(2)}, u32[]{:S(2)}) collective-permute-start(f32[1,1,2,2,2048]{4,3,2,1,0:T(2,128)} %param.5), channel_id=1, source_target_pairs={{1,0},{2,1},{3,2},{4,3},{5,4},{6,5},{7,6},{9,8},{10,9},{11,10},{12... | collective-permute-start | bytes 98312 | tf_op jit(solution)/shard_map/ppermute | solution.py:24
  12.5 1.0 slice_bitcast_fusion
  13.5 1.9 %collective-permute-start = (bf16[2,2,16,2048]{3,2,1,0:T(8,128)(2,1)S(1)}, bf16[2,2,16,2048]{3,2,1,0:T(8,128)(2,1)S(1)}, u32[]{:S(2)}, u32[]{:S(2)}) collective-permute-start(bf16[2,2,16,2048]{3,2,1,0:T(8,128)(2,1)S(1)} %slice_bitcast_fusion), channel_id=1, source_target_pairs={{1,0},{2,1},{3,2},{4,3},{5,4},{6,5},{7,6},{9,8},{10,9},{11,10},{12... | collective-permute-start | bytes 786440 | tf_op jit(solution)/shard_map/ppermute | solution.py:34
  15.4 0.7 fusion.32
  16.1 0.7 reduce.1
  16.9 0.1 squeeze.35
  17.0 0.0 collective-permute-done.1
  17.0 4.5 %collective-permute-done.2 = f32[1,1,2,2,2048]{4,3,2,1,0:T(2,128)S(1)} collective-permute-done((f32[1,1,2,2,2048]{4,3,2,1,0:T(2,128)}, f32[1,1,2,2,2048]{4,3,2,1,0:T(2,128)S(1)}, u32[]{:S(2)}, u32[]{:S(2)}) %collective-permute-start.2) | collective-permute-done | bytes 32800 | tf_op jit(solution)/shard_map/ppermute | solution.py:24
  21.5 1.4 %maximum_bitcast_fusion.rate_ref = f32[3,2,2,2048]{3,2,1,0:T(2,128)} fusion(f32[1,1,2,2,2048]{4,3,2,1,0:T(2,128)S(1)} %collective-permute-done.2, f32[1,1,2,2,2048]{4,3,2,1,0:T(2,128)} %param.5, f32[1,1,2,2,2048]{4,3,2,1,0:T(2,128)S(1)} %collective-permute-done.1), kind=kLoop, calls=%fused_computation.23 | loop fusion | flops 49152 | bytes 196608 | tf_op jit(solution)/shard_map/squeeze | solution.py:178
  22.9 5.3 %collective-permute-done.edge_ref = bf16[2,2,16,2048]{3,2,1,0:T(8,128)(2,1)S(1)} collective-permute-done((bf16[2,2,16,2048]{3,2,1,0:T(8,128)(2,1)S(1)}, bf16[2,2,16,2048]{3,2,1,0:T(8,128)(2,1)S(1)}, u32[]{:S(2)}, u32[]{:S(2)}) %collective-permute-start) | collective-permute-done | bytes 262176 | tf_op jit(solution)/shard_map/ppermute | solution.py:34
  28.2 0.0 copy-start.1
  28.2 0.7 copy-done.1
  28.9 4.3 %shard_map.46 = f32[2,2,64,80]{3,2,1,0:T(8,128)} custom-call(bf16[2,3,64,2048]{3,2,1,0:T(8,128)(2,1)} %bitcast.48, bf16[2,2,16,2048]{3,2,1,0:T(8,128)(2,1)} %copy-done.1, f32[3,2,2,2048]{3,2,1,0:T(2,128)} %maximum_bitcast_fusion.rate_ref), custom_call_target="tpu_custom_call" | custom-call | tf_op jit(solution)/shard_map/pallas_call | solution.py:95
  33.3 0.9 convert_element_type.17
  34.2 0.2 reshape.61
  34.3 0.0 copy-start
  34.3 0.6 copy.26
  34.9 5.1 %gather_fusion = bf16[2560,4]{1,0:T(8,128)(2,1)S(1)} fusion(bf16[4,5120]{0,1:T(8,128)(2,1)S(1)} %copy.26, s32[3072]{0:T(1024)S(1)} %pad_clamp_fusion), kind=kCustom, calls=%fused_computation | custom fusion | bytes 51200 | tf_op jit(solution)/shard_map/jit(_take)/gather | solution.py:110
  40.0 0.5 copy.27
  40.5 0.1 select_bitcast_fusion
  40.6 0.1 reshape_reshape.7
  40.7 15.9 %all_to_all.20 = bf16[8,8,160]{2,0,1:T(8,128)(2,1)S(1)} all-to-all(bf16[8,8,160]{2,0,1:T(8,128)(2,1)S(1)} %copy.28), channel_id=1, replica_groups=mesh['energy_outer'=8,'energy_inner'=8,'domain'=8] {'energy_inner'}, dimensions={1} | all-to-all | bytes 40960 | tf_op jit(solution)/shard_map/all_to_all | solution.py:169
  56.6 13.6 %all_to_all.21 = bf16[8,8,160]{2,1,0:T(8,128)(2,1)} all-to-all(bf16[8,8,160]{2,1,0:T(8,128)(2,1)S(1)} %copy.29), channel_id=1, replica_groups=mesh['energy_outer'=8,'energy_inner'=8,'domain'=8] {'energy_outer'}, dimensions={0} | all-to-all | bytes 40960 | tf_op jit(solution)/shard_map/all_to_all | solution.py:170
  70.2 2.9 %shard_map.47 = bf16[64,80]{1,0:T(8,128)(2,1)} custom-call(bf16[64,160]{1,0:T(8,128)(2,1)} %bitcast.50), custom_call_target="tpu_custom_call" | custom-call | tf_op jit(solution)/shard_map/pallas_call | solution.py:132
  73.1 0.7 copy.30
  73.8 9.5 %all_to_all.22 = bf16[8,8,80]{2,0,1:T(8,128)(2,1)S(1)} all-to-all(bf16[8,8,80]{2,0,1:T(8,128)(2,1)S(1)} %copy.30), channel_id=1, replica_groups=mesh['energy_outer'=8,'energy_inner'=8,'domain'=8] {'energy_inner'}, dimensions={1} | all-to-all | bytes 20480 | tf_op jit(solution)/shard_map/all_to_all | solution.py:169
  83.3 0.6 copy.31
  83.9 3.3 %all-to-all-start.3 = ((bf16[8,8,80]{2,1,0:T(8,128)(2,1)}), bf16[8,8,80]{2,1,0:T(8,128)(2,1)S(1)}, u32[]{:S(2)}, u32[]{:S(2)}) async-start(bf16[8,8,80]{2,1,0:T(8,128)(2,1)} %copy.31), calls=%async_computation.3 | async-start | bytes 32768 | tf_op jit(solution)/shard_map/all_to_all | solution.py:170
  87.2 0.0 copy-done
  87.3 6.5 %all-to-all-done.3 = bf16[8,8,80]{2,1,0:T(8,128)(2,1)S(1)} async-done(((bf16[8,8,80]{2,1,0:T(8,128)(2,1)}), bf16[8,8,80]{2,1,0:T(8,128)(2,1)S(1)}, u32[]{:S(2)}, u32[]{:S(2)}) %all-to-all-start.3) | async-done | bytes 10272 | tf_op jit(solution)/shard_map/all_to_all | solution.py:170
  93.8 0.1 reshape_reshape.8
  93.9 0.1 reshape.74
  94.0 0.4 copy.33
  94.4 7.5 %scatter_custom_fusion = bf16[2,5120]{0,1:T(8,128)(2,1)S(1)} fusion(s32[2560]{0:T(1024)S(1)} %fusion.32, bf16[2560,2]{1,0:T(8,128)(2,1)S(1)} %copy.33, bf16[]{:T(256)} %constant.6.clone.1), kind=kCustom, calls=%fused_computation.20 | custom fusion | bytes 20482 | tf_op jit(solution)/shard_map/scatter | solution.py:142
  101.9 1.2 %slice_reduce_fusion.1 = (bf16[5120]{0:T(1024)(128)(2,1)S(1)}, bf16[5120]{0:T(1024)(128)(2,1)S(1)}) fusion(bf16[2,5120]{0,1:T(8,128)(2,1)S(1)} %scatter_custom_fusion), kind=kLoop, calls=%fused_computation.3 | loop fusion | bytes 40960 | tf_op jit(solution)/shard_map/slice | solution.py:146
  103.1 0.1 squeeze.39
  103.2 0.1 fusion.34
  103.3 0.1 squeeze.41
  103.4 0.1 fusion.33
  103.6 0.2 fusion.20
  103.8 0.2 fusion.16
  104.0 0.2 fusion.6
  104.3 0.2 fusion.14
  104.5 0.2 fusion.10
  104.7 0.1 fusion.4
  104.8 0.2 fusion.30
  105.0 0.1 fusion.5
  105.2 0.2 fusion.26
  105.3 0.2 convolution_subtract_fusion.1
  105.5 0.2 fusion.7
  105.8 0.2 convolution_add_fusion
  106.0 0.2 fusion.3
  106.2 0.2 fusion.1
  106.4 0.7 copy.34
  (7 shorter events, 0.1 us)
Async XLA Ops:
  0.0 17.0 %collective-permute-start.1 = (f32[1,1,2,2,2048]{4,3,2,1,0:T(2,128)}, f32[1,1,2,2,2048]{4,3,2,1,0:T(2,128)S(1)}, u32[]{:S(2)}, u32[]{:S(2)}) collective-permute-start(f32[1,1,2,2,2048]{4,3,2,1,0:T(2,128)} %param.5), channel_id=1, source_target_pairs={{0,1},{1,2},{2,3},{3,4},{4,5},{5,6},{6,7},{8,9},{9,10},{10,11},{11... | collective-permute-start | bytes 98312 | tf_op jit(solution)/shard_map/ppermute | solution.py:22
  10.5 10.9 %collective-permute-start.2 = (f32[1,1,2,2,2048]{4,3,2,1,0:T(2,128)}, f32[1,1,2,2,2048]{4,3,2,1,0:T(2,128)S(1)}, u32[]{:S(2)}, u32[]{:S(2)}) collective-permute-start(f32[1,1,2,2,2048]{4,3,2,1,0:T(2,128)} %param.5), channel_id=1, source_target_pairs={{1,0},{2,1},{3,2},{4,3},{5,4},{6,5},{7,6},{9,8},{10,9},{11,10},{12... | collective-permute-start | bytes 98312 | tf_op jit(solution)/shard_map/ppermute | solution.py:24
  13.5 14.8 %collective-permute-start = (bf16[2,2,16,2048]{3,2,1,0:T(8,128)(2,1)S(1)}, bf16[2,2,16,2048]{3,2,1,0:T(8,128)(2,1)S(1)}, u32[]{:S(2)}, u32[]{:S(2)}) collective-permute-start(bf16[2,2,16,2048]{3,2,1,0:T(8,128)(2,1)S(1)} %slice_bitcast_fusion), channel_id=1, source_target_pairs={{1,0},{2,1},{3,2},{4,3},{5,4},{6,5},{7,6},{9,8},{10,9},{11,10},{12... | collective-permute-start | bytes 786440 | tf_op jit(solution)/shard_map/ppermute | solution.py:34
  28.2 0.7 copy-start.1
  34.3 52.9 %copy-start = (bf16[1,1,2,64,80]{4,3,2,1,0:T(8,128)(2,1)S(1)}, bf16[1,1,2,64,80]{4,3,2,1,0:T(8,128)(2,1)}, u32[]{:S(2)}) copy-start(bf16[1,1,2,64,80]{4,3,2,1,0:T(8,128)(2,1)} %param.7) | copy-start | bytes 61444
  83.9 9.9 %all-to-all-start.3 = ((bf16[8,8,80]{2,1,0:T(8,128)(2,1)}), bf16[8,8,80]{2,1,0:T(8,128)(2,1)S(1)}, u32[]{:S(2)}, u32[]{:S(2)}) async-start(bf16[8,8,80]{2,1,0:T(8,128)(2,1)} %copy.31), calls=%async_computation.3 | async-start | bytes 32768 | tf_op jit(solution)/shard_map/all_to_all | solution.py:170

commit v7 on v5

--- a/solution.py
+++ b/solution.py
@@ -31,26 +31,6 @@
     length = lax.axis_size(axis)
     pairs = [(i, i + by) for i in range(length) if 0 <= i + by < length]
     return lax.ppermute(x, axis, pairs)
-
-
-def times_adjoint(left_real, left_imag, right_real, right_imag):
-    real_sum = jnp.dot(left_real, right_real.T, preferred_element_type=jnp.float32) + jnp.dot(
-        left_imag, right_imag.T, preferred_element_type=jnp.float32
-    )
-    imag_sum = jnp.dot(left_imag, right_real.T, preferred_element_type=jnp.float32) - jnp.dot(
-        left_real, right_imag.T, preferred_element_type=jnp.float32
-    )
-    return (real_sum, imag_sum)
-
-
-def complex_product(left_real, left_imag, right_real, right_imag):
-    real_sum = jnp.dot(left_real, right_real, preferred_element_type=jnp.float32) - jnp.dot(
-        left_imag, right_imag, preferred_element_type=jnp.float32
-    )
-    imag_sum = jnp.dot(left_real, right_imag, preferred_element_type=jnp.float32) + jnp.dot(
-        left_imag, right_real, preferred_element_type=jnp.float32
-    )
-    return (real_sum, imag_sum)
 
 
 def _weigh_kernel(slab_ref, edge_ref, rate_ref, out_ref, *, factor, rows, edge):
@@ -134,30 +114,51 @@
     )(by_element)
 
 
+def _screen_kernel(dense_ref, screen_ref, out_ref, *, rows):
+    def nt(a, b):
+        return lax.dot_general(a, b, (((1,), (1,)), ((), ())), preferred_element_type=jnp.float32)
+
+    def nn(a, b):
+        return jnp.dot(a, b, preferred_element_type=jnp.float32)
+
+    dense_real = dense_ref[0]
+    dense_imag = dense_ref[1]
+    screen_real = screen_ref[0]
+    screen_imag = screen_ref[1]
+    inner_real = (nt(dense_real, screen_real) + nt(dense_imag, screen_imag)).astype(jnp.bfloat16)
+    inner_imag = (nt(dense_imag, screen_real) - nt(dense_real, screen_imag)).astype(jnp.bfloat16)
+    near_real = screen_real[:, :rows]
+    near_imag = screen_imag[:, :rows]
+    side_real = screen_real[:, rows:]
+    side_imag = screen_imag[:, rows:]
+    edge_real = dense_real[:, rows:]
+    edge_imag = dense_imag[:, rows:]
+    across_real = (nn(near_real, edge_real) - nn(near_imag, edge_imag)).astype(jnp.bfloat16)
+    across_imag = (nn(near_real, edge_imag) + nn(near_imag, edge_real)).astype(jnp.bfloat16)
+    first_real = nn(near_real, inner_real) - nn(near_imag, inner_imag)
+    first_imag = nn(near_real, inner_imag) + nn(near_imag, inner_real)
+    second_real = nt(side_real, across_real) + nt(side_imag, across_imag)
+    second_imag = nt(side_imag, across_real) - nt(side_real, across_imag)
+    out_ref[0] = first_real + second_real
+    out_ref[1] = first_imag + second_imag
+
+
+def screen_products(dense_pol, screen_block):
+    rows = screen_block.shape[1]
+    kernel = functools.partial(_screen_kernel, rows=rows)
+    return pl.pallas_call(
+        kernel,
+        out_shape=jax.ShapeDtypeStruct((2, rows, rows), jnp.float32),
+    )(dense_pol, screen_block)
+
+
 def screen(polar_row, pattern_row, screen_block):
     row_count = screen_block.shape[1]
     col_count = screen_block.shape[2]
     flat_dense = (
         jnp.zeros((2, row_count * col_count), jnp.bfloat16).at[:, pattern_row].set(polar_row)
     )
-    dense_pol = flat_dense.reshape(2, row_count, col_count)
-    inner_real, inner_imag = times_adjoint(
-        dense_pol[0], dense_pol[1], screen_block[0], screen_block[1]
-    )
-    inner_real = inner_real.astype(jnp.bfloat16)
-    inner_imag = inner_imag.astype(jnp.bfloat16)
-    near_real = screen_block[0][:, :row_count]
-    near_imag = screen_block[1][:, :row_count]
-    across_real, across_imag = complex_product(
-        near_real, near_imag, dense_pol[0][:, row_count:], dense_pol[1][:, row_count:]
-    )
-    across_real = across_real.astype(jnp.bfloat16)
-    across_imag = across_imag.astype(jnp.bfloat16)
-    first_real, first_imag = complex_product(near_real, near_imag, inner_real, inner_imag)
-    second_real, second_imag = times_adjoint(
-        screen_block[0][:, row_count:], screen_block[1][:, row_count:], across_real, across_imag
-    )
-    return jnp.stack([first_real + second_real, first_imag + second_imag], axis=0)
+    return screen_products(flat_dense.reshape(2, row_count, col_count), screen_block)
 
 
 def body(green_slab, self_energy, pattern, screened):

time: 101 us -> 96.9 us (0.959)
  blocking collectives: 26.9 us -> 40.2 us
  waiting for transfers between devices: 19.3 us -> 9.7 us
  starting transfers between devices: 18.8 us -> 14.4 us
  matrix products: 3.05 us -> 0 us
  Pallas kernels: 7.22 us -> 9 us
  local copies, waits for them, and re-layouts: 20.6 us -> 18.9 us
    all_to_all x0 -> x1, blocking collectives: none -> 13.4 us  [body(): lax.all_to_all(polarization, 'energy', split_axis=0, concat_axis=0, tiled...]
    all_to_all x1 -> x0, waiting for transfers between devices: 9.64 us -> none  [body(): lax.all_to_all(polarization, 'energy', split_axis=0, concat_axis=0, tiled...]
    all_to_all x1 -> x0, starting transfers between devices: 4.42 us -> none  [body(): lax.all_to_all(polarization, 'energy', split_axis=0, concat_axis=0, tiled...]
    dot_general x16 -> x0, matrix products: 3.05 us -> none  [the longest x2 0.43 us: complex_product(): jnp.dot(left_real, right_real, preferred_element_type=jnp.float32)]
    pallas_call x0 -> x1, Pallas kernels: none -> 1.77 us  [screen_products(): pl.pallas_call(kernel, out_shape=jax.ShapeDtypeStruct((2, rows, rows), jn...]
    slice x1 -> x0, local copies, waits for them, and re-layouts: 1.23 us -> none  [screen(): dense_pol[0]]
    reshape x0 -> x1, local copies, waits for them, and re-layouts: none -> 1.12 us  [screen(): flat_dense.reshape(2, row_count, col_count)]
  transfers between devices with their start and end apart: 4 -> 3, of which waited for: 3 -> 2; matrix products, arithmetic and copies ran while one was open for 4% -> 4% of each run, Pallas kernels for 0% -> 0%
where the time goes in v7:
time: 96.9 us; the launch traced here: 96.2 us
  blocking collectives  40.2 us (41%)
  local copies, waits for them, and re-layouts  18.9 us (20%)
  starting transfers between devices  14.4 us (15%)
  waiting for transfers between devices  9.7 us (10%)
  Pallas kernels  9 us (9%)
  other arithmetic  3.85 us (4%)
    all_to_all x1, blocking collectives, body(): lax.all_to_all(values, 'energy', split_axis=0, concat_axis=0, tiled=True)  26.9 us
    all_to_all x1, blocking collectives, body(): lax.all_to_all(polarization, 'energy', split_axis=0, concat_axis=0, tiled...  13.4 us
    ppermute x1, starting transfers between devices, padded_2(): lax.ppermute(tail, axis, [(i, (i + 1) % count) for i in range(ends)])  10.5 us
    scatter x1, local copies, waits for them, and re-layouts, screen(): jnp.zeros((2, row_count * col_count), jnp.bfloat16).at[:, pattern_row]  7.46 us
    gather x2, local copies, waits for them, and re-layouts, element_values(): jnp.take(joined.reshape(4, -1), pattern_row, axis=1).reshape(2, 2, -1)  5.53 us
    ppermute x1, waiting for transfers between devices, passed_along(): return lax.ppermute(x, axis, pairs)  5.32 us
    ppermute x1, waiting for transfers between devices, padded_2(): lax.ppermute(head, axis, [((i + 1) % count, i) for i in range(ends)])  4.38 us
    pallas_call x1, Pallas kernels, weighed_products(): pl.pallas_call(kernel, grid=(blocks,), in_specs=[pl.BlockSpec((2, 1, rows...  4.34 us
  transfers between devices with their start and end apart: 3, of which 2 were waited for; matrix products, arithmetic and copies ran while one was open for 4% of the time, Pallas kernels for 0%

profile of v7, /device:TPU:7, one launch (start us, length us, event | category | flops | bytes accessed | tf_op | source)
XLA Modules:
  0.0 96.2 jit_solution(12130550033904481635)
XLA Ops:
  0.0 10.5 %collective-permute-start.1 = (f32[1,1,2,2,2048]{4,3,2,1,0:T(2,128)}, f32[1,1,2,2,2048]{4,3,2,1,0:T(2,128)S(1)}, u32[]{:S(2)}, u32[]{:S(2)}) collective-permute-start(f32[1,1,2,2,2048]{4,3,2,1,0:T(2,128)} %param.5), channel_id=1, source_target_pairs={{0,1},{1,2},{2,3},{3,4},{4,5},{5,6},{6,7},{8,9},{9,10},{10,11},{11... | collective-permute-start | bytes 98312 | tf_op jit(solution)/shard_map/ppermute | solution.py:21
  10.5 1.9 %collective-permute-start.2 = (f32[1,1,2,2,2048]{4,3,2,1,0:T(2,128)}, f32[1,1,2,2,2048]{4,3,2,1,0:T(2,128)S(1)}, u32[]{:S(2)}, u32[]{:S(2)}) collective-permute-start(f32[1,1,2,2,2048]{4,3,2,1,0:T(2,128)} %param.5), channel_id=1, source_target_pairs={{1,0},{2,1},{3,2},{4,3},{5,4},{6,5},{7,6},{9,8},{10,9},{11,10},{12... | collective-permute-start | bytes 98312 | tf_op jit(solution)/shard_map/ppermute | solution.py:23
  12.5 1.0 %slice_bitcast_fusion = bf16[2,2,16,2048]{3,2,1,0:T(8,128)(2,1)S(1)} fusion(bf16[1,1,2,3,64,2048]{5,4,3,2,1,0:T(8,128)(2,1)} %param.4), kind=kLoop, calls=%fused_computation.4 | loop fusion | bytes 524288 | tf_op jit(solution)/shard_map/squeeze | solution.py:166
  13.5 1.9 %collective-permute-start = (bf16[2,2,16,2048]{3,2,1,0:T(8,128)(2,1)S(1)}, bf16[2,2,16,2048]{3,2,1,0:T(8,128)(2,1)S(1)}, u32[]{:S(2)}, u32[]{:S(2)}) collective-permute-start(bf16[2,2,16,2048]{3,2,1,0:T(8,128)(2,1)S(1)} %slice_bitcast_fusion), channel_id=1, source_target_pairs={{1,0},{2,1},{3,2},{4,3},{5,4},{6,5},{7,6},{9,8},{10,9},{11,10},{12... | collective-permute-start | bytes 786440 | tf_op jit(solution)/shard_map/ppermute | solution.py:33
  15.4 0.7 fusion.2
  16.1 0.7 reduce.1
  16.9 0.1 squeeze.19
  17.0 0.1 copy.32
  17.1 0.0 collective-permute-done.1
  17.1 4.4 %collective-permute-done.2 = f32[1,1,2,2,2048]{4,3,2,1,0:T(2,128)S(1)} collective-permute-done((f32[1,1,2,2,2048]{4,3,2,1,0:T(2,128)}, f32[1,1,2,2,2048]{4,3,2,1,0:T(2,128)S(1)}, u32[]{:S(2)}, u32[]{:S(2)}) %collective-permute-start.2) | collective-permute-done | bytes 32800 | tf_op jit(solution)/shard_map/ppermute | solution.py:23
  21.5 1.4 %maximum_bitcast_fusion.rate_ref = f32[3,2,2,2048]{3,2,1,0:T(2,128)} fusion(f32[1,1,2,2,2048]{4,3,2,1,0:T(2,128)S(1)} %collective-permute-done.2, f32[1,1,2,2,2048]{4,3,2,1,0:T(2,128)} %param.5, f32[1,1,2,2,2048]{4,3,2,1,0:T(2,128)S(1)} %collective-permute-done.1), kind=kLoop, calls=%fused_computation.5 | loop fusion | flops 49152 | bytes 196608 | tf_op jit(solution)/shard_map/squeeze | solution.py:168
  22.9 5.3 %collective-permute-done.edge_ref = bf16[2,2,16,2048]{3,2,1,0:T(8,128)(2,1)S(1)} collective-permute-done((bf16[2,2,16,2048]{3,2,1,0:T(8,128)(2,1)S(1)}, bf16[2,2,16,2048]{3,2,1,0:T(8,128)(2,1)S(1)}, u32[]{:S(2)}, u32[]{:S(2)}) %collective-permute-start) | collective-permute-done | bytes 262176 | tf_op jit(solution)/shard_map/ppermute | solution.py:33
  28.2 0.0 copy-start
  28.2 0.7 copy-done
  28.9 4.3 %shard_map.46 = f32[2,2,64,80]{3,2,1,0:T(8,128)} custom-call(bf16[2,3,64,2048]{3,2,1,0:T(8,128)(2,1)} %bitcast.27, bf16[2,2,16,2048]{3,2,1,0:T(8,128)(2,1)} %copy-done, f32[3,2,2,2048]{3,2,1,0:T(2,128)} %maximum_bitcast_fusion.rate_ref), custom_call_target="tpu_custom_call" | custom-call | tf_op jit(solution)/shard_map/pallas_call | solution.py:74
  33.3 0.9 convert_element_type.3
  34.2 0.2 reshape.59
  34.3 0.6 copy.33
  34.9 5.1 %gather_fusion = bf16[2560,4]{1,0:T(8,128)(2,1)S(1)} fusion(bf16[4,5120]{0,1:T(8,128)(2,1)S(1)} %copy.33, s32[3072]{0:T(1024)S(1)} %pad_clamp_fusion), kind=kCustom, calls=%fused_computation | custom fusion | bytes 51200 | tf_op jit(solution)/shard_map/jit(_take)/gather | solution.py:89
  40.0 0.5 copy.34
  40.5 0.1 copy.35
  40.6 26.9 %all_to_all.20 = bf16[64,1,160]{2,1,0:T(2,128)(2,1)S(1)} all-to-all(bf16[64,1,160]{2,1,0:T(2,128)(2,1)S(1)} %copy.35), channel_id=1, replica_groups=mesh['energy'=64,'domain'=8] {'energy'}, dimensions={0} | all-to-all | bytes 40960 | tf_op jit(solution)/shard_map/all_to_all | solution.py:171
  67.5 0.6 copy.44
  68.1 2.9 %shard_map.47 = bf16[64,80]{1,0:T(8,128)(2,1)} custom-call(bf16[64,160]{1,0:T(8,128)(2,1)} %bitcast.30), custom_call_target="tpu_custom_call" | custom-call | tf_op jit(solution)/shard_map/pallas_call | solution.py:111
  71.0 0.7 copy.36
  71.7 13.4 %all_to_all.21 = bf16[64,1,80]{2,1,0:T(2,128)(2,1)S(1)} all-to-all(bf16[64,1,80]{2,1,0:T(2,128)(2,1)S(1)} %copy.36), channel_id=1, replica_groups=mesh['energy'=64,'domain'=8] {'energy'}, dimensions={0} | all-to-all | bytes 20480 | tf_op jit(solution)/shard_map/all_to_all | solution.py:173
  85.1 0.1 copy.37
  85.2 0.1 copy.38
  85.3 0.1 reshape.72
  85.4 0.4 copy.39
  85.9 7.5 %scatter_custom_fusion = bf16[2,5120]{0,1:T(8,128)(2,1)S(1)} fusion(s32[2560]{0:T(1024)S(1)} %fusion.2, bf16[2560,2]{1,0:T(8,128)(2,1)S(1)} %copy.39, bf16[]{:T(256)} %constant.6.clone.1), kind=kCustom, calls=%fused_computation.2 | custom fusion | bytes 20482 | tf_op jit(solution)/shard_map/scatter | solution.py:159
  93.3 1.1 %copy.41.dense_ref = bf16[2,64,80]{2,1,0:T(8,128)(2,1)} copy(bf16[2,64,80]{0,2,1:T(8,128)(2,1)S(1)} %bitcast.26) | data formatting | bytes 40960 | tf_op jit(solution)/shard_map/reshape | solution.py:161
  94.5 1.8 %shard_map.48 = f32[2,64,64]{2,1,0:T(8,128)} custom-call(bf16[2,64,80]{2,1,0:T(8,128)(2,1)} %copy.41.dense_ref, bf16[2,64,80]{2,1,0:T(8,128)(2,1)} %bitcast.34), custom_call_target="tpu_custom_call" | custom-call | tf_op jit(solution)/shard_map/pallas_call | solution.py:149
  (3 shorter events, 0.0 us)
Async XLA Ops:
  0.0 17.1 %collective-permute-start.1 = (f32[1,1,2,2,2048]{4,3,2,1,0:T(2,128)}, f32[1,1,2,2,2048]{4,3,2,1,0:T(2,128)S(1)}, u32[]{:S(2)}, u32[]{:S(2)}) collective-permute-start(f32[1,1,2,2,2048]{4,3,2,1,0:T(2,128)} %param.5), channel_id=1, source_target_pairs={{0,1},{1,2},{2,3},{3,4},{4,5},{5,6},{6,7},{8,9},{9,10},{10,11},{11... | collective-permute-start | bytes 98312 | tf_op jit(solution)/shard_map/ppermute | solution.py:21
  10.5 10.9 %collective-permute-start.2 = (f32[1,1,2,2,2048]{4,3,2,1,0:T(2,128)}, f32[1,1,2,2,2048]{4,3,2,1,0:T(2,128)S(1)}, u32[]{:S(2)}, u32[]{:S(2)}) collective-permute-start(f32[1,1,2,2,2048]{4,3,2,1,0:T(2,128)} %param.5), channel_id=1, source_target_pairs={{1,0},{2,1},{3,2},{4,3},{5,4},{6,5},{7,6},{9,8},{10,9},{11,10},{12... | collective-permute-start | bytes 98312 | tf_op jit(solution)/shard_map/ppermute | solution.py:23
  13.5 14.8 %collective-permute-start = (bf16[2,2,16,2048]{3,2,1,0:T(8,128)(2,1)S(1)}, bf16[2,2,16,2048]{3,2,1,0:T(8,128)(2,1)S(1)}, u32[]{:S(2)}, u32[]{:S(2)}) collective-permute-start(bf16[2,2,16,2048]{3,2,1,0:T(8,128)(2,1)S(1)} %slice_bitcast_fusion), channel_id=1, source_target_pairs={{1,0},{2,1},{3,2},{4,3},{5,4},{6,5},{7,6},{9,8},{10,9},{11,10},{12... | collective-permute-start | bytes 786440 | tf_op jit(solution)/shard_map/ppermute | solution.py:33
  28.2 0.7 copy-start

commit v8 on v7

--- a/solution.py
+++ b/solution.py
@@ -8,23 +8,6 @@
 from jax.sharding import PartitionSpec as P
 
 EDGE = 16
-
-
-def padded_2(cells, sides, width):
-    for axis, dim in sides:
-        count = lax.axis_size(axis)
-        ends = count - 1
-        head = lax.slice_in_dim(cells, 0, width, axis=dim)
-        tail = lax.slice_in_dim(cells, cells.shape[dim] - width, cells.shape[dim], axis=dim)
-        cells = jnp.concatenate(
-            [
-                lax.ppermute(tail, axis, [(i, (i + 1) % count) for i in range(ends)]),
-                cells,
-                lax.ppermute(head, axis, [((i + 1) % count, i) for i in range(ends)]),
-            ],
-            axis=dim,
-        )
-    return cells
 
 
 def passed_along(x, axis, by):
@@ -161,10 +144,32 @@
     return screen_products(flat_dense.reshape(2, row_count, col_count), screen_block)
 
 
+def split_exact(value):
+    high = value.astype(jnp.bfloat16)
+    rest = value - high.astype(jnp.float32)
+    middle = rest.astype(jnp.bfloat16)
+    low = (rest - middle.astype(jnp.float32)).astype(jnp.bfloat16)
+    return jnp.stack([high, middle, low], axis=0)
+
+
+def join_exact(pieces):
+    pieces = pieces.astype(jnp.float32)
+    return (pieces[0] + pieces[1]) + pieces[2]
+
+
 def body(green_slab, self_energy, pattern, screened):
-    nearby = padded_2(self_energy, (("domain", 1),), 1)
+    own_rate = self_energy[0, 0]
+    block_order = own_rate.shape[-1]
+    previous_rate = passed_along(own_rate, "domain", 1)
     edge_block = green_slab[0, 0, :, 0:2, :EDGE, :]
-    following = passed_along(edge_block, "domain", -1)
+    bundle = jnp.concatenate(
+        [edge_block.reshape(-1, block_order), split_exact(own_rate).reshape(-1, block_order)], axis=0
+    )
+    bundle = passed_along(bundle, "domain", -1)
+    edge_rows = edge_block.size // block_order
+    following = bundle[:edge_rows].reshape(edge_block.shape)
+    next_rate = join_exact(bundle[edge_rows:].reshape(3, *own_rate.shape))
+    nearby = jnp.stack([previous_rate, own_rate, next_rate], axis=0)[None]
     values = element_values(green_slab[0, 0], following, nearby[0], pattern[0])
     chunks = lax.axis_size("energy")
     values = values.reshape(4, chunks, -1).transpose(1, 0, 2).reshape(chunks, -1)

time: 96.9 us -> 90.9 us (0.938)
  waiting for transfers between devices: 9.7 us -> 5.18 us
  starting transfers between devices: 14.4 us -> 12.5 us
    ppermute x2 -> x0, starting transfers between devices: 12.5 us -> none  [the longest x1 10.5 us: padded_2(): lax.ppermute(tail, axis, [(i, (i + 1) % count) for i in range(ends)])]
    ppermute x1 -> x2, starting transfers between devices: 1.92 us -> 12.5 us  [passed_along(): return lax.ppermute(x, axis, pairs)]
    ppermute x2 -> x0, waiting for transfers between devices: 4.38 us -> none  [the longest x1 4.38 us: padded_2(): lax.ppermute(head, axis, [((i + 1) % count, i) for i in range(ends)])]
    slice x0 -> x2, local copies, waits for them, and re-layouts: none -> 1.68 us  [the longest x1 0.97 us: body(): edge_block = green_slab[0, 0, :, 0:2, :EDGE, :]]
    convert_element_type x0 -> x3, other arithmetic: none -> 1.63 us  [the longest x1 0.85 us: split_exact(): middle = rest.astype(jnp.bfloat16)]
    squeeze x1 -> x0, other arithmetic: 1.43 us -> none  [body(): values = element_values(green_slab[0, 0], following, nearby[0], pattern[0])]
    squeeze x1 -> x0, local copies, waits for them, and re-layouts: 0.97 us -> none  [body(): edge_block = green_slab[0, 0, :, 0:2, :EDGE, :]]
    ppermute x1 -> x2, waiting for transfers between devices: 5.32 us -> 5.18 us  [passed_along(): return lax.ppermute(x, axis, pairs)]
  transfers between devices with their start and end apart: 3 -> 2, of which waited for: 2 -> 1; matrix products, arithmetic and copies ran while one was open for 4% -> 0% of each run, Pallas kernels for 0% -> 0%
where the time goes in v8:
time: 90.9 us; the launch traced here: 90.3 us
  blocking collectives  41 us (45%)
  local copies, waits for them, and re-layouts  19 us (21%)
  starting transfers between devices  12.5 us (14%)
  Pallas kernels  9 us (10%)
  waiting for transfers between devices  5.18 us (6%)
  other arithmetic  3.44 us (4%)
    all_to_all x1, blocking collectives, body(): lax.all_to_all(values, 'energy', split_axis=0, concat_axis=0, tiled=True)  27.6 us
    all_to_all x1, blocking collectives, body(): lax.all_to_all(polarization, 'energy', split_axis=0, concat_axis=0, tiled...  13.4 us
    ppermute x2, starting transfers between devices, passed_along(): return lax.ppermute(x, axis, pairs)  12.5 us
    scatter x1, local copies, waits for them, and re-layouts, screen(): jnp.zeros((2, row_count * col_count), jnp.bfloat16).at[:, pattern_row]  7.46 us
    gather x2, local copies, waits for them, and re-layouts, element_values(): jnp.take(joined.reshape(4, -1), pattern_row, axis=1).reshape(2, 2, -1)  5.53 us
    ppermute x2, waiting for transfers between devices, passed_along(): return lax.ppermute(x, axis, pairs)  5.18 us
    pallas_call x1, Pallas kernels, weighed_products(): pl.pallas_call(kernel, grid=(blocks,), in_specs=[pl.BlockSpec((2, 1, rows...  4.34 us
    pallas_call x1, Pallas kernels, lag_sums(): pl.pallas_call(kernel, out_shape=jax.ShapeDtypeStruct((energy_count, 2 *...  2.89 us
  transfers between devices with their start and end apart: 2, of which 1 were waited for; matrix products, arithmetic and copies ran while one was open for 0% of the time, Pallas kernels for 0%

profile of v8, /device:TPU:7, one launch (start us, length us, event | category | flops | bytes accessed | tf_op | source)
XLA Modules:
  0.0 90.3 jit_solution(5725503188075680289)
XLA Ops:
  0.0 0.0 copy-start
  0.0 0.0 copy-start.1
  0.0 0.9 fusion.2
  0.9 0.8 bitcast_convert_fusion
  1.6 0.1 pad_maximum_fusion.2
  1.8 1.0 %slice.21 = bf16[1,1,2,2,16,2048]{5,4,3,2,1,0:T(8,128)(2,1)S(1)} slice(bf16[1,1,2,3,64,2048]{5,4,3,2,1,0:T(8,128)(2,1)} %param.4), slice={[0:1], [0:1], [0:2], [0:2], [0:16], [0:2048]} | slice | bytes 524288 | tf_op jit(solution)/shard_map/slice | solution.py:164
  2.8 2.5 %collective-permute-start = (bf16[76,2048]{1,0:T(8,128)(2,1)S(1)}, bf16[76,2048]{1,0:T(8,128)(2,1)S(1)}, u32[]{:S(2)}, u32[]{:S(2)}) collective-permute-start(bf16[76,2048]{1,0:T(8,128)(2,1)S(1)} %pad_maximum_fusion), channel_id=1, source_target_pairs={{1,0},{2,1},{3,2},{4,3},{5,4},{6,5},{7,6},{9,8},{10,9},{11,10},{12... | collective-permute-start | bytes 933896 | tf_op jit(solution)/shard_map/ppermute | solution.py:16
  5.2 0.0 copy-done
  5.2 10.0 %collective-permute-start.1 = (f32[2,2,2048]{2,1,0:T(2,128)S(1)}, f32[2,2,2048]{2,1,0:T(2,128)S(1)}, u32[]{:S(2)}, u32[]{:S(2)}) collective-permute-start(f32[2,2,2048]{2,1,0:T(2,128)S(1)} %bitcast.35), channel_id=1, source_target_pairs={{0,1},{1,2},{2,3},{3,4},{4,5},{5,6},{6,7},{8,9},{9,10},{10,11},{11... | collective-permute-start | bytes 98312 | tf_op jit(solution)/shard_map/ppermute | solution.py:16
  15.3 0.0 copy-done.1
  15.3 0.1 squeeze.21
  15.4 0.1 copy.32
  15.6 5.2 %collective-permute-done = bf16[76,2048]{1,0:T(8,128)(2,1)S(1)} collective-permute-done((bf16[76,2048]{1,0:T(8,128)(2,1)S(1)}, bf16[76,2048]{1,0:T(8,128)(2,1)S(1)}, u32[]{:S(2)}, u32[]{:S(2)}) %collective-permute-start) | collective-permute-done | bytes 311328 | tf_op jit(solution)/shard_map/ppermute | solution.py:16
  20.8 0.0 collective-permute-done.1
  20.8 0.7 pad_maximum_fusion.1.rate_ref
  21.5 0.7 slice.29
  22.2 4.3 %shard_map.46 = f32[2,2,64,80]{3,2,1,0:T(8,128)} custom-call(bf16[2,3,64,2048]{3,2,1,0:T(8,128)(2,1)} %bitcast.31, bf16[2,2,16,2048]{3,2,1,0:T(8,128)(2,1)} %bitcast.33, f32[3,2,2,2048]{3,2,1,0:T(2,128)} %pad_maximum_fusion.1.rate_ref), custom_call_target="tpu_custom_call" | custom-call | tf_op jit(solution)/shard_map/pallas_call | solution.py:57
  26.5 0.9 %convert_element_type.79 = bf16[2,2,64,80]{3,2,1,0:T(8,128)(2,1)S(1)} convert(f32[2,2,64,80]{3,2,1,0:T(8,128)} %shard_map.46) | non-fusion elementwise | flops 20480 | bytes 122880 | tf_op jit(solution)/shard_map/convert_element_type | solution.py:71
  27.5 0.2 reshape.119
  27.6 0.6 copy.33
  28.2 5.1 %gather_fusion = bf16[2560,4]{1,0:T(8,128)(2,1)S(1)} fusion(bf16[4,5120]{0,1:T(8,128)(2,1)S(1)} %copy.33, s32[3072]{0:T(1024)S(1)} %pad_clamp_fusion), kind=kCustom, calls=%fused_computation | custom fusion | bytes 51200 | tf_op jit(solution)/shard_map/jit(_take)/gather | solution.py:72
  33.3 0.5 copy.34
  33.8 0.1 copy.35
  33.9 27.6 %all_to_all.20 = bf16[64,1,160]{2,1,0:T(2,128)(2,1)S(1)} all-to-all(bf16[64,1,160]{2,1,0:T(2,128)(2,1)S(1)} %copy.35), channel_id=1, replica_groups=mesh['energy'=64,'domain'=8] {'energy'}, dimensions={0} | all-to-all | bytes 40960 | tf_op jit(solution)/shard_map/all_to_all | solution.py:176
  61.6 0.6 copy.44
  62.2 2.9 %shard_map.47 = bf16[64,80]{1,0:T(8,128)(2,1)} custom-call(bf16[64,160]{1,0:T(8,128)(2,1)} %bitcast.38), custom_call_target="tpu_custom_call" | custom-call | tf_op jit(solution)/shard_map/pallas_call | solution.py:94
  65.1 0.7 copy.36
  65.8 13.4 %all_to_all.21 = bf16[64,1,80]{2,1,0:T(2,128)(2,1)S(1)} all-to-all(bf16[64,1,80]{2,1,0:T(2,128)(2,1)S(1)} %copy.36), channel_id=1, replica_groups=mesh['energy'=64,'domain'=8] {'energy'}, dimensions={0} | all-to-all | bytes 20480 | tf_op jit(solution)/shard_map/all_to_all | solution.py:178
  79.2 0.1 copy.37
  79.3 0.1 copy.38
  79.4 0.1 reshape.132
  79.5 0.4 copy.39
  79.9 7.5 %scatter_custom_fusion = bf16[2,5120]{0,1:T(8,128)(2,1)S(1)} fusion(s32[2560]{0:T(1024)S(1)} %fusion.3, bf16[2560,2]{1,0:T(8,128)(2,1)S(1)} %copy.39, bf16[]{:T(256)} %constant.6.clone.1), kind=kCustom, calls=%fused_computation.2 | custom fusion | bytes 20482 | tf_op jit(solution)/shard_map/scatter | solution.py:142
  87.4 1.1 %copy.41.dense_ref = bf16[2,64,80]{2,1,0:T(8,128)(2,1)} copy(bf16[2,64,80]{0,2,1:T(8,128)(2,1)S(1)} %bitcast.30) | data formatting | bytes 40960 | tf_op jit(solution)/shard_map/reshape | solution.py:144
  88.5 1.8 %shard_map.48 = f32[2,64,64]{2,1,0:T(8,128)} custom-call(bf16[2,64,80]{2,1,0:T(8,128)(2,1)} %copy.41.dense_ref, bf16[2,64,80]{2,1,0:T(8,128)(2,1)} %bitcast.42), custom_call_target="tpu_custom_call" | custom-call | tf_op jit(solution)/shard_map/pallas_call | solution.py:132
  (10 shorter events, 0.2 us)
Async XLA Ops:
  0.0 5.2 %copy-start = (f32[1,1,2,2,2048]{4,3,2,1,0:T(2,128)S(1)}, f32[1,1,2,2,2048]{4,3,2,1,0:T(2,128)}, u32[]{:S(2)}) copy-start(f32[1,1,2,2,2048]{4,3,2,1,0:T(2,128)} %param.5) | copy-start | bytes 98308
  0.0 15.3 %copy-start.1 = (s32[1,2560]{1,0:T(1,128)S(1)}, s32[1,2560]{1,0:T(1,128)}, u32[]{:S(2)}) copy-start(s32[1,2560]{1,0:T(1,128)} %param.6) | copy-start | bytes 30724
  2.8 18.0 %collective-permute-start = (bf16[76,2048]{1,0:T(8,128)(2,1)S(1)}, bf16[76,2048]{1,0:T(8,128)(2,1)S(1)}, u32[]{:S(2)}, u32[]{:S(2)}) collective-permute-start(bf16[76,2048]{1,0:T(8,128)(2,1)S(1)} %pad_maximum_fusion), channel_id=1, source_target_pairs={{1,0},{2,1},{3,2},{4,3},{5,4},{6,5},{7,6},{9,8},{10,9},{11,10},{12... | collective-permute-start | bytes 933896 | tf_op jit(solution)/shard_map/ppermute | solution.py:16
  5.2 15.6 %collective-permute-start.1 = (f32[2,2,2048]{2,1,0:T(2,128)S(1)}, f32[2,2,2048]{2,1,0:T(2,128)S(1)}, u32[]{:S(2)}, u32[]{:S(2)}) collective-permute-start(f32[2,2,2048]{2,1,0:T(2,128)S(1)} %bitcast.35), channel_id=1, source_target_pairs={{0,1},{1,2},{2,3},{3,4},{4,5},{5,6},{6,7},{8,9},{9,10},{10,11},{11... | collective-permute-start | bytes 98312 | tf_op jit(solution)/shard_map/ppermute | solution.py:16

commit v9 on v8

--- a/solution.py
+++ b/solution.py
@@ -145,11 +145,11 @@
 
 
 def split_exact(value):
-    high = value.astype(jnp.bfloat16)
-    rest = value - high.astype(jnp.float32)
-    middle = rest.astype(jnp.bfloat16)
-    low = (rest - middle.astype(jnp.float32)).astype(jnp.bfloat16)
-    return jnp.stack([high, middle, low], axis=0)
+    high = lax.reduce_precision(value, exponent_bits=8, mantissa_bits=7)
+    rest = value - high
+    middle = lax.reduce_precision(rest, exponent_bits=8, mantissa_bits=7)
+    low = rest - middle
+    return jnp.stack([high, middle, low], axis=0).astype(jnp.bfloat16)
 
 
 def join_exact(pieces):

time: 90.9 us -> 90.1 us (level)
    convert_element_type x2 -> x0, other arithmetic: 1.62 us -> none  [the longest x1 0.85 us: split_exact(): middle = rest.astype(jnp.bfloat16)]
where the time goes in v9:
time: 90.1 us; the launch traced here: 89.5 us
  blocking collectives  41 us (46%)
  local copies, waits for them, and re-layouts  19 us (21%)
  starting transfers between devices  12.5 us (14%)
  Pallas kernels  9 us (10%)
  waiting for transfers between devices  5.18 us (6%)
  other arithmetic  2.68 us (3%)
    all_to_all x1, blocking collectives, body(): lax.all_to_all(values, 'energy', split_axis=0, concat_axis=0, tiled=True)  27.6 us
    all_to_all x1, blocking collectives, body(): lax.all_to_all(polarization, 'energy', split_axis=0, concat_axis=0, tiled...  13.4 us
    ppermute x2, starting transfers between devices, passed_along(): return lax.ppermute(x, axis, pairs)  12.5 us
    scatter x1, local copies, waits for them, and re-layouts, screen(): jnp.zeros((2, row_count * col_count), jnp.bfloat16).at[:, pattern_row]  7.46 us
    gather x2, local copies, waits for them, and re-layouts, element_values(): jnp.take(joined.reshape(4, -1), pattern_row, axis=1).reshape(2, 2, -1)  5.53 us
    ppermute x2, waiting for transfers between devices, passed_along(): return lax.ppermute(x, axis, pairs)  5.18 us
    pallas_call x1, Pallas kernels, weighed_products(): pl.pallas_call(kernel, grid=(blocks,), in_specs=[pl.BlockSpec((2, 1, rows...  4.34 us
    pallas_call x1, Pallas kernels, lag_sums(): pl.pallas_call(kernel, out_shape=jax.ShapeDtypeStruct((energy_count, 2 *...  2.89 us
  transfers between devices with their start and end apart: 2, of which 1 were waited for; matrix products, arithmetic and copies ran while one was open for 0% of the time, Pallas kernels for 0%

profile of v9, /device:TPU:7, one launch (start us, length us, event | category | flops | bytes accessed | tf_op | source)
XLA Modules:
  0.0 89.5 jit_solution(11836897987677627892)
XLA Ops:
  0.0 0.0 copy-start
  0.0 0.0 copy-start.1
  0.0 0.9 reduce-precision_convert_fusion.1
  0.9 0.1 pad_maximum_fusion.2
  1.0 1.0 %slice.21 = bf16[1,1,2,2,16,2048]{5,4,3,2,1,0:T(8,128)(2,1)S(1)} slice(bf16[1,1,2,3,64,2048]{5,4,3,2,1,0:T(8,128)(2,1)} %param.4), slice={[0:1], [0:1], [0:2], [0:2], [0:16], [0:2048]} | slice | bytes 524288 | tf_op jit(solution)/shard_map/slice | solution.py:164
  2.0 2.5 %collective-permute-start = (bf16[76,2048]{1,0:T(8,128)(2,1)S(1)}, bf16[76,2048]{1,0:T(8,128)(2,1)S(1)}, u32[]{:S(2)}, u32[]{:S(2)}) collective-permute-start(bf16[76,2048]{1,0:T(8,128)(2,1)S(1)} %pad_maximum_fusion), channel_id=1, source_target_pairs={{1,0},{2,1},{3,2},{4,3},{5,4},{6,5},{7,6},{9,8},{10,9},{11,10},{12... | collective-permute-start | bytes 933896 | tf_op jit(solution)/shard_map/ppermute | solution.py:16
  4.5 0.0 copy-done
  4.5 10.0 %collective-permute-start.1 = (f32[2,2,2048]{2,1,0:T(2,128)S(1)}, f32[2,2,2048]{2,1,0:T(2,128)S(1)}, u32[]{:S(2)}, u32[]{:S(2)}) collective-permute-start(f32[2,2,2048]{2,1,0:T(2,128)S(1)} %bitcast.37), channel_id=1, source_target_pairs={{0,1},{1,2},{2,3},{3,4},{4,5},{5,6},{6,7},{8,9},{9,10},{10,11},{11... | collective-permute-start | bytes 98312 | tf_op jit(solution)/shard_map/ppermute | solution.py:16
  14.5 0.0 copy-done.1
  14.5 0.1 squeeze.21
  14.7 0.1 copy.32
  14.8 5.2 %collective-permute-done = bf16[76,2048]{1,0:T(8,128)(2,1)S(1)} collective-permute-done((bf16[76,2048]{1,0:T(8,128)(2,1)S(1)}, bf16[76,2048]{1,0:T(8,128)(2,1)S(1)}, u32[]{:S(2)}, u32[]{:S(2)}) %collective-permute-start) | collective-permute-done | bytes 311328 | tf_op jit(solution)/shard_map/ppermute | solution.py:16
  20.0 0.0 collective-permute-done.1
  20.1 0.7 pad_maximum_fusion.1.rate_ref
  20.7 0.7 slice.29
  21.4 4.3 %shard_map.46 = f32[2,2,64,80]{3,2,1,0:T(8,128)} custom-call(bf16[2,3,64,2048]{3,2,1,0:T(8,128)(2,1)} %bitcast.31, bf16[2,2,16,2048]{3,2,1,0:T(8,128)(2,1)} %bitcast.33, f32[3,2,2,2048]{3,2,1,0:T(2,128)} %pad_maximum_fusion.1.rate_ref), custom_call_target="tpu_custom_call" | custom-call | tf_op jit(solution)/shard_map/pallas_call | solution.py:57
  25.8 0.9 %convert_element_type.14 = bf16[2,2,64,80]{3,2,1,0:T(8,128)(2,1)S(1)} convert(f32[2,2,64,80]{3,2,1,0:T(8,128)} %shard_map.46) | non-fusion elementwise | flops 20480 | bytes 122880 | tf_op jit(solution)/shard_map/convert_element_type | solution.py:71
  26.7 0.2 reshape.109
  26.9 0.6 copy.33
  27.5 5.1 %gather_fusion = bf16[2560,4]{1,0:T(8,128)(2,1)S(1)} fusion(bf16[4,5120]{0,1:T(8,128)(2,1)S(1)} %copy.33, s32[3072]{0:T(1024)S(1)} %pad_clamp_fusion), kind=kCustom, calls=%fused_computation | custom fusion | bytes 51200 | tf_op jit(solution)/shard_map/jit(_take)/gather | solution.py:72
  32.5 0.5 copy.34
  33.0 0.1 copy.35
  33.1 27.6 %all_to_all.20 = bf16[64,1,160]{2,1,0:T(2,128)(2,1)S(1)} all-to-all(bf16[64,1,160]{2,1,0:T(2,128)(2,1)S(1)} %copy.35), channel_id=1, replica_groups=mesh['energy'=64,'domain'=8] {'energy'}, dimensions={0} | all-to-all | bytes 40960 | tf_op jit(solution)/shard_map/all_to_all | solution.py:176
  60.8 0.6 copy.44
  61.4 2.9 %shard_map.47 = bf16[64,80]{1,0:T(8,128)(2,1)} custom-call(bf16[64,160]{1,0:T(8,128)(2,1)} %bitcast.36), custom_call_target="tpu_custom_call" | custom-call | tf_op jit(solution)/shard_map/pallas_call | solution.py:94
  64.3 0.7 copy.36
  65.0 13.4 %all_to_all.21 = bf16[64,1,80]{2,1,0:T(2,128)(2,1)S(1)} all-to-all(bf16[64,1,80]{2,1,0:T(2,128)(2,1)S(1)} %copy.36), channel_id=1, replica_groups=mesh['energy'=64,'domain'=8] {'energy'}, dimensions={0} | all-to-all | bytes 20480 | tf_op jit(solution)/shard_map/all_to_all | solution.py:178
  78.4 0.1 copy.37
  78.5 0.1 copy.38
  78.6 0.1 reshape.122
  78.7 0.4 copy.39
  79.2 7.5 %scatter_custom_fusion = bf16[2,5120]{0,1:T(8,128)(2,1)S(1)} fusion(s32[2560]{0:T(1024)S(1)} %fusion.3, bf16[2560,2]{1,0:T(8,128)(2,1)S(1)} %copy.39, bf16[]{:T(256)} %constant.6.clone.1), kind=kCustom, calls=%fused_computation.2 | custom fusion | bytes 20482 | tf_op jit(solution)/shard_map/scatter | solution.py:142
  86.6 1.1 %copy.41.dense_ref = bf16[2,64,80]{2,1,0:T(8,128)(2,1)} copy(bf16[2,64,80]{0,2,1:T(8,128)(2,1)S(1)} %bitcast.30) | data formatting | bytes 40960 | tf_op jit(solution)/shard_map/reshape | solution.py:144
  87.8 1.8 %shard_map.48 = f32[2,64,64]{2,1,0:T(8,128)} custom-call(bf16[2,64,80]{2,1,0:T(8,128)(2,1)} %copy.41.dense_ref, bf16[2,64,80]{2,1,0:T(8,128)(2,1)} %bitcast.42), custom_call_target="tpu_custom_call" | custom-call | tf_op jit(solution)/shard_map/pallas_call | solution.py:132
  (10 shorter events, 0.2 us)
Async XLA Ops:
  0.0 4.5 %copy-start = (f32[1,1,2,2,2048]{4,3,2,1,0:T(2,128)S(1)}, f32[1,1,2,2,2048]{4,3,2,1,0:T(2,128)}, u32[]{:S(2)}) copy-start(f32[1,1,2,2,2048]{4,3,2,1,0:T(2,128)} %param.5) | copy-start | bytes 98308
  0.0 14.5 %copy-start.1 = (s32[1,2560]{1,0:T(1,128)S(1)}, s32[1,2560]{1,0:T(1,128)}, u32[]{:S(2)}) copy-start(s32[1,2560]{1,0:T(1,128)} %param.6) | copy-start | bytes 30724
  2.0 18.0 %collective-permute-start = (bf16[76,2048]{1,0:T(8,128)(2,1)S(1)}, bf16[76,2048]{1,0:T(8,128)(2,1)S(1)}, u32[]{:S(2)}, u32[]{:S(2)}) collective-permute-start(bf16[76,2048]{1,0:T(8,128)(2,1)S(1)} %pad_maximum_fusion), channel_id=1, source_target_pairs={{1,0},{2,1},{3,2},{4,3},{5,4},{6,5},{7,6},{9,8},{10,9},{11,10},{12... | collective-permute-start | bytes 933896 | tf_op jit(solution)/shard_map/ppermute | solution.py:16
  4.5 15.6 %collective-permute-start.1 = (f32[2,2,2048]{2,1,0:T(2,128)S(1)}, f32[2,2,2048]{2,1,0:T(2,128)S(1)}, u32[]{:S(2)}, u32[]{:S(2)}) collective-permute-start(f32[2,2,2048]{2,1,0:T(2,128)S(1)} %bitcast.37), channel_id=1, source_target_pairs={{0,1},{1,2},{2,3},{3,4},{4,5},{5,6},{6,7},{8,9},{9,10},{10,11},{11... | collective-permute-start | bytes 98312 | tf_op jit(solution)/shard_map/ppermute | solution.py:16

commit v10 on v9

--- a/solution.py
+++ b/solution.py
@@ -97,15 +97,22 @@
     )(by_element)
 
 
-def _screen_kernel(dense_ref, screen_ref, out_ref, *, rows):
+def _screen_kernel(polar_ref, place_ref, screen_ref, out_ref, *, rows, cols):
     def nt(a, b):
         return lax.dot_general(a, b, (((1,), (1,)), ((), ())), preferred_element_type=jnp.float32)
 
     def nn(a, b):
         return jnp.dot(a, b, preferred_element_type=jnp.float32)
 
-    dense_real = dense_ref[0]
-    dense_imag = dense_ref[1]
+    count = place_ref.shape[1]
+    row_hit = lax.broadcasted_iota(jnp.int32, (rows, count), 0) == place_ref[0:1, :]
+    col_hit = (lax.broadcasted_iota(jnp.int32, (cols, count), 0) == place_ref[1:2, :]).astype(jnp.bfloat16)
+    polar = polar_ref[...].astype(jnp.float32)
+    dense = []
+    for part in range(2):
+        spread = jnp.where(row_hit, polar[part:part + 1, :], 0.0).astype(jnp.bfloat16)
+        dense.append(nt(spread, col_hit).astype(jnp.bfloat16))
+    dense_real, dense_imag = dense
     screen_real = screen_ref[0]
     screen_imag = screen_ref[1]
     inner_real = (nt(dense_real, screen_real) + nt(dense_imag, screen_imag)).astype(jnp.bfloat16)
@@ -126,22 +133,15 @@
     out_ref[1] = first_imag + second_imag
 
 
-def screen_products(dense_pol, screen_block):
+def screen(polar_row, pattern_row, screen_block):
     rows = screen_block.shape[1]
-    kernel = functools.partial(_screen_kernel, rows=rows)
+    cols = screen_block.shape[2]
+    place = jnp.stack([pattern_row // cols, pattern_row % cols], axis=0)
+    kernel = functools.partial(_screen_kernel, rows=rows, cols=cols)
     return pl.pallas_call(
         kernel,
         out_shape=jax.ShapeDtypeStruct((2, rows, rows), jnp.float32),
-    )(dense_pol, screen_block)
-
-
-def screen(polar_row, pattern_row, screen_block):
-    row_count = screen_block.shape[1]
-    col_count = screen_block.shape[2]
-    flat_dense = (
-        jnp.zeros((2, row_count * col_count), jnp.bfloat16).at[:, pattern_row].set(polar_row)
-    )
-    return screen_products(flat_dense.reshape(2, row_count, col_count), screen_block)
+    )(polar_row, place, screen_block)
 
 
 def split_exact(value):

time: 90.1 us -> 83.4 us (0.926)
  blocking collectives: 41 us -> 27.6 us
  waiting for transfers between devices: 5.18 us -> 14.1 us
  local copies, waits for them, and re-layouts: 19 us -> 11.2 us
  starting transfers between devices: 12.5 us -> 16.9 us
    all_to_all x1 -> x0, blocking collectives: 13.4 us -> none  [body(): lax.all_to_all(polarization, 'energy', split_axis=0, concat_axis=0, tiled...]
    all_to_all x0 -> x1, waiting for transfers between devices: none -> 9.03 us  [body(): lax.all_to_all(polarization, 'energy', split_axis=0, concat_axis=0, tiled...]
    scatter x1 -> x0, local copies, waits for them, and re-layouts: 7.46 us -> none  [screen(): jnp.zeros((2, row_count * col_count), jnp.bfloat16).at[:, pattern_row]]
    all_to_all x0 -> x1, starting transfers between devices: none -> 4.42 us  [body(): lax.all_to_all(polarization, 'energy', split_axis=0, concat_axis=0, tiled...]
    reshape x1 -> x0, local copies, waits for them, and re-layouts: 1.12 us -> none  [screen(): flat_dense.reshape(2, row_count, col_count)]
  transfers between devices with their start and end apart: 2 -> 3, of which waited for: 1 -> 2; matrix products, arithmetic and copies ran while one was open for 0% -> 1% of each run, Pallas kernels for 0% -> 0%
where the time goes in v10:
time: 83.4 us; the launch traced here: 82.8 us
  blocking collectives  27.6 us (33%)
  starting transfers between devices  16.9 us (20%)
  waiting for transfers between devices  14.1 us (17%)
  local copies, waits for them, and re-layouts  11.2 us (13%)
  Pallas kernels  9.39 us (11%)
  other arithmetic  3.39 us (4%)
    all_to_all x1, blocking collectives, body(): lax.all_to_all(values, 'energy', split_axis=0, concat_axis=0, tiled=True)  27.6 us
    ppermute x2, starting transfers between devices, passed_along(): return lax.ppermute(x, axis, pairs)  12.5 us
    all_to_all x1, waiting for transfers between devices, body(): lax.all_to_all(polarization, 'energy', split_axis=0, concat_axis=0, tiled...  9.03 us
    gather x2, local copies, waits for them, and re-layouts, element_values(): jnp.take(joined.reshape(4, -1), pattern_row, axis=1).reshape(2, 2, -1)  5.53 us
    ppermute x2, waiting for transfers between devices, passed_along(): return lax.ppermute(x, axis, pairs)  5.1 us
    all_to_all x1, starting transfers between devices, body(): lax.all_to_all(polarization, 'energy', split_axis=0, concat_axis=0, tiled...  4.42 us
    pallas_call x1, Pallas kernels, weighed_products(): pl.pallas_call(kernel, grid=(blocks,), in_specs=[pl.BlockSpec((2, 1, rows...  4.35 us
    pallas_call x1, Pallas kernels, lag_sums(): pl.pallas_call(kernel, out_shape=jax.ShapeDtypeStruct((energy_count, 2 *...  2.89 us
  transfers between devices with their start and end apart: 3, of which 2 were waited for; matrix products, arithmetic and copies ran while one was open for 1% of the time, Pallas kernels for 0%

profile of v10, /device:TPU:7, one launch (start us, length us, event | category | flops | bytes accessed | tf_op | source)
XLA Modules:
  0.0 82.8 jit_solution(7382095709211944561)
XLA Ops:
  0.0 0.0 copy-start
  0.0 0.0 copy-start.1
  0.0 0.9 %reduce-precision_convert_fusion.1 = (bf16[1,2,2,2048]{3,2,1,0:T(2,128)(2,1)S(1)}, bf16[1,2,2,2048]{3,2,1,0:T(2,128)(2,1)S(1)}, bf16[1,2,2,2048]{3,2,1,0:T(2,128)(2,1)S(1)}) fusion(f32[1,1,2,2,2048]{4,3,2,1,0:T(2,128)} %param.5), kind=kLoop, calls=%fused_computation.10 | loop fusion | flops 57344 | bytes 81920 | tf_op jit(solution)/shard_map/convert
  0.9 0.1 pad_maximum_fusion.2
  1.0 1.0 %slice.21 = bf16[1,1,2,2,16,2048]{5,4,3,2,1,0:T(8,128)(2,1)S(1)} slice(bf16[1,1,2,3,64,2048]{5,4,3,2,1,0:T(8,128)(2,1)} %param.4), slice={[0:1], [0:1], [0:2], [0:2], [0:16], [0:2048]} | slice | bytes 524288 | tf_op jit(solution)/shard_map/slice | solution.py:164
  2.0 2.5 %collective-permute-start = (bf16[76,2048]{1,0:T(8,128)(2,1)S(1)}, bf16[76,2048]{1,0:T(8,128)(2,1)S(1)}, u32[]{:S(2)}, u32[]{:S(2)}) collective-permute-start(bf16[76,2048]{1,0:T(8,128)(2,1)S(1)} %pad_maximum_fusion), channel_id=1, source_target_pairs={{1,0},{2,1},{3,2},{4,3},{5,4},{6,5},{7,6},{9,8},{10,9},{11,10},{12... | collective-permute-start | bytes 933896 | tf_op jit(solution)/shard_map/ppermute | solution.py:16
  4.5 0.0 copy-done
  4.5 10.0 %collective-permute-start.1 = (f32[2,2,2048]{2,1,0:T(2,128)S(1)}, f32[2,2,2048]{2,1,0:T(2,128)S(1)}, u32[]{:S(2)}, u32[]{:S(2)}) collective-permute-start(f32[2,2,2048]{2,1,0:T(2,128)S(1)} %bitcast.34), channel_id=1, source_target_pairs={{0,1},{1,2},{2,3},{3,4},{4,5},{5,6},{6,7},{8,9},{9,10},{10,11},{11... | collective-permute-start | bytes 98312 | tf_op jit(solution)/shard_map/ppermute | solution.py:16
  14.5 0.0 copy-done.1
  14.5 0.1 and_select_fusion.1
  14.6 0.1 squeeze.20
  14.7 0.1 copy.21
  14.9 5.1 %collective-permute-done = bf16[76,2048]{1,0:T(8,128)(2,1)S(1)} collective-permute-done((bf16[76,2048]{1,0:T(8,128)(2,1)S(1)}, bf16[76,2048]{1,0:T(8,128)(2,1)S(1)}, u32[]{:S(2)}, u32[]{:S(2)}) %collective-permute-start) | collective-permute-done | bytes 311328 | tf_op jit(solution)/shard_map/ppermute | solution.py:16
  20.0 0.0 collective-permute-done.1
  20.1 0.7 pad_maximum_fusion.1.rate_ref
  20.7 0.7 slice.29
  21.4 4.3 %shard_map.46 = f32[2,2,64,80]{3,2,1,0:T(8,128)} custom-call(bf16[2,3,64,2048]{3,2,1,0:T(8,128)(2,1)} %bitcast.28, bf16[2,2,16,2048]{3,2,1,0:T(8,128)(2,1)} %bitcast.30, f32[3,2,2,2048]{3,2,1,0:T(2,128)} %pad_maximum_fusion.1.rate_ref), custom_call_target="tpu_custom_call" | custom-call | tf_op jit(solution)/shard_map/pallas_call | solution.py:57
  25.8 0.9 %convert_element_type.14 = bf16[2,2,64,80]{3,2,1,0:T(8,128)(2,1)S(1)} convert(f32[2,2,64,80]{3,2,1,0:T(8,128)} %shard_map.46) | non-fusion elementwise | flops 20480 | bytes 122880 | tf_op jit(solution)/shard_map/convert_element_type | solution.py:71
  26.7 0.2 reshape.106
  26.9 0.6 copy.22
  27.5 5.1 %gather_fusion = bf16[2560,4]{1,0:T(8,128)(2,1)S(1)} fusion(bf16[4,5120]{0,1:T(8,128)(2,1)S(1)} %copy.22, s32[3072]{0:T(1024)S(1)} %pad_clamp_fusion), kind=kCustom, calls=%fused_computation | custom fusion | bytes 51200 | tf_op jit(solution)/shard_map/jit(_take)/gather | solution.py:72
  32.5 0.5 copy.23
  33.0 0.1 copy.24
  33.1 27.6 %all_to_all.20 = bf16[64,1,160]{2,1,0:T(2,128)(2,1)S(1)} all-to-all(bf16[64,1,160]{2,1,0:T(2,128)(2,1)S(1)} %copy.24), channel_id=1, replica_groups=mesh['energy'=64,'domain'=8] {'energy'}, dimensions={0} | all-to-all | bytes 40960 | tf_op jit(solution)/shard_map/all_to_all | solution.py:176
  60.8 0.6 copy.30
  61.4 2.9 %shard_map.47 = bf16[64,80]{1,0:T(8,128)(2,1)} custom-call(bf16[64,160]{1,0:T(8,128)(2,1)} %bitcast.33), custom_call_target="tpu_custom_call" | custom-call | tf_op jit(solution)/shard_map/pallas_call | solution.py:94
  64.3 1.4 %copy.25 = bf16[64,1,80]{2,1,0:T(2,128)(2,1)} copy(bf16[64,1,80]{2,0,1:T(8,128)(2,1)} %bitcast.37) | data formatting | bytes 20480 | tf_op jit(solution)/shard_map/all_to_all | solution.py:178
  65.7 4.4 %all-to-all-start.1 = ((bf16[64,1,80]{2,1,0:T(2,128)(2,1)}), bf16[64,1,80]{2,1,0:T(2,128)(2,1)S(1)}, u32[]{:S(2)}, u32[]{:S(2)}) async-start(bf16[64,1,80]{2,1,0:T(2,128)(2,1)} %copy.25), calls=%async_computation.1 | async-start | bytes 65536 | tf_op jit(solution)/shard_map/all_to_all | solution.py:178
  70.1 0.6 pad_add_fusion.place_ref
  70.7 9.0 %all-to-all-done.1 = bf16[64,1,80]{2,1,0:T(2,128)(2,1)S(1)} async-done(((bf16[64,1,80]{2,1,0:T(2,128)(2,1)}), bf16[64,1,80]{2,1,0:T(2,128)(2,1)S(1)}, u32[]{:S(2)}, u32[]{:S(2)}) %all-to-all-start.1) | async-done | bytes 10272 | tf_op jit(solution)/shard_map/all_to_all | solution.py:178
  79.8 0.1 copy.26
  79.9 0.1 copy.27
  80.0 0.7 reshape.108.polar_ref
  80.7 2.1 %shard_map.48 = f32[2,64,64]{2,1,0:T(8,128)} custom-call(bf16[2,2560]{1,0:T(2,128)(2,1)} %reshape.108.polar_ref, s32[2,2560]{1,0:T(2,128)} %pad_add_fusion.place_ref, bf16[2,64,80]{2,1,0:T(8,128)(2,1)} %bitcast.38), custom_call_target="tpu_custom_call" | custom-call | tf_op jit(solution)/shard_map/pallas_call | solution.py:141
  (9 shorter events, 0.2 us)
Async XLA Ops:
  0.0 4.5 %copy-start = (f32[1,1,2,2,2048]{4,3,2,1,0:T(2,128)S(1)}, f32[1,1,2,2,2048]{4,3,2,1,0:T(2,128)}, u32[]{:S(2)}) copy-start(f32[1,1,2,2,2048]{4,3,2,1,0:T(2,128)} %param.5) | copy-start | bytes 98308
  0.0 14.5 %copy-start.1 = (s32[1,2560]{1,0:T(1,128)S(1)}, s32[1,2560]{1,0:T(1,128)}, u32[]{:S(2)}) copy-start(s32[1,2560]{1,0:T(1,128)} %param.6) | copy-start | bytes 30724
  2.0 18.0 %collective-permute-start = (bf16[76,2048]{1,0:T(8,128)(2,1)S(1)}, bf16[76,2048]{1,0:T(8,128)(2,1)S(1)}, u32[]{:S(2)}, u32[]{:S(2)}) collective-permute-start(bf16[76,2048]{1,0:T(8,128)(2,1)S(1)} %pad_maximum_fusion), channel_id=1, source_target_pairs={{1,0},{2,1},{3,2},{4,3},{5,4},{6,5},{7,6},{9,8},{10,9},{11,10},{12... | collective-permute-start | bytes 933896 | tf_op jit(solution)/shard_map/ppermute | solution.py:16
  4.5 15.6 %collective-permute-start.1 = (f32[2,2,2048]{2,1,0:T(2,128)S(1)}, f32[2,2,2048]{2,1,0:T(2,128)S(1)}, u32[]{:S(2)}, u32[]{:S(2)}) collective-permute-start(f32[2,2,2048]{2,1,0:T(2,128)S(1)} %bitcast.34), channel_id=1, source_target_pairs={{0,1},{1,2},{2,3},{3,4},{4,5},{5,6},{6,7},{8,9},{9,10},{10,11},{11... | collective-permute-start | bytes 98312 | tf_op jit(solution)/shard_map/ppermute | solution.py:16
  65.7 14.1 %all-to-all-start.1 = ((bf16[64,1,80]{2,1,0:T(2,128)(2,1)}), bf16[64,1,80]{2,1,0:T(2,128)(2,1)S(1)}, u32[]{:S(2)}, u32[]{:S(2)}) async-start(bf16[64,1,80]{2,1,0:T(2,128)(2,1)} %copy.25), calls=%async_computation.1 | async-start | bytes 65536 | tf_op jit(solution)/shard_map/all_to_all | solution.py:178

commit v11 on v10

--- a/solution.py
+++ b/solution.py
@@ -5,6 +5,7 @@
 import jax.numpy as jnp
 from jax import lax
 from jax.experimental import pallas as pl
+from jax.experimental.pallas import tpu as pltpu
 from jax.sharding import PartitionSpec as P
 
 EDGE = 16
@@ -16,12 +17,12 @@
     return lax.ppermute(x, axis, pairs)
 
 
-def _weigh_kernel(slab_ref, edge_ref, rate_ref, out_ref, *, factor, rows, edge):
+def _weigh_kernel(slab_ref, edge_ref, rate_ref, place_ref, out_ref, acc_ref, *, factor, rows, edge):
     step = pl.program_id(0)
 
     @pl.when(step == 0)
     def _():
-        out_ref[...] = jnp.zeros_like(out_ref)
+        acc_ref[...] = jnp.zeros_like(acc_ref)
 
     slab_real = slab_ref[0, 0]
     slab_imag = slab_ref[1, 0]
@@ -39,19 +40,36 @@
     for q in range(2):
         wr = prod[2 * q * rows:(2 * q + 1) * rows]
         wi = prod[(2 * q + 1) * rows:(2 * q + 2) * rows]
-        out_ref[q, 0, :, 0:rows] += wr[:, 0:rows] + wi[:, rows:2 * rows]
-        out_ref[q, 1, :, 0:rows] += wi[:, 0:rows] - wr[:, rows:2 * rows]
+        acc_ref[q, 0, :, 0:rows] += wr[:, 0:rows] + wi[:, rows:2 * rows]
+        acc_ref[q, 1, :, 0:rows] += wi[:, 0:rows] - wr[:, rows:2 * rows]
 
         @pl.when(step > 0)
         def _():
             e0 = 2 * rows
-            out_ref[q, 0, :, rows:rows + edge] += wr[:, e0:e0 + edge] + wi[:, e0 + edge:e0 + 2 * edge]
-            out_ref[q, 1, :, rows:rows + edge] += wi[:, e0:e0 + edge] - wr[:, e0 + edge:e0 + 2 * edge]
-
-
-def weighed_products(own_slab, next_edge, diag_rates):
+            acc_ref[q, 0, :, rows:rows + edge] += wr[:, e0:e0 + edge] + wi[:, e0 + edge:e0 + 2 * edge]
+            acc_ref[q, 1, :, rows:rows + edge] += wi[:, e0:e0 + edge] - wr[:, e0 + edge:e0 + 2 * edge]
+
+    @pl.when(step == pl.num_programs(0) - 1)
+    def _():
+        cols = rows + edge
+        count = place_ref.shape[1]
+        joined = jnp.concatenate(
+            [acc_ref[q, p] for q in range(2) for p in range(2)], axis=0
+        ).astype(jnp.bfloat16)
+        col_hit = (lax.broadcasted_iota(jnp.int32, (cols, count), 0) == place_ref[1:2, :]).astype(jnp.bfloat16)
+        row_hit = lax.broadcasted_iota(jnp.int32, (rows, count), 0) == place_ref[0:1, :]
+        by_column = jnp.dot(joined, col_hit, preferred_element_type=jnp.float32)
+        for k in range(4):
+            picked = jnp.where(row_hit, by_column[k * rows:(k + 1) * rows], 0.0)
+            out_ref[k:k + 1, :] = jnp.sum(picked, axis=0, keepdims=True).astype(out_ref.dtype)
+
+
+def element_values(own_slab, next_edge, diag_rates, pattern_row):
     _, blocks, rows, block_order = own_slab.shape
     edge = next_edge.shape[2]
+    cols = rows + edge
+    count = pattern_row.shape[0]
+    place = jnp.stack([pattern_row // cols, pattern_row % cols], axis=0)
     factor = 1.0 / math.sqrt(3.0 * block_order)
     kernel = functools.partial(_weigh_kernel, factor=factor, rows=rows, edge=edge)
     return pl.pallas_call(
@@ -61,15 +79,12 @@
             pl.BlockSpec((2, 1, rows, block_order), lambda j: (0, j, 0, 0)),
             pl.BlockSpec((2, 1, edge, block_order), lambda j: (0, jnp.maximum(j - 1, 0), 0, 0)),
             pl.BlockSpec((1, 2, 2, block_order), lambda j: (j, 0, 0, 0)),
+            pl.BlockSpec((2, count), lambda j: (0, 0)),
         ],
-        out_specs=pl.BlockSpec((2, 2, rows, rows + edge), lambda j: (0, 0, 0, 0)),
-        out_shape=jax.ShapeDtypeStruct((2, 2, rows, rows + edge), jnp.float32),
-    )(own_slab, next_edge, diag_rates)
-
-
-def element_values(own_slab, next_edge, diag_rates, pattern_row):
-    joined = weighed_products(own_slab, next_edge, diag_rates).astype(jnp.bfloat16)
-    return jnp.take(joined.reshape(4, -1), pattern_row, axis=1).reshape(2, 2, -1)
+        out_specs=pl.BlockSpec((4, count), lambda j: (0, 0)),
+        out_shape=jax.ShapeDtypeStruct((4, count), jnp.bfloat16),
+        scratch_shapes=[pltpu.VMEM((2, 2, rows, cols), jnp.float32)],
+    )(own_slab, next_edge, diag_rates, place)
 
 
 def _lag_kernel(in_ref, out_ref, *, width, factor):

time: 83.4 us -> 76.4 us (0.916)
  blocking collectives: 27.6 us -> 41 us
  waiting for transfers between devices: 14.1 us -> 4.09 us
  local copies, waits for them, and re-layouts: 11.2 us -> 5.1 us
  starting transfers between devices: 16.9 us -> 12.5 us
    all_to_all x0 -> x1, blocking collectives: none -> 13.4 us  [body(): lax.all_to_all(polarization, 'energy', split_axis=0, concat_axis=0, tiled...]
    all_to_all x1 -> x0, waiting for transfers between devices: 9.03 us -> none  [body(): lax.all_to_all(polarization, 'energy', split_axis=0, concat_axis=0, tiled...]
    gather x2 -> x0, local copies, waits for them, and re-layouts: 5.53 us -> none  [element_values(): jnp.take(joined.reshape(4, -1), pattern_row, axis=1).reshape(2, 2, -1)]
    all_to_all x1 -> x0, starting transfers between devices: 4.42 us -> none  [body(): lax.all_to_all(polarization, 'energy', split_axis=0, concat_axis=0, tiled...]
    ppermute x2, waiting for transfers between devices: 5.1 us -> 4.09 us  [passed_along(): return lax.ppermute(x, axis, pairs)]
    convert_element_type x1 -> x0, other arithmetic: 0.91 us -> none  [element_values(): weighed_products(own_slab, next_edge, diag_rates).astype(jnp.bfloat16)]
  transfers between devices with their start and end apart: 3 -> 2, of which waited for: 2 -> 1; matrix products, arithmetic and copies ran while one was open for 1% -> 2% of each run, Pallas kernels for 0% -> 0%
where the time goes in v11:
time: 76.4 us; the launch traced here: 75.8 us
  blocking collectives  41 us (54%)
  starting transfers between devices  12.5 us (16%)
  Pallas kernels  9.91 us (13%)
  local copies, waits for them, and re-layouts  5.1 us (7%)
  waiting for transfers between devices  4.09 us (5%)
  other arithmetic  3.09 us (4%)
    all_to_all x1, blocking collectives, body(): lax.all_to_all(values, 'energy', split_axis=0, concat_axis=0, tiled=True)  27.6 us
    all_to_all x1, blocking collectives, body(): lax.all_to_all(polarization, 'energy', split_axis=0, concat_axis=0, tiled...  13.4 us
    ppermute x2, starting transfers between devices, passed_along(): return lax.ppermute(x, axis, pairs)  12.5 us
    pallas_call x1, Pallas kernels, element_values(): pl.pallas_call(kernel, grid=(blocks,), in_specs=[pl.BlockSpec((2, 1, rows...  4.87 us
    ppermute x2, waiting for transfers between devices, passed_along(): return lax.ppermute(x, axis, pairs)  4.09 us
    pallas_call x1, Pallas kernels, lag_sums(): pl.pallas_call(kernel, out_shape=jax.ShapeDtypeStruct((energy_count, 2 *...  2.89 us
    pallas_call x1, Pallas kernels, screen(): pl.pallas_call(kernel, out_shape=jax.ShapeDtypeStruct((2, rows, rows), jn...  2.15 us
  transfers between devices with their start and end apart: 2, of which 1 were waited for; matrix products, arithmetic and copies ran while one was open for 2% of the time, Pallas kernels for 0%

profile of v11, /device:TPU:7, one launch (start us, length us, event | category | flops | bytes accessed | tf_op | source)
XLA Modules:
  0.0 75.8 jit_solution(9589536500948031471)
XLA Ops:
  0.0 0.0 copy-start
  0.0 0.9 %reduce-precision_convert_fusion.1 = (bf16[1,2,2,2048]{3,2,1,0:T(2,128)(2,1)S(1)}, bf16[1,2,2,2048]{3,2,1,0:T(2,128)(2,1)S(1)}, bf16[1,2,2,2048]{3,2,1,0:T(2,128)(2,1)S(1)}) fusion(f32[1,1,2,2,2048]{4,3,2,1,0:T(2,128)} %param.5), kind=kLoop, calls=%fused_computation.7 | loop fusion | flops 57344 | bytes 81920 | tf_op jit(solution)/shard_map/convert
  0.9 0.1 pad_maximum_fusion.2
  1.0 1.0 %slice.21 = bf16[1,1,2,2,16,2048]{5,4,3,2,1,0:T(8,128)(2,1)S(1)} slice(bf16[1,1,2,3,64,2048]{5,4,3,2,1,0:T(8,128)(2,1)} %param.4), slice={[0:1], [0:1], [0:2], [0:2], [0:16], [0:2048]} | slice | bytes 524288 | tf_op jit(solution)/shard_map/slice | solution.py:179
  2.0 2.5 %collective-permute-start = (bf16[76,2048]{1,0:T(8,128)(2,1)S(1)}, bf16[76,2048]{1,0:T(8,128)(2,1)S(1)}, u32[]{:S(2)}, u32[]{:S(2)}) collective-permute-start(bf16[76,2048]{1,0:T(8,128)(2,1)S(1)} %pad_maximum_fusion), channel_id=1, source_target_pairs={{1,0},{2,1},{3,2},{4,3},{5,4},{6,5},{7,6},{9,8},{10,9},{11,10},{12... | collective-permute-start | bytes 933896 | tf_op jit(solution)/shard_map/ppermute | solution.py:17
  4.5 10.0 %collective-permute-start.1 = (f32[2,2,2048]{2,1,0:T(2,128)}, f32[2,2,2048]{2,1,0:T(2,128)S(1)}, u32[]{:S(2)}, u32[]{:S(2)}) collective-permute-start(f32[2,2,2048]{2,1,0:T(2,128)} %bitcast.26), channel_id=1, source_target_pairs={{0,1},{1,2},{2,3},{3,4},{4,5},{5,6},{6,7},{8,9},{9,10},{10,11},{11... | collective-permute-start | bytes 98312 | tf_op jit(solution)/shard_map/ppermute | solution.py:17
  14.5 0.8 %and_select_fusion.1 = (s32[1,2560]{1,0:T(1,128)S(1)}, s32[1,2560]{1,0:T(1,128)S(1)}) fusion(s32[1,2560]{1,0:T(1,128)} %param.6), kind=kLoop, calls=%fused_computation.9 | loop fusion | flops 30720 | bytes 30720 | tf_op jit(solution)/shard_map/jit(floor_divide)/jit(_where)/select_n | solution.py:72
  15.3 0.6 pad_add_fusion.place_ref
  15.9 4.1 %collective-permute-done = bf16[76,2048]{1,0:T(8,128)(2,1)S(1)} collective-permute-done((bf16[76,2048]{1,0:T(8,128)(2,1)S(1)}, bf16[76,2048]{1,0:T(8,128)(2,1)S(1)}, u32[]{:S(2)}, u32[]{:S(2)}) %collective-permute-start) | collective-permute-done | bytes 311328 | tf_op jit(solution)/shard_map/ppermute | solution.py:17
  20.0 0.0 collective-permute-done.1
  20.1 0.0 copy-done
  20.1 0.7 pad_maximum_fusion.1.rate_ref
  20.8 0.7 slice.27
  21.5 4.9 %shard_map.46 = bf16[4,2560]{1,0:T(4,128)(2,1)} custom-call(bf16[2,3,64,2048]{3,2,1,0:T(8,128)(2,1)} %bitcast.20, bf16[2,2,16,2048]{3,2,1,0:T(8,128)(2,1)} %bitcast.21, f32[3,2,2,2048]{3,2,1,0:T(2,128)} %pad_maximum_fusion.1.rate_ref, s32[2,2560]{1,0:T(2,128)} %pad_add_fusion.place_ref), custom_call_target="tpu_custom_call" | custom-call | tf_op jit(solution)/shard_map/pallas_call | solution.py:75
  26.3 0.9 %reshape.66 = bf16[4,64,40]{2,1,0:T(8,128)(2,1)S(1)} reshape(bf16[4,2560]{1,0:T(4,128)(2,1)} %shard_map.46) | data formatting | bytes 40960 | tf_op jit(solution)/shard_map/reshape | solution.py:190
  27.2 0.1 copy.16
  27.3 0.1 copy.17
  27.4 27.6 %all_to_all.20 = bf16[64,1,160]{2,1,0:T(2,128)(2,1)S(1)} all-to-all(bf16[64,1,160]{2,1,0:T(2,128)(2,1)S(1)} %copy.17), channel_id=1, replica_groups=mesh['energy'=64,'domain'=8] {'energy'}, dimensions={0} | all-to-all | bytes 40960 | tf_op jit(solution)/shard_map/all_to_all | solution.py:191
  55.1 0.6 copy.23
  55.7 2.9 %shard_map.47 = bf16[64,80]{1,0:T(8,128)(2,1)} custom-call(bf16[64,160]{1,0:T(8,128)(2,1)} %bitcast.25), custom_call_target="tpu_custom_call" | custom-call | tf_op jit(solution)/shard_map/pallas_call | solution.py:109
  58.6 0.7 copy.18
  59.3 13.4 %all_to_all.21 = bf16[64,1,80]{2,1,0:T(2,128)(2,1)S(1)} all-to-all(bf16[64,1,80]{2,1,0:T(2,128)(2,1)S(1)} %copy.18), channel_id=1, replica_groups=mesh['energy'=64,'domain'=8] {'energy'}, dimensions={0} | all-to-all | bytes 20480 | tf_op jit(solution)/shard_map/all_to_all | solution.py:193
  72.7 0.1 copy.19
  72.8 0.1 copy.20
  72.9 0.7 reshape.68.polar_ref
  73.6 2.1 %shard_map.48 = f32[2,64,64]{2,1,0:T(8,128)} custom-call(bf16[2,2560]{1,0:T(2,128)(2,1)} %reshape.68.polar_ref, s32[2,2560]{1,0:T(2,128)} %pad_add_fusion.place_ref, bf16[2,64,80]{2,1,0:T(8,128)(2,1)} %bitcast.30), custom_call_target="tpu_custom_call" | custom-call | tf_op jit(solution)/shard_map/pallas_call | solution.py:156
  (5 shorter events, 0.1 us)
Async XLA Ops:
  0.0 20.1 %copy-start = (f32[1,1,2,2,2048]{4,3,2,1,0:T(2,128)S(1)}, f32[1,1,2,2,2048]{4,3,2,1,0:T(2,128)}, u32[]{:S(2)}) copy-start(f32[1,1,2,2,2048]{4,3,2,1,0:T(2,128)} %param.5) | copy-start | bytes 98308
  2.0 18.0 %collective-permute-start = (bf16[76,2048]{1,0:T(8,128)(2,1)S(1)}, bf16[76,2048]{1,0:T(8,128)(2,1)S(1)}, u32[]{:S(2)}, u32[]{:S(2)}) collective-permute-start(bf16[76,2048]{1,0:T(8,128)(2,1)S(1)} %pad_maximum_fusion), channel_id=1, source_target_pairs={{1,0},{2,1},{3,2},{4,3},{5,4},{6,5},{7,6},{9,8},{10,9},{11,10},{12... | collective-permute-start | bytes 933896 | tf_op jit(solution)/shard_map/ppermute | solution.py:17
  4.5 15.6 %collective-permute-start.1 = (f32[2,2,2048]{2,1,0:T(2,128)}, f32[2,2,2048]{2,1,0:T(2,128)S(1)}, u32[]{:S(2)}, u32[]{:S(2)}) collective-permute-start(f32[2,2,2048]{2,1,0:T(2,128)} %bitcast.26), channel_id=1, source_target_pairs={{0,1},{1,2},{2,3},{3,4},{4,5},{5,6},{6,7},{8,9},{9,10},{10,11},{11... | collective-permute-start | bytes 98312 | tf_op jit(solution)/shard_map/ppermute | solution.py:17

commit v12 on v11

--- a/solution.py
+++ b/solution.py
@@ -159,6 +159,19 @@
     )(polar_row, place, screen_block)
 
 
+def own_lag(by_energy):
+    energy_count = by_energy.shape[0]
+    lag = lax.axis_index("energy")
+    lesser = by_energy[:, 0:2].astype(jnp.float32)
+    greater = jnp.roll(by_energy[:, 2:4].astype(jnp.float32), lag, axis=0)
+    inside = (jnp.arange(energy_count) >= lag)[:, None]
+    greater = jnp.where(inside[:, None], greater, 0.0)
+    real_sum = jnp.sum(lesser[:, 0] * greater[:, 0] - lesser[:, 1] * greater[:, 1], axis=0)
+    imag_sum = jnp.sum(lesser[:, 0] * greater[:, 1] + lesser[:, 1] * greater[:, 0], axis=0)
+    factor = 1.0 / math.sqrt(energy_count)
+    return (jnp.stack([real_sum, imag_sum], axis=0) * factor).astype(jnp.bfloat16)
+
+
 def split_exact(value):
     high = lax.reduce_precision(value, exponent_bits=8, mantissa_bits=7)
     rest = value - high
@@ -186,12 +199,10 @@
     next_rate = join_exact(bundle[edge_rows:].reshape(3, *own_rate.shape))
     nearby = jnp.stack([previous_rate, own_rate, next_rate], axis=0)[None]
     values = element_values(green_slab[0, 0], following, nearby[0], pattern[0])
-    chunks = lax.axis_size("energy")
-    values = values.reshape(4, chunks, -1).transpose(1, 0, 2).reshape(chunks, -1)
-    by_element = lax.all_to_all(values, "energy", split_axis=0, concat_axis=0, tiled=True)
-    polarization = lag_sums(by_element)
-    per_energy = lax.all_to_all(polarization, "energy", split_axis=0, concat_axis=0, tiled=True)
-    per_energy = per_energy.reshape(chunks, 2, -1).transpose(1, 0, 2).reshape(2, -1)
+    energy_count = lax.axis_size("energy")
+    spread = jnp.broadcast_to(values[None], (energy_count, *values.shape))
+    by_energy = lax.all_to_all(spread, "energy", split_axis=0, concat_axis=0, tiled=True)
+    per_energy = own_lag(by_energy)
     result = screen(per_energy, pattern[0], screened[0, 0])
     return result[None, None]
 

time: 76.4 us -> 100 us (1.31)
  waiting for transfers between devices: 4.09 us -> 47.7 us
  blocking collectives: 41 us -> 0 us
  starting transfers between devices: 12.5 us -> 30.9 us
  other arithmetic: 3.09 us -> 9.71 us
  Pallas kernels: 9.91 us -> 7.04 us
  local copies, waits for them, and re-layouts: 5.1 us -> 3.9 us
    all_to_all x2 -> x0, blocking collectives: 41 us -> none  [the longest x1 27.6 us: body(): lax.all_to_all(values, 'energy', split_axis=0, concat_axis=0, tiled=True)]
    all_to_all x0 -> x1, waiting for transfers between devices: none -> 34.2 us  [body(): lax.all_to_all(spread, 'energy', split_axis=0, concat_axis=0, tiled=True)]
    all_to_all x0 -> x1, starting transfers between devices: none -> 18.3 us  [body(): lax.all_to_all(spread, 'energy', split_axis=0, concat_axis=0, tiled=True)]
    ppermute x2, waiting for transfers between devices: 4.09 us -> 13.5 us  [passed_along(): return lax.ppermute(x, axis, pairs)]
    select_n x0 -> x1, other arithmetic: none -> 3.37 us  [own_lag(): greater = jnp.where(inside[:, None], greater, 0.0)]
    pallas_call x1 -> x0, Pallas kernels: 2.89 us -> none  [lag_sums(): pl.pallas_call(kernel, out_shape=jax.ShapeDtypeStruct((energy_count, 2 *...]
    reduce_sum x0 -> x1, other arithmetic: none -> 2.47 us  [own_lag(): jnp.sum(lesser[:, 0] * greater[:, 0] - lesser[:, 1] * greater[:, 1], axis=0)]
    broadcast_in_dim x0 -> x1, local copies, waits for them, and re-layouts: none -> 2.14 us  [body(): spread = jnp.broadcast_to(values[None], (energy_count, *values.shape))]
  transfers between devices with their start and end apart: 2 -> 3, of which waited for: 1 -> 2; matrix products, arithmetic and copies ran while one was open for 2% -> 3% of each run, Pallas kernels for 0% -> 0%
where the time goes in v12:
time: 100 us; the launch traced here: 99.4 us
  waiting for transfers between devices  47.7 us (48%)
  starting transfers between devices  30.9 us (31%)
  other arithmetic  9.71 us (10%)
  Pallas kernels  7.04 us (7%)
  local copies, waits for them, and re-layouts  3.9 us (4%)
    all_to_all x1, waiting for transfers between devices, body(): lax.all_to_all(spread, 'energy', split_axis=0, concat_axis=0, tiled=True)  34.2 us
    all_to_all x1, starting transfers between devices, body(): lax.all_to_all(spread, 'energy', split_axis=0, concat_axis=0, tiled=True)  18.3 us
    ppermute x2, waiting for transfers between devices, passed_along(): return lax.ppermute(x, axis, pairs)  13.5 us
    ppermute x2, starting transfers between devices, passed_along(): return lax.ppermute(x, axis, pairs)  12.6 us
    pallas_call x1, Pallas kernels, element_values(): pl.pallas_call(kernel, grid=(blocks,), in_specs=[pl.BlockSpec((2, 1, rows...  4.88 us
    select_n x1, other arithmetic, own_lag(): greater = jnp.where(inside[:, None], greater, 0.0)  3.37 us
    reduce_sum x1, other arithmetic, own_lag(): jnp.sum(lesser[:, 0] * greater[:, 0] - lesser[:, 1] * greater[:, 1], axis=0)  2.47 us
    pallas_call x1, Pallas kernels, screen(): pl.pallas_call(kernel, out_shape=jax.ShapeDtypeStruct((2, rows, rows), jn...  2.16 us
  transfers between devices with their start and end apart: 3, of which 2 were waited for; matrix products, arithmetic and copies ran while one was open for 3% of the time, Pallas kernels for 0%

profile of v12, /device:TPU:7, one launch (start us, length us, event | category | flops | bytes accessed | tf_op | source)
XLA Modules:
  0.0 99.4 jit_solution(4786983434993209234)
XLA Ops:
  0.0 0.0 copy-start
  0.0 0.0 copy-start.1
  0.0 10.7 %collective-permute-start.1 = (f32[2,2,2048]{2,1,0:T(2,128)}, f32[2,2,2048]{2,1,0:T(2,128)S(1)}, u32[]{:S(2)}, u32[]{:S(2)}) collective-permute-start(f32[2,2,2048]{2,1,0:T(2,128)} %bitcast.14), channel_id=1, source_target_pairs={{0,1},{1,2},{2,3},{3,4},{4,5},{5,6},{6,7},{8,9},{9,10},{10,11},{11... | collective-permute-start | bytes 98312 | tf_op jit(solution)/shard_map/ppermute | solution.py:17
  10.7 0.8 reduce-precision_convert_fusion.1
  11.5 0.1 pad_maximum_fusion.2
  11.6 1.0 slice.43
  12.6 1.9 %collective-permute-start = (bf16[76,2048]{1,0:T(8,128)(2,1)S(1)}, bf16[76,2048]{1,0:T(8,128)(2,1)S(1)}, u32[]{:S(2)}, u32[]{:S(2)}) collective-permute-start(bf16[76,2048]{1,0:T(8,128)(2,1)S(1)} %pad_maximum_fusion), channel_id=1, source_target_pairs={{1,0},{2,1},{3,2},{4,3},{5,4},{6,5},{7,6},{9,8},{10,9},{11,10},{12... | collective-permute-start | bytes 933896 | tf_op jit(solution)/shard_map/ppermute | solution.py:17
  14.5 0.0 copy-done.1
  14.6 0.1 and_select_fusion.1
  14.6 0.6 pad_add_fusion.place_ref
  15.3 13.5 %collective-permute-done = bf16[76,2048]{1,0:T(8,128)(2,1)S(1)} collective-permute-done((bf16[76,2048]{1,0:T(8,128)(2,1)S(1)}, bf16[76,2048]{1,0:T(8,128)(2,1)S(1)}, u32[]{:S(2)}, u32[]{:S(2)}) %collective-permute-start) | collective-permute-done | bytes 311328 | tf_op jit(solution)/shard_map/ppermute | solution.py:17
  28.9 0.0 collective-permute-done.1
  28.9 0.0 copy-done
  28.9 0.7 pad_maximum_fusion.1.rate_ref
  29.6 0.7 slice.55
  30.3 4.9 %shard_map.46 = bf16[4,2560]{1,0:T(4,128)(2,1)} custom-call(bf16[2,3,64,2048]{3,2,1,0:T(8,128)(2,1)} %bitcast.11, bf16[2,2,16,2048]{3,2,1,0:T(8,128)(2,1)} %bitcast.12, f32[3,2,2,2048]{3,2,1,0:T(2,128)} %pad_maximum_fusion.1.rate_ref, s32[2,2560]{1,0:T(2,128)} %pad_add_fusion.place_ref), custom_call_target="tpu_custom_call" | custom-call | tf_op jit(solution)/shard_map/pallas_call | solution.py:75
  35.2 2.1 %broadcast_in_dim.21 = bf16[64,4,2560]{2,1,0:T(4,128)(2,1)} broadcast(bf16[4,2560]{1,0:T(4,128)(2,1)} %shard_map.46), dimensions={1,2} | broadcast | bytes 1331200 | tf_op jit(solution)/shard_map/broadcast_in_dim | solution.py:203
  37.3 18.3 %all-to-all-start = ((bf16[64,4,2560]{2,1,0:T(4,128)(2,1)}), bf16[64,4,2560]{2,1,0:T(4,128)(2,1)S(1)}, u32[]{:S(2)}, u32[]{:S(2)}) async-start(bf16[64,4,2560]{2,1,0:T(4,128)(2,1)} %broadcast_in_dim.21), calls=%async_computation | async-start | bytes 2621440 | tf_op jit(solution)/shard_map/all_to_all | solution.py:204
  55.7 34.2 %all-to-all-done = bf16[64,4,2560]{2,1,0:T(4,128)(2,1)S(1)} async-done(((bf16[64,4,2560]{2,1,0:T(4,128)(2,1)}), bf16[64,4,2560]{2,1,0:T(4,128)(2,1)S(1)}, u32[]{:S(2)}, u32[]{:S(2)}) %all-to-all-start) | async-done | bytes 1310752 | tf_op jit(solution)/shard_map/all_to_all | solution.py:204
  89.8 0.9 slice_convert_fusion
  90.7 3.4 %convert_select_fusion = f32[64,2,2560]{2,1,0:T(2,128)S(1)} fusion(pred[64]{0:T(512)(128)(4,1)S(1)} %iota_compare_fusion, s32[]{:T(128)S(6)} %select_n.36, bf16[64,2,2560]{2,1,0:T(2,128)(2,1)S(1)} %get-tuple-element.8), kind=kLoop, calls=%fused_computation.2 | loop fusion | flops 983040 | bytes 1966148 | tf_op jit(solution)/shard_map/jit(_where)/select_n | solution.py:168
  94.1 2.5 %subtract_reduce_fusion = (f32[2560]{0:T(1024)S(1)}, f32[2560]{0:T(1024)S(1)}) fusion(f32[64,2,2560]{2,1,0:T(2,128)S(1)} %convert_select_fusion, f32[64,2,2560]{2,1,0:T(2,128)S(1)} %get-tuple-element.7), kind=kLoop, calls=%fused_computation.6 | loop fusion | flops 1305600 | bytes 2641920 | tf_op jit(solution)/shard_map/reduce_sum | solution.py:169
  96.6 0.6 fusion.2.polar_ref
  97.2 2.2 %shard_map.47 = f32[2,64,64]{2,1,0:T(8,128)} custom-call(bf16[2,2560]{1,0:T(2,128)(2,1)} %fusion.2.polar_ref, s32[2,2560]{1,0:T(2,128)} %pad_add_fusion.place_ref, bf16[2,64,80]{2,1,0:T(8,128)(2,1)} %bitcast.16), custom_call_target="tpu_custom_call" | custom-call | tf_op jit(solution)/shard_map/pallas_call | solution.py:156
  (8 shorter events, 0.1 us)
Async XLA Ops:
  0.0 28.9 %copy-start = (f32[1,1,2,2,2048]{4,3,2,1,0:T(2,128)S(1)}, f32[1,1,2,2,2048]{4,3,2,1,0:T(2,128)}, u32[]{:S(2)}) copy-start(f32[1,1,2,2,2048]{4,3,2,1,0:T(2,128)} %param.5) | copy-start | bytes 98308
  0.0 14.5 %copy-start.1 = (s32[1,2560]{1,0:T(1,128)S(1)}, s32[1,2560]{1,0:T(1,128)}, u32[]{:S(2)}) copy-start(s32[1,2560]{1,0:T(1,128)} %param.6) | copy-start | bytes 30724
  0.0 28.9 %collective-permute-start.1 = (f32[2,2,2048]{2,1,0:T(2,128)}, f32[2,2,2048]{2,1,0:T(2,128)S(1)}, u32[]{:S(2)}, u32[]{:S(2)}) collective-permute-start(f32[2,2,2048]{2,1,0:T(2,128)} %bitcast.14), channel_id=1, source_target_pairs={{0,1},{1,2},{2,3},{3,4},{4,5},{5,6},{6,7},{8,9},{9,10},{10,11},{11... | collective-permute-start | bytes 98312 | tf_op jit(solution)/shard_map/ppermute | solution.py:17
  12.6 16.2 %collective-permute-start = (bf16[76,2048]{1,0:T(8,128)(2,1)S(1)}, bf16[76,2048]{1,0:T(8,128)(2,1)S(1)}, u32[]{:S(2)}, u32[]{:S(2)}) collective-permute-start(bf16[76,2048]{1,0:T(8,128)(2,1)S(1)} %pad_maximum_fusion), channel_id=1, source_target_pairs={{1,0},{2,1},{3,2},{4,3},{5,4},{6,5},{7,6},{9,8},{10,9},{11,10},{12... | collective-permute-start | bytes 933896 | tf_op jit(solution)/shard_map/ppermute | solution.py:17
  37.3 52.5 %all-to-all-start = ((bf16[64,4,2560]{2,1,0:T(4,128)(2,1)}), bf16[64,4,2560]{2,1,0:T(4,128)(2,1)S(1)}, u32[]{:S(2)}, u32[]{:S(2)}) async-start(bf16[64,4,2560]{2,1,0:T(4,128)(2,1)} %broadcast_in_dim.21), calls=%async_computation | async-start | bytes 2621440 | tf_op jit(solution)/shard_map/all_to_all | solution.py:204

commit v13 on v11

--- a/solution.py
+++ b/solution.py
@@ -88,7 +88,7 @@
 
 
 def _lag_kernel(in_ref, out_ref, *, width, factor):
-    values = in_ref[...].astype(jnp.float32)
+    values = in_ref[:, 0, :].astype(jnp.float32)
     energy_count = values.shape[0]
     lesser = values[:, 0:2 * width]
     greater = values[:, 2 * width:4 * width]
@@ -99,16 +99,16 @@
         straight = jnp.sum(head * greater[:energy_count - lag], axis=0, keepdims=True)
         crossed = jnp.sum(head * swapped[:energy_count - lag], axis=0, keepdims=True)
         rows.append(jnp.concatenate([straight[:, :width] - straight[:, width:], crossed[:, :width] + crossed[:, width:]], axis=1))
-    out_ref[...] = (jnp.concatenate(rows, axis=0) * factor).astype(out_ref.dtype)
+    out_ref[:, 0, :] = (jnp.concatenate(rows, axis=0) * factor).astype(out_ref.dtype)
 
 
 def lag_sums(by_element):
-    energy_count, joined = by_element.shape
+    energy_count, _, joined = by_element.shape
     width = joined // 4
     kernel = functools.partial(_lag_kernel, width=width, factor=1.0 / math.sqrt(energy_count))
     return pl.pallas_call(
         kernel,
-        out_shape=jax.ShapeDtypeStruct((energy_count, 2 * width), jnp.bfloat16),
+        out_shape=jax.ShapeDtypeStruct((energy_count, 1, 2 * width), jnp.bfloat16),
     )(by_element)
 
 
@@ -187,7 +187,7 @@
     nearby = jnp.stack([previous_rate, own_rate, next_rate], axis=0)[None]
     values = element_values(green_slab[0, 0], following, nearby[0], pattern[0])
     chunks = lax.axis_size("energy")
-    values = values.reshape(4, chunks, -1).transpose(1, 0, 2).reshape(chunks, -1)
+    values = values.reshape(4, chunks, -1).transpose(1, 0, 2).reshape(chunks, 1, -1)
     by_element = lax.all_to_all(values, "energy", split_axis=0, concat_axis=0, tiled=True)
     polarization = lag_sums(by_element)
     per_energy = lax.all_to_all(polarization, "energy", split_axis=0, concat_axis=0, tiled=True)

time: 76.4 us -> 76.3 us (level)
  local copies, waits for them, and re-layouts: 5.1 us -> 3.73 us
  blocking collectives: 41 us -> 41.9 us
    all_to_all x1, blocking collectives: 13.4 us -> 14.1 us  [body(): lax.all_to_all(polarization, 'energy', split_axis=0, concat_axis=0, tiled...]
where the time goes in v13:
time: 76.3 us; the launch traced here: 75.7 us
  blocking collectives  41.9 us (55%)
  starting transfers between devices  12.5 us (16%)
  Pallas kernels  10.3 us (13%)
  waiting for transfers between devices  4.09 us (5%)
  local copies, waits for them, and re-layouts  3.73 us (5%)
  other arithmetic  3.09 us (4%)
    all_to_all x1, blocking collectives, body(): lax.all_to_all(values, 'energy', split_axis=0, concat_axis=0, tiled=True)  27.8 us
    all_to_all x1, blocking collectives, body(): lax.all_to_all(polarization, 'energy', split_axis=0, concat_axis=0, tiled...  14.1 us
    ppermute x2, starting transfers between devices, passed_along(): return lax.ppermute(x, axis, pairs)  12.5 us
    pallas_call x1, Pallas kernels, element_values(): pl.pallas_call(kernel, grid=(blocks,), in_specs=[pl.BlockSpec((2, 1, rows...  4.87 us
    ppermute x2, waiting for transfers between devices, passed_along(): return lax.ppermute(x, axis, pairs)  4.09 us
    pallas_call x1, Pallas kernels, lag_sums(): pl.pallas_call(kernel, out_shape=jax.ShapeDtypeStruct((energy_count, 1, 2...  3.32 us
    pallas_call x1, Pallas kernels, screen(): pl.pallas_call(kernel, out_shape=jax.ShapeDtypeStruct((2, rows, rows), jn...  2.15 us
  transfers between devices with their start and end apart: 2, of which 1 were waited for; matrix products, arithmetic and copies ran while one was open for 2% of the time, Pallas kernels for 0%

profile of v13, /device:TPU:7, one launch (start us, length us, event | category | flops | bytes accessed | tf_op | source)
XLA Modules:
  0.0 75.7 jit_solution(12301894486678500781)
XLA Ops:
  0.0 0.0 copy-start
  0.0 0.9 %reduce-precision_convert_fusion.1 = (bf16[1,2,2,2048]{3,2,1,0:T(2,128)(2,1)S(1)}, bf16[1,2,2,2048]{3,2,1,0:T(2,128)(2,1)S(1)}, bf16[1,2,2,2048]{3,2,1,0:T(2,128)(2,1)S(1)}) fusion(f32[1,1,2,2,2048]{4,3,2,1,0:T(2,128)} %param.5), kind=kLoop, calls=%fused_computation.7 | loop fusion | flops 57344 | bytes 81920 | tf_op jit(solution)/shard_map/convert
  0.9 0.1 pad_maximum_fusion.2
  1.0 1.0 %slice.21 = bf16[1,1,2,2,16,2048]{5,4,3,2,1,0:T(8,128)(2,1)S(1)} slice(bf16[1,1,2,3,64,2048]{5,4,3,2,1,0:T(8,128)(2,1)} %param.4), slice={[0:1], [0:1], [0:2], [0:2], [0:16], [0:2048]} | slice | bytes 524288 | tf_op jit(solution)/shard_map/slice | solution.py:179
  2.0 2.5 %collective-permute-start = (bf16[76,2048]{1,0:T(8,128)(2,1)S(1)}, bf16[76,2048]{1,0:T(8,128)(2,1)S(1)}, u32[]{:S(2)}, u32[]{:S(2)}) collective-permute-start(bf16[76,2048]{1,0:T(8,128)(2,1)S(1)} %pad_maximum_fusion), channel_id=1, source_target_pairs={{1,0},{2,1},{3,2},{4,3},{5,4},{6,5},{7,6},{9,8},{10,9},{11,10},{12... | collective-permute-start | bytes 933896 | tf_op jit(solution)/shard_map/ppermute | solution.py:17
  4.5 10.0 %collective-permute-start.1 = (f32[2,2,2048]{2,1,0:T(2,128)}, f32[2,2,2048]{2,1,0:T(2,128)S(1)}, u32[]{:S(2)}, u32[]{:S(2)}) collective-permute-start(f32[2,2,2048]{2,1,0:T(2,128)} %bitcast.21), channel_id=1, source_target_pairs={{0,1},{1,2},{2,3},{3,4},{4,5},{5,6},{6,7},{8,9},{9,10},{10,11},{11... | collective-permute-start | bytes 98312 | tf_op jit(solution)/shard_map/ppermute | solution.py:17
  14.5 0.8 %and_select_fusion.1 = (s32[1,2560]{1,0:T(1,128)S(1)}, s32[1,2560]{1,0:T(1,128)S(1)}) fusion(s32[1,2560]{1,0:T(1,128)} %param.6), kind=kLoop, calls=%fused_computation.9 | loop fusion | flops 30720 | bytes 30720 | tf_op jit(solution)/shard_map/jit(floor_divide)/jit(_where)/select_n | solution.py:72
  15.3 0.6 pad_add_fusion.place_ref
  15.9 4.1 %collective-permute-done = bf16[76,2048]{1,0:T(8,128)(2,1)S(1)} collective-permute-done((bf16[76,2048]{1,0:T(8,128)(2,1)S(1)}, bf16[76,2048]{1,0:T(8,128)(2,1)S(1)}, u32[]{:S(2)}, u32[]{:S(2)}) %collective-permute-start) | collective-permute-done | bytes 311328 | tf_op jit(solution)/shard_map/ppermute | solution.py:17
  20.0 0.0 collective-permute-done.1
  20.1 0.0 copy-done
  20.1 0.7 pad_maximum_fusion.1.rate_ref
  20.8 0.7 slice.27
  21.5 4.9 %shard_map.46 = bf16[4,2560]{1,0:T(4,128)(2,1)} custom-call(bf16[2,3,64,2048]{3,2,1,0:T(8,128)(2,1)} %bitcast.16, bf16[2,2,16,2048]{3,2,1,0:T(8,128)(2,1)} %bitcast.17, f32[3,2,2,2048]{3,2,1,0:T(2,128)} %pad_maximum_fusion.1.rate_ref, s32[2,2560]{1,0:T(2,128)} %pad_add_fusion.place_ref), custom_call_target="tpu_custom_call" | custom-call | tf_op jit(solution)/shard_map/pallas_call | solution.py:75
  26.3 0.9 %reshape.62 = bf16[4,64,40]{2,1,0:T(8,128)(2,1)S(1)} reshape(bf16[4,2560]{1,0:T(4,128)(2,1)} %shard_map.46) | data formatting | bytes 40960 | tf_op jit(solution)/shard_map/reshape | solution.py:190
  27.2 0.1 copy.7
  27.3 0.1 copy.8
  27.4 27.8 %all_to_all.10.in_ref = bf16[64,1,160]{2,1,0:T(2,128)(2,1)} all-to-all(bf16[64,1,160]{2,1,0:T(2,128)(2,1)S(1)} %copy.8), channel_id=1, replica_groups=mesh['energy'=64,'domain'=8] {'energy'}, dimensions={0} | all-to-all | bytes 40960 | tf_op jit(solution)/shard_map/all_to_all | solution.py:191
  55.2 3.3 %shard_map.47 = bf16[64,1,80]{2,1,0:T(2,128)(2,1)} custom-call(bf16[64,1,160]{2,1,0:T(2,128)(2,1)} %all_to_all.10.in_ref), custom_call_target="tpu_custom_call" | custom-call | tf_op jit(solution)/shard_map/pallas_call | solution.py:109
  58.5 14.1 %all_to_all.11 = bf16[64,1,80]{2,1,0:T(2,128)(2,1)S(1)} all-to-all(bf16[64,1,80]{2,1,0:T(2,128)(2,1)} %shard_map.47), channel_id=1, replica_groups=mesh['energy'=64,'domain'=8] {'energy'}, dimensions={0} | all-to-all | bytes 20480 | tf_op jit(solution)/shard_map/all_to_all | solution.py:193
  72.7 0.1 copy.9
  72.8 0.1 copy.10
  72.9 0.7 reshape.65.polar_ref
  73.6 2.2 %shard_map.48 = f32[2,64,64]{2,1,0:T(8,128)} custom-call(bf16[2,2560]{1,0:T(2,128)(2,1)} %reshape.65.polar_ref, s32[2,2560]{1,0:T(2,128)} %pad_add_fusion.place_ref, bf16[2,64,80]{2,1,0:T(8,128)(2,1)} %bitcast.24), custom_call_target="tpu_custom_call" | custom-call | tf_op jit(solution)/shard_map/pallas_call | solution.py:156
  (5 shorter events, 0.1 us)
Async XLA Ops:
  0.0 20.1 %copy-start = (f32[1,1,2,2,2048]{4,3,2,1,0:T(2,128)S(1)}, f32[1,1,2,2,2048]{4,3,2,1,0:T(2,128)}, u32[]{:S(2)}) copy-start(f32[1,1,2,2,2048]{4,3,2,1,0:T(2,128)} %param.5) | copy-start | bytes 98308
  2.0 18.0 %collective-permute-start = (bf16[76,2048]{1,0:T(8,128)(2,1)S(1)}, bf16[76,2048]{1,0:T(8,128)(2,1)S(1)}, u32[]{:S(2)}, u32[]{:S(2)}) collective-permute-start(bf16[76,2048]{1,0:T(8,128)(2,1)S(1)} %pad_maximum_fusion), channel_id=1, source_target_pairs={{1,0},{2,1},{3,2},{4,3},{5,4},{6,5},{7,6},{9,8},{10,9},{11,10},{12... | collective-permute-start | bytes 933896 | tf_op jit(solution)/shard_map/ppermute | solution.py:17
  4.5 15.6 %collective-permute-start.1 = (f32[2,2,2048]{2,1,0:T(2,128)}, f32[2,2,2048]{2,1,0:T(2,128)S(1)}, u32[]{:S(2)}, u32[]{:S(2)}) collective-permute-start(f32[2,2,2048]{2,1,0:T(2,128)} %bitcast.21), channel_id=1, source_target_pairs={{0,1},{1,2},{2,3},{3,4},{4,5},{5,6},{6,7},{8,9},{9,10},{10,11},{11... | collective-permute-start | bytes 98312 | tf_op jit(solution)/shard_map/ppermute | solution.py:17

commit v14 on v13

--- a/solution.py
+++ b/solution.py
@@ -17,74 +17,123 @@
     return lax.ppermute(x, axis, pairs)
 
 
-def _weigh_kernel(slab_ref, edge_ref, rate_ref, place_ref, out_ref, acc_ref, *, factor, rows, edge):
+def _weigh(real_f, imag_f, rate_ref, block, factor):
+    pieces = []
+    for q in range(2):
+        rate_real = rate_ref[block, q, 0:1, :]
+        rate_imag = rate_ref[block, q, 1:2, :]
+        pieces.append(((real_f * rate_real - imag_f * rate_imag) * factor).astype(jnp.bfloat16))
+        pieces.append(((real_f * rate_imag + imag_f * rate_real) * factor).astype(jnp.bfloat16))
+    return jnp.concatenate(pieces, axis=0)
+
+
+def _adjoint_parts(prod, q, rows, start, width):
+    wr = prod[2 * q * rows:(2 * q + 1) * rows]
+    wi = prod[(2 * q + 1) * rows:(2 * q + 2) * rows]
+    real = wr[:, start:start + width] + wi[:, start + width:start + 2 * width]
+    imag = wi[:, start:start + width] - wr[:, start + width:start + 2 * width]
+    return real, imag
+
+
+def _nt(a, b):
+    return lax.dot_general(a, b, (((1,), (1,)), ((), ())), preferred_element_type=jnp.float32)
+
+
+def _early_kernel(slab_ref, rate_ref, near_ref, held_ref, *, factor, rows):
     step = pl.program_id(0)
 
     @pl.when(step == 0)
     def _():
-        acc_ref[...] = jnp.zeros_like(acc_ref)
+        near_ref[...] = jnp.zeros_like(near_ref)
 
     slab_real = slab_ref[0, 0]
     slab_imag = slab_ref[1, 0]
-    real_f = slab_real.astype(jnp.float32)
-    imag_f = slab_imag.astype(jnp.float32)
-    pieces = []
+    left = _weigh(slab_real.astype(jnp.float32), slab_imag.astype(jnp.float32), rate_ref, 0, factor)
+    prod = _nt(left, jnp.concatenate([slab_real, slab_imag], axis=0))
     for q in range(2):
-        rate_real = rate_ref[0, q, 0:1, :]
-        rate_imag = rate_ref[0, q, 1:2, :]
-        pieces.append(((real_f * rate_real - imag_f * rate_imag) * factor).astype(jnp.bfloat16))
-        pieces.append(((real_f * rate_imag + imag_f * rate_real) * factor).astype(jnp.bfloat16))
-    left = jnp.concatenate(pieces, axis=0)
-    right = jnp.concatenate([slab_real, slab_imag, edge_ref[0, 0], edge_ref[1, 0]], axis=0)
-    prod = lax.dot_general(left, right, (((1,), (1,)), ((), ())), preferred_element_type=jnp.float32)
-    for q in range(2):
-        wr = prod[2 * q * rows:(2 * q + 1) * rows]
-        wi = prod[(2 * q + 1) * rows:(2 * q + 2) * rows]
-        acc_ref[q, 0, :, 0:rows] += wr[:, 0:rows] + wi[:, rows:2 * rows]
-        acc_ref[q, 1, :, 0:rows] += wi[:, 0:rows] - wr[:, rows:2 * rows]
-
-        @pl.when(step > 0)
-        def _():
-            e0 = 2 * rows
-            acc_ref[q, 0, :, rows:rows + edge] += wr[:, e0:e0 + edge] + wi[:, e0 + edge:e0 + 2 * edge]
-            acc_ref[q, 1, :, rows:rows + edge] += wi[:, e0:e0 + edge] - wr[:, e0 + edge:e0 + 2 * edge]
+        real, imag = _adjoint_parts(prod, q, rows, 0, rows)
+        near_ref[q, 0] += real
+        near_ref[q, 1] += imag
 
     @pl.when(step == pl.num_programs(0) - 1)
     def _():
-        cols = rows + edge
-        count = place_ref.shape[1]
-        joined = jnp.concatenate(
-            [acc_ref[q, p] for q in range(2) for p in range(2)], axis=0
-        ).astype(jnp.bfloat16)
-        col_hit = (lax.broadcasted_iota(jnp.int32, (cols, count), 0) == place_ref[1:2, :]).astype(jnp.bfloat16)
-        row_hit = lax.broadcasted_iota(jnp.int32, (rows, count), 0) == place_ref[0:1, :]
-        by_column = jnp.dot(joined, col_hit, preferred_element_type=jnp.float32)
-        for k in range(4):
-            picked = jnp.where(row_hit, by_column[k * rows:(k + 1) * rows], 0.0)
-            out_ref[k:k + 1, :] = jnp.sum(picked, axis=0, keepdims=True).astype(out_ref.dtype)
-
-
-def element_values(own_slab, next_edge, diag_rates, pattern_row):
+        held_ref[...] = left
+
+
+def _late_kernel(slab_ref, bundle_ref, near_ref, held_ref, place_ref, out_ref, rate_scr,
+                 *, factor, rows, edge):
+    cols = rows + edge
+    edge_rows = 4 * edge
+    for piece_q in range(2):
+        for part in range(2):
+            k = piece_q * 2 + part
+            pieces = [bundle_ref[edge_rows + 4 * t + k:edge_rows + 4 * t + k + 1, :].astype(jnp.float32)
+                      for t in range(3)]
+            rate_scr[0, piece_q, part:part + 1, :] = (pieces[0] + pieces[1]) + pieces[2]
+    slab_real = slab_ref[0, 0]
+    slab_imag = slab_ref[1, 0]
+    left = _weigh(slab_real.astype(jnp.float32), slab_imag.astype(jnp.float32), rate_scr, 0, factor)
+
+    def edge_of(part, block):
+        start = part * 2 * edge + block * edge
+        return bundle_ref[start:start + edge, :]
+
+    far = _nt(left, jnp.concatenate([slab_real, slab_imag, edge_of(0, 1), edge_of(1, 1)], axis=0))
+    own = _nt(held_ref[...], jnp.concatenate([edge_of(0, 0), edge_of(1, 0)], axis=0))
+    joined = []
+    for q in range(2):
+        near_real, near_imag = _adjoint_parts(far, q, rows, 0, rows)
+        far_real, far_imag = _adjoint_parts(far, q, rows, 2 * rows, edge)
+        own_real, own_imag = _adjoint_parts(own, q, rows, 0, edge)
+        joined.append(jnp.concatenate([near_ref[q, 0] + near_real, far_real + own_real], axis=1))
+        joined.append(jnp.concatenate([near_ref[q, 1] + near_imag, far_imag + own_imag], axis=1))
+    joined = jnp.concatenate(joined, axis=0).astype(jnp.bfloat16)
+    count = place_ref.shape[1]
+    col_hit = (lax.broadcasted_iota(jnp.int32, (cols, count), 0) == place_ref[1:2, :]).astype(jnp.bfloat16)
+    row_hit = lax.broadcasted_iota(jnp.int32, (rows, count), 0) == place_ref[0:1, :]
+    by_column = jnp.dot(joined, col_hit, preferred_element_type=jnp.float32)
+    for k in range(4):
+        picked = jnp.where(row_hit, by_column[k * rows:(k + 1) * rows], 0.0)
+        out_ref[k:k + 1, :] = jnp.sum(picked, axis=0, keepdims=True).astype(out_ref.dtype)
+
+
+def element_values(own_slab, bundle, early_rates, pattern_row, edge):
     _, blocks, rows, block_order = own_slab.shape
-    edge = next_edge.shape[2]
     cols = rows + edge
     count = pattern_row.shape[0]
     place = jnp.stack([pattern_row // cols, pattern_row % cols], axis=0)
     factor = 1.0 / math.sqrt(3.0 * block_order)
-    kernel = functools.partial(_weigh_kernel, factor=factor, rows=rows, edge=edge)
-    return pl.pallas_call(
-        kernel,
-        grid=(blocks,),
+    near, held = pl.pallas_call(
+        functools.partial(_early_kernel, factor=factor, rows=rows),
+        grid=(blocks - 1,),
         in_specs=[
             pl.BlockSpec((2, 1, rows, block_order), lambda j: (0, j, 0, 0)),
-            pl.BlockSpec((2, 1, edge, block_order), lambda j: (0, jnp.maximum(j - 1, 0), 0, 0)),
             pl.BlockSpec((1, 2, 2, block_order), lambda j: (j, 0, 0, 0)),
+        ],
+        out_specs=[
+            pl.BlockSpec((2, 2, rows, rows), lambda j: (0, 0, 0, 0)),
+            pl.BlockSpec((4 * rows, block_order), lambda j: (0, 0)),
+        ],
+        out_shape=[
+            jax.ShapeDtypeStruct((2, 2, rows, rows), jnp.float32),
+            jax.ShapeDtypeStruct((4 * rows, block_order), jnp.bfloat16),
+        ],
+    )(own_slab, early_rates)
+    last = blocks - 1
+    return pl.pallas_call(
+        functools.partial(_late_kernel, factor=factor, rows=rows, edge=edge),
+        grid=(1,),
+        in_specs=[
+            pl.BlockSpec((2, 1, rows, block_order), lambda j: (0, last, 0, 0)),
+            pl.BlockSpec(bundle.shape, lambda j: (0, 0)),
+            pl.BlockSpec((2, 2, rows, rows), lambda j: (0, 0, 0, 0)),
+            pl.BlockSpec((4 * rows, block_order), lambda j: (0, 0)),
             pl.BlockSpec((2, count), lambda j: (0, 0)),
         ],
         out_specs=pl.BlockSpec((4, count), lambda j: (0, 0)),
         out_shape=jax.ShapeDtypeStruct((4, count), jnp.bfloat16),
-        scratch_shapes=[pltpu.VMEM((2, 2, rows, cols), jnp.float32)],
-    )(own_slab, next_edge, diag_rates, place)
+        scratch_shapes=[pltpu.VMEM((1, 2, 2, block_order), jnp.float32)],
+    )(own_slab, bundle, near, held, place)
 
 
 def _lag_kernel(in_ref, out_ref, *, width, factor):
@@ -167,11 +216,6 @@
     return jnp.stack([high, middle, low], axis=0).astype(jnp.bfloat16)
 
 
-def join_exact(pieces):
-    pieces = pieces.astype(jnp.float32)
-    return (pieces[0] + pieces[1]) + pieces[2]
-
-
 def body(green_slab, self_energy, pattern, screened):
     own_rate = self_energy[0, 0]
     block_order = own_rate.shape[-1]
@@ -181,11 +225,8 @@
         [edge_block.reshape(-1, block_order), split_exact(own_rate).reshape(-1, block_order)], axis=0
     )
     bundle = passed_along(bundle, "domain", -1)
-    edge_rows = edge_block.size // block_order
-    following = bundle[:edge_rows].reshape(edge_block.shape)
-    next_rate = join_exact(bundle[edge_rows:].reshape(3, *own_rate.shape))
-    nearby = jnp.stack([previous_rate, own_rate, next_rate], axis=0)[None]
-    values = element_values(green_slab[0, 0], following, nearby[0], pattern[0])
+    early_rates = jnp.stack([previous_rate, own_rate], axis=0)
+    values = element_values(green_slab[0, 0], bundle, early_rates, pattern[0], EDGE)
     chunks = lax.axis_size("energy")
     values = values.reshape(4, chunks, -1).transpose(1, 0, 2).reshape(chunks, 1, -1)
     by_element = lax.all_to_all(values, "energy", split_axis=0, concat_axis=0, tiled=True)

time: 76.3 us -> 74.2 us (0.972)
  waiting for transfers between devices: 4.09 us -> 0.01 us
  Pallas kernels: 10.3 us -> 12.4 us
    ppermute x2, waiting for transfers between devices: 4.09 us -> 0.01 us  [passed_along(): return lax.ppermute(x, axis, pairs)]
    pallas_call x1 -> x2, Pallas kernels: 4.87 us -> 6.92 us  [the longest x1 3.51 us: element_values(): pl.pallas_call(functools.partial(_late_kernel, factor=factor, rows=rows,...]
  transfers between devices with their start and end apart: 2 -> 2, of which waited for: 1 -> 0; matrix products, arithmetic and copies ran while one was open for 2% -> 3% of each run, Pallas kernels for 0% -> 5%
where the time goes in v14:
time: 74.2 us; the launch traced here: 73.7 us
  blocking collectives  41.9 us (56%)
  starting transfers between devices  12.5 us (17%)
  Pallas kernels  12.4 us (17%)
  local copies, waits for them, and re-layouts  3.73 us (5%)
  other arithmetic  3.03 us (4%)
    all_to_all x1, blocking collectives, body(): lax.all_to_all(values, 'energy', split_axis=0, concat_axis=0, tiled=True)  27.8 us
    all_to_all x1, blocking collectives, body(): lax.all_to_all(polarization, 'energy', split_axis=0, concat_axis=0, tiled...  14.1 us
    ppermute x2, starting transfers between devices, passed_along(): return lax.ppermute(x, axis, pairs)  12.5 us
    pallas_call x1, Pallas kernels, element_values(): pl.pallas_call(functools.partial(_late_kernel, factor=factor, rows=rows,...  3.51 us
    pallas_call x1, Pallas kernels, element_values(): pl.pallas_call(functools.partial(_early_kernel, factor=factor, rows=rows)...  3.41 us
    pallas_call x1, Pallas kernels, lag_sums(): pl.pallas_call(kernel, out_shape=jax.ShapeDtypeStruct((energy_count, 1, 2...  3.32 us
    pallas_call x1, Pallas kernels, screen(): pl.pallas_call(kernel, out_shape=jax.ShapeDtypeStruct((2, rows, rows), jn...  2.15 us
  transfers between devices with their start and end apart: 2, of which 0 were waited for; matrix products, arithmetic and copies ran while one was open for 3% of the time, Pallas kernels for 5%

profile of v14, /device:TPU:7, one launch (start us, length us, event | category | flops | bytes accessed | tf_op | source)
XLA Modules:
  0.0 73.7 jit_solution(13574480622067100038)
XLA Ops:
  0.0 0.0 copy-start.1
  0.0 0.9 %reduce-precision_convert_fusion.1 = (bf16[1,2,2,2048]{3,2,1,0:T(2,128)(2,1)S(1)}, bf16[1,2,2,2048]{3,2,1,0:T(2,128)(2,1)S(1)}, bf16[1,2,2,2048]{3,2,1,0:T(2,128)(2,1)S(1)}) fusion(f32[1,1,2,2,2048]{4,3,2,1,0:T(2,128)} %param.5), kind=kLoop, calls=%fused_computation.6 | loop fusion | flops 57344 | bytes 81920 | tf_op jit(solution)/shard_map/convert
  0.9 0.1 pad_maximum_fusion.2
  1.0 1.0 %slice.3 = bf16[1,1,2,2,16,2048]{5,4,3,2,1,0:T(8,128)(2,1)S(1)} slice(bf16[1,1,2,3,64,2048]{5,4,3,2,1,0:T(8,128)(2,1)} %param.4), slice={[0:1], [0:1], [0:2], [0:2], [0:16], [0:2048]} | slice | bytes 524288 | tf_op jit(solution)/shard_map/slice | solution.py:223
  2.0 2.5 %collective-permute-start = (bf16[76,2048]{1,0:T(8,128)(2,1)S(1)}, bf16[76,2048]{1,0:T(8,128)(2,1)S(1)}, u32[]{:S(2)}, u32[]{:S(2)}) collective-permute-start(bf16[76,2048]{1,0:T(8,128)(2,1)S(1)} %pad_maximum_fusion), channel_id=1, source_target_pairs={{1,0},{2,1},{3,2},{4,3},{5,4},{6,5},{7,6},{9,8},{10,9},{11,10},{12... | collective-permute-start | bytes 933896 | tf_op jit(solution)/shard_map/ppermute | solution.py:17
  4.5 10.0 %collective-permute-start.1 = (f32[2,2,2048]{2,1,0:T(2,128)}, f32[2,2,2048]{2,1,0:T(2,128)S(1)}, u32[]{:S(2)}, u32[]{:S(2)}) collective-permute-start(f32[2,2,2048]{2,1,0:T(2,128)} %bitcast.20), channel_id=1, source_target_pairs={{0,1},{1,2},{2,3},{3,4},{4,5},{5,6},{6,7},{8,9},{9,10},{10,11},{11... | collective-permute-start | bytes 98312 | tf_op jit(solution)/shard_map/ppermute | solution.py:17
  14.5 0.8 %and_select_fusion.1 = (s32[1,2560]{1,0:T(1,128)S(1)}, s32[1,2560]{1,0:T(1,128)S(1)}) fusion(s32[1,2560]{1,0:T(1,128)} %param.6), kind=kLoop, calls=%fused_computation.8 | loop fusion | flops 30720 | bytes 30720 | tf_op jit(solution)/shard_map/jit(floor_divide)/jit(_where)/select_n | solution.py:104
  15.3 0.6 pad_add_fusion.place_ref
  15.9 0.0 collective-permute-done.1
  15.9 0.0 copy-done.1
  15.9 0.7 pad_maximum_fusion.1.rate_ref
  16.6 3.4 %shard_map.46 = (f32[2,2,64,64]{3,2,1,0:T(8,128)}, bf16[256,2048]{1,0:T(8,128)(2,1)}) custom-call(bf16[2,3,64,2048]{3,2,1,0:T(8,128)(2,1)} %bitcast.15, f32[2,2,2,2048]{3,2,1,0:T(2,128)} %pad_maximum_fusion.1.rate_ref), custom_call_target="tpu_custom_call" | custom-call | tf_op jit(solution)/shard_map/pallas_call | solution.py:106
  20.0 0.0 collective-permute-done.bundle_ref
  20.0 0.0 copy-start
  20.0 0.7 copy-done
  20.7 3.5 %shard_map.47 = bf16[4,2560]{1,0:T(4,128)(2,1)} custom-call(bf16[2,3,64,2048]{3,2,1,0:T(8,128)(2,1)} %bitcast.16, bf16[76,2048]{1,0:T(8,128)(2,1)} %copy-done, f32[2,2,64,64]{3,2,1,0:T(8,128)} %get-tuple-element.7.near_ref, bf16[256,2048]{1,0:T(8,128)(2,1)} %get-tuple-element.8.held_ref, s32[2,2560]{1,0:T(2,128)} %pad_add_fusion.place_ref), custom_call_target="tpu_custom_call" | custom-call | tf_op jit(solution)/shard_map/pallas_call | solution.py:123
  24.2 0.9 %reshape.51 = bf16[4,64,40]{2,1,0:T(8,128)(2,1)S(1)} reshape(bf16[4,2560]{1,0:T(4,128)(2,1)} %shard_map.47) | data formatting | bytes 40960 | tf_op jit(solution)/shard_map/reshape | solution.py:231
  25.1 0.1 copy.7
  25.2 0.1 copy.8
  25.3 27.8 %all_to_all.10.in_ref = bf16[64,1,160]{2,1,0:T(2,128)(2,1)} all-to-all(bf16[64,1,160]{2,1,0:T(2,128)(2,1)S(1)} %copy.8), channel_id=1, replica_groups=mesh['energy'=64,'domain'=8] {'energy'}, dimensions={0} | all-to-all | bytes 40960 | tf_op jit(solution)/shard_map/all_to_all | solution.py:232
  53.1 3.3 %shard_map.48 = bf16[64,1,80]{2,1,0:T(2,128)(2,1)} custom-call(bf16[64,1,160]{2,1,0:T(2,128)(2,1)} %all_to_all.10.in_ref), custom_call_target="tpu_custom_call" | custom-call | tf_op jit(solution)/shard_map/pallas_call | solution.py:158
  56.4 14.1 %all_to_all.11 = bf16[64,1,80]{2,1,0:T(2,128)(2,1)S(1)} all-to-all(bf16[64,1,80]{2,1,0:T(2,128)(2,1)} %shard_map.48), channel_id=1, replica_groups=mesh['energy'=64,'domain'=8] {'energy'}, dimensions={0} | all-to-all | bytes 20480 | tf_op jit(solution)/shard_map/all_to_all | solution.py:234
  70.6 0.1 copy.9
  70.7 0.1 copy.10
  70.8 0.7 reshape.54.polar_ref
  71.5 2.1 %shard_map.49 = f32[2,64,64]{2,1,0:T(8,128)} custom-call(bf16[2,2560]{1,0:T(2,128)(2,1)} %reshape.54.polar_ref, s32[2,2560]{1,0:T(2,128)} %pad_add_fusion.place_ref, bf16[2,64,80]{2,1,0:T(8,128)(2,1)} %bitcast.23), custom_call_target="tpu_custom_call" | custom-call | tf_op jit(solution)/shard_map/pallas_call | solution.py:205
  (2 shorter events, 0.0 us)
Async XLA Ops:
  0.0 15.9 %copy-start.1 = (f32[1,1,2,2,2048]{4,3,2,1,0:T(2,128)S(1)}, f32[1,1,2,2,2048]{4,3,2,1,0:T(2,128)}, u32[]{:S(2)}) copy-start(f32[1,1,2,2,2048]{4,3,2,1,0:T(2,128)} %param.5) | copy-start | bytes 98308
  2.0 18.0 %collective-permute-start = (bf16[76,2048]{1,0:T(8,128)(2,1)S(1)}, bf16[76,2048]{1,0:T(8,128)(2,1)S(1)}, u32[]{:S(2)}, u32[]{:S(2)}) collective-permute-start(bf16[76,2048]{1,0:T(8,128)(2,1)S(1)} %pad_maximum_fusion), channel_id=1, source_target_pairs={{1,0},{2,1},{3,2},{4,3},{5,4},{6,5},{7,6},{9,8},{10,9},{11,10},{12... | collective-permute-start | bytes 933896 | tf_op jit(solution)/shard_map/ppermute | solution.py:17
  4.5 11.4 %collective-permute-start.1 = (f32[2,2,2048]{2,1,0:T(2,128)}, f32[2,2,2048]{2,1,0:T(2,128)S(1)}, u32[]{:S(2)}, u32[]{:S(2)}) collective-permute-start(f32[2,2,2048]{2,1,0:T(2,128)} %bitcast.20), channel_id=1, source_target_pairs={{0,1},{1,2},{2,3},{3,4},{4,5},{5,6},{6,7},{8,9},{9,10},{10,11},{11... | collective-permute-start | bytes 98312 | tf_op jit(solution)/shard_map/ppermute | solution.py:17
  20.0 0.7 copy-start

commit v15 on v14

--- a/solution.py
+++ b/solution.py
@@ -35,20 +35,35 @@
     return real, imag
 
 
+def _place_hits(pattern_ref, rows, cols):
+    count = pattern_ref.shape[1]
+    position = pattern_ref[...].astype(jnp.float32)
+    row = jnp.floor((position + 0.5) * (1.0 / cols))
+    col = position - row * cols
+    row_hit = lax.broadcasted_iota(jnp.int32, (rows, count), 0).astype(jnp.float32) == row
+    col_hit = lax.broadcasted_iota(jnp.int32, (cols, count), 0).astype(jnp.float32) == col
+    return row_hit, col_hit
+
+
 def _nt(a, b):
     return lax.dot_general(a, b, (((1,), (1,)), ((), ())), preferred_element_type=jnp.float32)
 
 
-def _early_kernel(slab_ref, rate_ref, near_ref, held_ref, *, factor, rows):
+def _early_kernel(slab_ref, previous_ref, own_ref, near_ref, held_ref, rate_scr, *, factor, rows):
     step = pl.program_id(0)
 
     @pl.when(step == 0)
     def _():
         near_ref[...] = jnp.zeros_like(near_ref)
+        rate_scr[0] = previous_ref[...]
+
+    @pl.when(step > 0)
+    def _():
+        rate_scr[0] = own_ref[...]
 
     slab_real = slab_ref[0, 0]
     slab_imag = slab_ref[1, 0]
-    left = _weigh(slab_real.astype(jnp.float32), slab_imag.astype(jnp.float32), rate_ref, 0, factor)
+    left = _weigh(slab_real.astype(jnp.float32), slab_imag.astype(jnp.float32), rate_scr, 0, factor)
     prod = _nt(left, jnp.concatenate([slab_real, slab_imag], axis=0))
     for q in range(2):
         real, imag = _adjoint_parts(prod, q, rows, 0, rows)
@@ -88,37 +103,35 @@
         joined.append(jnp.concatenate([near_ref[q, 0] + near_real, far_real + own_real], axis=1))
         joined.append(jnp.concatenate([near_ref[q, 1] + near_imag, far_imag + own_imag], axis=1))
     joined = jnp.concatenate(joined, axis=0).astype(jnp.bfloat16)
-    count = place_ref.shape[1]
-    col_hit = (lax.broadcasted_iota(jnp.int32, (cols, count), 0) == place_ref[1:2, :]).astype(jnp.bfloat16)
-    row_hit = lax.broadcasted_iota(jnp.int32, (rows, count), 0) == place_ref[0:1, :]
-    by_column = jnp.dot(joined, col_hit, preferred_element_type=jnp.float32)
+    row_hit, col_hit = _place_hits(place_ref, rows, cols)
+    by_column = jnp.dot(joined, col_hit.astype(jnp.bfloat16), preferred_element_type=jnp.float32)
     for k in range(4):
         picked = jnp.where(row_hit, by_column[k * rows:(k + 1) * rows], 0.0)
         out_ref[k:k + 1, :] = jnp.sum(picked, axis=0, keepdims=True).astype(out_ref.dtype)
 
 
-def element_values(own_slab, bundle, early_rates, pattern_row, edge):
+def element_values(own_slab, bundle, previous_rate, own_rate, pattern_row, edge):
     _, blocks, rows, block_order = own_slab.shape
-    cols = rows + edge
-    count = pattern_row.shape[0]
-    place = jnp.stack([pattern_row // cols, pattern_row % cols], axis=0)
+    count = pattern_row.shape[1]
     factor = 1.0 / math.sqrt(3.0 * block_order)
     near, held = pl.pallas_call(
         functools.partial(_early_kernel, factor=factor, rows=rows),
         grid=(blocks - 1,),
         in_specs=[
             pl.BlockSpec((2, 1, rows, block_order), lambda j: (0, j, 0, 0)),
-            pl.BlockSpec((1, 2, 2, block_order), lambda j: (j, 0, 0, 0)),
+            pl.BlockSpec((2, 2, block_order), lambda j: (0, 0, 0)),
+            pl.BlockSpec((2, 2, block_order), lambda j: (0, 0, 0)),
         ],
         out_specs=[
             pl.BlockSpec((2, 2, rows, rows), lambda j: (0, 0, 0, 0)),
             pl.BlockSpec((4 * rows, block_order), lambda j: (0, 0)),
         ],
+        scratch_shapes=[pltpu.VMEM((1, 2, 2, block_order), jnp.float32)],
         out_shape=[
             jax.ShapeDtypeStruct((2, 2, rows, rows), jnp.float32),
             jax.ShapeDtypeStruct((4 * rows, block_order), jnp.bfloat16),
         ],
-    )(own_slab, early_rates)
+    )(own_slab, previous_rate, own_rate)
     last = blocks - 1
     return pl.pallas_call(
         functools.partial(_late_kernel, factor=factor, rows=rows, edge=edge),
@@ -128,12 +141,12 @@
             pl.BlockSpec(bundle.shape, lambda j: (0, 0)),
             pl.BlockSpec((2, 2, rows, rows), lambda j: (0, 0, 0, 0)),
             pl.BlockSpec((4 * rows, block_order), lambda j: (0, 0)),
-            pl.BlockSpec((2, count), lambda j: (0, 0)),
+            pl.BlockSpec((1, count), lambda j: (0, 0)),
         ],
         out_specs=pl.BlockSpec((4, count), lambda j: (0, 0)),
         out_shape=jax.ShapeDtypeStruct((4, count), jnp.bfloat16),
         scratch_shapes=[pltpu.VMEM((1, 2, 2, block_order), jnp.float32)],
-    )(own_slab, bundle, near, held, place)
+    )(own_slab, bundle, near, held, pattern_row)
 
 
 def _lag_kernel(in_ref, out_ref, *, width, factor):
@@ -168,9 +181,8 @@
     def nn(a, b):
         return jnp.dot(a, b, preferred_element_type=jnp.float32)
 
-    count = place_ref.shape[1]
-    row_hit = lax.broadcasted_iota(jnp.int32, (rows, count), 0) == place_ref[0:1, :]
-    col_hit = (lax.broadcasted_iota(jnp.int32, (cols, count), 0) == place_ref[1:2, :]).astype(jnp.bfloat16)
+    row_hit, col_hit = _place_hits(place_ref, rows, cols)
+    col_hit = col_hit.astype(jnp.bfloat16)
     polar = polar_ref[...].astype(jnp.float32)
     dense = []
     for part in range(2):
@@ -200,12 +212,11 @@
 def screen(polar_row, pattern_row, screen_block):
     rows = screen_block.shape[1]
     cols = screen_block.shape[2]
-    place = jnp.stack([pattern_row // cols, pattern_row % cols], axis=0)
     kernel = functools.partial(_screen_kernel, rows=rows, cols=cols)
     return pl.pallas_call(
         kernel,
         out_shape=jax.ShapeDtypeStruct((2, rows, rows), jnp.float32),
-    )(polar_row, place, screen_block)
+    )(polar_row, pattern_row, screen_block)
 
 
 def split_exact(value):
@@ -225,15 +236,14 @@
         [edge_block.reshape(-1, block_order), split_exact(own_rate).reshape(-1, block_order)], axis=0
     )
     bundle = passed_along(bundle, "domain", -1)
-    early_rates = jnp.stack([previous_rate, own_rate], axis=0)
-    values = element_values(green_slab[0, 0], bundle, early_rates, pattern[0], EDGE)
+    values = element_values(green_slab[0, 0], bundle, previous_rate, own_rate, pattern, EDGE)
     chunks = lax.axis_size("energy")
     values = values.reshape(4, chunks, -1).transpose(1, 0, 2).reshape(chunks, 1, -1)
     by_element = lax.all_to_all(values, "energy", split_axis=0, concat_axis=0, tiled=True)
     polarization = lag_sums(by_element)
     per_energy = lax.all_to_all(polarization, "energy", split_axis=0, concat_axis=0, tiled=True)
     per_energy = per_energy.reshape(chunks, 2, -1).transpose(1, 0, 2).reshape(2, -1)
-    result = screen(per_energy, pattern[0], screened[0, 0])
+    result = screen(per_energy, pattern, screened[0, 0])
     return result[None, None]
 
 

time: 74.2 us -> 74 us (level)
  other arithmetic: 3.03 us -> 0.9 us
  waiting for transfers between devices: 0.01 us -> 1.36 us
    ppermute x2, waiting for transfers between devices: 0.01 us -> 1.36 us  [passed_along(): return lax.ppermute(x, axis, pairs)]
    another operation x3 -> x1, other arithmetic: 2.14 us -> 0.79 us
    select_n x1 -> x0, other arithmetic: 0.79 us -> none  [element_values(): place = jnp.stack([pattern_row // cols, pattern_row % cols], axis=0)]
  transfers between devices with their start and end apart: 2 -> 2, of which waited for: 0 -> 1; matrix products, arithmetic and copies ran while one was open for 3% -> 0% of each run, Pallas kernels for 5% -> 5%
where the time goes in v15:
time: 74 us; the launch traced here: 73.5 us
  blocking collectives  41.9 us (57%)
  starting transfers between devices  12.5 us (17%)
  Pallas kernels  12.5 us (17%)
  local copies, waits for them, and re-layouts  4.33 us (6%)
  waiting for transfers between devices  1.36 us (2%)
  other arithmetic  0.9 us (1%)
    all_to_all x1, blocking collectives, body(): lax.all_to_all(values, 'energy', split_axis=0, concat_axis=0, tiled=True)  27.8 us
    all_to_all x1, blocking collectives, body(): lax.all_to_all(polarization, 'energy', split_axis=0, concat_axis=0, tiled...  14.1 us
    ppermute x2, starting transfers between devices, passed_along(): return lax.ppermute(x, axis, pairs)  12.5 us
    pallas_call x1, Pallas kernels, element_values(): pl.pallas_call(functools.partial(_early_kernel, factor=factor, rows=rows)...  3.52 us
    pallas_call x1, Pallas kernels, element_values(): pl.pallas_call(functools.partial(_late_kernel, factor=factor, rows=rows,...  3.48 us
    pallas_call x1, Pallas kernels, lag_sums(): pl.pallas_call(kernel, out_shape=jax.ShapeDtypeStruct((energy_count, 1, 2...  3.32 us
    pallas_call x1, Pallas kernels, screen(): pl.pallas_call(kernel, out_shape=jax.ShapeDtypeStruct((2, rows, rows), jn...  2.17 us
  transfers between devices with their start and end apart: 2, of which 1 were waited for; matrix products, arithmetic and copies ran while one was open for 0% of the time, Pallas kernels for 5%

profile of v15, /device:TPU:7, one launch (start us, length us, event | category | flops | bytes accessed | tf_op | source)
XLA Modules:
  0.0 73.5 jit_solution(13002381311158357358)
XLA Ops:
  0.0 0.8 %reduce-precision_convert_fusion.1 = (bf16[1,2,2,2048]{3,2,1,0:T(2,128)(2,1)S(1)}, bf16[1,2,2,2048]{3,2,1,0:T(2,128)(2,1)S(1)}, bf16[1,2,2,2048]{3,2,1,0:T(2,128)(2,1)S(1)}) fusion(f32[1,1,2,2,2048]{4,3,2,1,0:T(2,128)} %param.5), kind=kLoop, calls=%fused_computation.5 | loop fusion | flops 57344 | bytes 81920 | tf_op jit(solution)/shard_map/convert
  0.8 0.1 pad_maximum_fusion.1
  0.9 1.0 %slice.3 = bf16[1,1,2,2,16,2048]{5,4,3,2,1,0:T(8,128)(2,1)S(1)} slice(bf16[1,1,2,3,64,2048]{5,4,3,2,1,0:T(8,128)(2,1)} %param.4), slice={[0:1], [0:1], [0:2], [0:2], [0:16], [0:2048]} | slice | bytes 524288 | tf_op jit(solution)/shard_map/slice | solution.py:234
  1.9 2.5 %collective-permute-start = (bf16[76,2048]{1,0:T(8,128)(2,1)S(1)}, bf16[76,2048]{1,0:T(8,128)(2,1)S(1)}, u32[]{:S(2)}, u32[]{:S(2)}) collective-permute-start(bf16[76,2048]{1,0:T(8,128)(2,1)S(1)} %pad_maximum_fusion), channel_id=1, source_target_pairs={{1,0},{2,1},{3,2},{4,3},{5,4},{6,5},{7,6},{9,8},{10,9},{11,10},{12... | collective-permute-start | bytes 933896 | tf_op jit(solution)/shard_map/ppermute | solution.py:17
  4.4 10.0 %collective-permute-start.1 = (f32[2,2,2048]{2,1,0:T(2,128)}, f32[2,2,2048]{2,1,0:T(2,128)S(1)}, u32[]{:S(2)}, u32[]{:S(2)}) collective-permute-start(f32[2,2,2048]{2,1,0:T(2,128)} %bitcast.22), channel_id=1, source_target_pairs={{0,1},{1,2},{2,3},{3,4},{4,5},{5,6},{6,7},{8,9},{9,10},{10,11},{11... | collective-permute-start | bytes 98312 | tf_op jit(solution)/shard_map/ppermute | solution.py:17
  14.4 1.3 %collective-permute-done.1.previous_ref = f32[2,2,2048]{2,1,0:T(2,128)S(1)} collective-permute-done((f32[2,2,2048]{2,1,0:T(2,128)}, f32[2,2,2048]{2,1,0:T(2,128)S(1)}, u32[]{:S(2)}, u32[]{:S(2)}) %collective-permute-start.1) | collective-permute-done | bytes 32800 | tf_op jit(solution)/shard_map/ppermute | solution.py:17
  15.7 0.0 copy-start.1
  15.7 0.6 copy-done.1
  16.3 3.5 %shard_map.46 = (f32[2,2,64,64]{3,2,1,0:T(8,128)}, bf16[256,2048]{1,0:T(8,128)(2,1)}) custom-call(bf16[2,3,64,2048]{3,2,1,0:T(8,128)(2,1)} %bitcast.17, f32[2,2,2048]{2,1,0:T(2,128)} %copy-done.1, f32[2,2,2048]{2,1,0:T(2,128)} %bitcast.23), custom_call_target="tpu_custom_call" | custom-call | tf_op jit(solution)/shard_map/pallas_call | solution.py:117
  19.9 0.0 collective-permute-done.bundle_ref
  19.9 0.0 copy-start
  19.9 0.7 copy-done
  20.6 3.5 %shard_map.47 = bf16[4,2560]{1,0:T(4,128)(2,1)} custom-call(bf16[2,3,64,2048]{3,2,1,0:T(8,128)(2,1)} %bitcast.18, bf16[76,2048]{1,0:T(8,128)(2,1)} %copy-done, f32[2,2,64,64]{3,2,1,0:T(8,128)} %get-tuple-element.7.near_ref, bf16[256,2048]{1,0:T(8,128)(2,1)} %get-tuple-element.8.held_ref, s32[1,2560]{1,0:T(1,128)} %place_ref.3), custom_call_target="tpu_custom_call" | custom-call | tf_op jit(solution)/shard_map/pallas_call | solution.py:136
  24.1 0.9 %reshape.51 = bf16[4,64,40]{2,1,0:T(8,128)(2,1)S(1)} reshape(bf16[4,2560]{1,0:T(4,128)(2,1)} %shard_map.47) | data formatting | bytes 40960 | tf_op jit(solution)/shard_map/reshape | solution.py:241
  25.0 0.1 copy.7
  25.1 0.1 copy.8
  25.2 27.8 %all_to_all.10.in_ref = bf16[64,1,160]{2,1,0:T(2,128)(2,1)} all-to-all(bf16[64,1,160]{2,1,0:T(2,128)(2,1)S(1)} %copy.8), channel_id=1, replica_groups=mesh['energy'=64,'domain'=8] {'energy'}, dimensions={0} | all-to-all | bytes 40960 | tf_op jit(solution)/shard_map/all_to_all | solution.py:242
  53.0 3.3 %shard_map.48 = bf16[64,1,80]{2,1,0:T(2,128)(2,1)} custom-call(bf16[64,1,160]{2,1,0:T(2,128)(2,1)} %all_to_all.10.in_ref), custom_call_target="tpu_custom_call" | custom-call | tf_op jit(solution)/shard_map/pallas_call | solution.py:171
  56.3 14.1 %all_to_all.11 = bf16[64,1,80]{2,1,0:T(2,128)(2,1)S(1)} all-to-all(bf16[64,1,80]{2,1,0:T(2,128)(2,1)} %shard_map.48), channel_id=1, replica_groups=mesh['energy'=64,'domain'=8] {'energy'}, dimensions={0} | all-to-all | bytes 20480 | tf_op jit(solution)/shard_map/all_to_all | solution.py:244
  70.4 0.1 copy.9
  70.5 0.1 copy.10
  70.6 0.7 reshape.54.polar_ref
  71.3 2.2 %shard_map.49 = f32[2,64,64]{2,1,0:T(8,128)} custom-call(bf16[2,2560]{1,0:T(2,128)(2,1)} %reshape.54.polar_ref, s32[1,2560]{1,0:T(1,128)} %place_ref.3, bf16[2,64,80]{2,1,0:T(8,128)(2,1)} %bitcast.25), custom_call_target="tpu_custom_call" | custom-call | tf_op jit(solution)/shard_map/pallas_call | solution.py:216
  (2 shorter events, 0.1 us)
Async XLA Ops:
  1.9 18.0 %collective-permute-start = (bf16[76,2048]{1,0:T(8,128)(2,1)S(1)}, bf16[76,2048]{1,0:T(8,128)(2,1)S(1)}, u32[]{:S(2)}, u32[]{:S(2)}) collective-permute-start(bf16[76,2048]{1,0:T(8,128)(2,1)S(1)} %pad_maximum_fusion), channel_id=1, source_target_pairs={{1,0},{2,1},{3,2},{4,3},{5,4},{6,5},{7,6},{9,8},{10,9},{11,10},{12... | collective-permute-start | bytes 933896 | tf_op jit(solution)/shard_map/ppermute | solution.py:17
  4.4 11.3 %collective-permute-start.1 = (f32[2,2,2048]{2,1,0:T(2,128)}, f32[2,2,2048]{2,1,0:T(2,128)S(1)}, u32[]{:S(2)}, u32[]{:S(2)}) collective-permute-start(f32[2,2,2048]{2,1,0:T(2,128)} %bitcast.22), channel_id=1, source_target_pairs={{0,1},{1,2},{2,3},{3,4},{4,5},{5,6},{6,7},{8,9},{9,10},{10,11},{11... | collective-permute-start | bytes 98312 | tf_op jit(solution)/shard_map/ppermute | solution.py:17
  15.7 0.6 copy-start.1
  19.9 0.7 copy-start

commit v16 on v15

--- a/solution.py
+++ b/solution.py
@@ -219,22 +219,40 @@
     )(polar_row, pattern_row, screen_block)
 
 
-def split_exact(value):
-    high = lax.reduce_precision(value, exponent_bits=8, mantissa_bits=7)
-    rest = value - high
-    middle = lax.reduce_precision(rest, exponent_bits=8, mantissa_bits=7)
-    low = rest - middle
-    return jnp.stack([high, middle, low], axis=0).astype(jnp.bfloat16)
+def _bundle_kernel(slab_ref, rate_ref, out_ref, *, edge):
+    for part in range(2):
+        for block in range(2):
+            start = (part * 2 + block) * edge
+            out_ref[start:start + edge, :] = slab_ref[part, block]
+    for q in range(2):
+        value = rate_ref[q]
+        high = value.astype(jnp.bfloat16)
+        rest = value - high.astype(jnp.float32)
+        middle = rest.astype(jnp.bfloat16)
+        low = (rest - middle.astype(jnp.float32)).astype(jnp.bfloat16)
+        for t, piece in enumerate((high, middle, low)):
+            start = 4 * edge + 4 * t + 2 * q
+            out_ref[start:start + 2, :] = piece
+
+
+def make_bundle(own_slab, own_rate, edge):
+    _, _, rows, block_order = own_slab.shape
+    return pl.pallas_call(
+        functools.partial(_bundle_kernel, edge=edge),
+        grid=(1,),
+        in_specs=[
+            pl.BlockSpec((2, 2, edge, block_order), lambda j: (0, 0, 0, 0)),
+            pl.BlockSpec(own_rate.shape, lambda j: (0, 0, 0)),
+        ],
+        out_specs=pl.BlockSpec((4 * edge + 12, block_order), lambda j: (0, 0)),
+        out_shape=jax.ShapeDtypeStruct((4 * edge + 12, block_order), jnp.bfloat16),
+    )(own_slab, own_rate)
 
 
 def body(green_slab, self_energy, pattern, screened):
     own_rate = self_energy[0, 0]
-    block_order = own_rate.shape[-1]
     previous_rate = passed_along(own_rate, "domain", 1)
-    edge_block = green_slab[0, 0, :, 0:2, :EDGE, :]
-    bundle = jnp.concatenate(
-        [edge_block.reshape(-1, block_order), split_exact(own_rate).reshape(-1, block_order)], axis=0
-    )
+    bundle = make_bundle(green_slab[0, 0], own_rate, EDGE)
     bundle = passed_along(bundle, "domain", -1)
     values = element_values(green_slab[0, 0], bundle, previous_rate, own_rate, pattern, EDGE)
     chunks = lax.axis_size("energy")

time: 74 us -> 74 us (level)
  Pallas kernels: 12.5 us -> 14.2 us
  local copies, waits for them, and re-layouts: 4.33 us -> 3.33 us
  other arithmetic: 0.9 us -> 0 us
    pallas_call x0 -> x1, Pallas kernels: none -> 1.77 us  [make_bundle(): pl.pallas_call(functools.partial(_bundle_kernel, edge=edge), grid=(1,), i...]
    slice x1 -> x0, local copies, waits for them, and re-layouts: 0.97 us -> none  [body(): edge_block = green_slab[0, 0, :, 0:2, :EDGE, :]]
    another operation x2 -> x0, other arithmetic: 0.87 us -> none
  transfers between devices with their start and end apart: 2 -> 2, of which waited for: 1 -> 2; matrix products, arithmetic and copies ran while one was open for 0% -> 0% of each run, Pallas kernels for 5% -> 5%
where the time goes in v16:
time: 74 us; the launch traced here: 73.6 us
  blocking collectives  41.9 us (57%)
  Pallas kernels  14.2 us (19%)
  starting transfers between devices  12.5 us (17%)
  local copies, waits for them, and re-layouts  3.33 us (4%)
  waiting for transfers between devices  1.56 us (2%)
    all_to_all x1, blocking collectives, body(): lax.all_to_all(values, 'energy', split_axis=0, concat_axis=0, tiled=True)  27.8 us
    all_to_all x1, blocking collectives, body(): lax.all_to_all(polarization, 'energy', split_axis=0, concat_axis=0, tiled...  14.1 us
    ppermute x2, starting transfers between devices, passed_along(): return lax.ppermute(x, axis, pairs)  12.5 us
    pallas_call x1, Pallas kernels, element_values(): pl.pallas_call(functools.partial(_early_kernel, factor=factor, rows=rows)...  3.52 us
    pallas_call x1, Pallas kernels, element_values(): pl.pallas_call(functools.partial(_late_kernel, factor=factor, rows=rows,...  3.47 us
    pallas_call x1, Pallas kernels, lag_sums(): pl.pallas_call(kernel, out_shape=jax.ShapeDtypeStruct((energy_count, 1, 2...  3.32 us
    pallas_call x1, Pallas kernels, screen(): pl.pallas_call(kernel, out_shape=jax.ShapeDtypeStruct((2, rows, rows), jn...  2.15 us
    pallas_call x1, Pallas kernels, make_bundle(): pl.pallas_call(functools.partial(_bundle_kernel, edge=edge), grid=(1,), i...  1.77 us
  transfers between devices with their start and end apart: 2, of which 2 were waited for; matrix products, arithmetic and copies ran while one was open for 0% of the time, Pallas kernels for 5%

profile of v16, /device:TPU:7, one launch (start us, length us, event | category | flops | bytes accessed | tf_op | source)
XLA Modules:
  0.0 73.6 jit_solution(6361385168062472512)
XLA Ops:
  0.0 0.0 copy-start.1
  0.0 1.8 %shard_map.46 = bf16[76,2048]{1,0:T(8,128)(2,1)} custom-call(bf16[2,3,64,2048]{3,2,1,0:T(8,128)(2,1)} %bitcast.9, f32[2,2,2048]{2,1,0:T(2,128)} %bitcast.14), custom_call_target="tpu_custom_call" | custom-call | tf_op jit(solution)/shard_map/pallas_call | solution.py:240
  1.8 2.4 %collective-permute-start = (bf16[76,2048]{1,0:T(8,128)(2,1)}, bf16[76,2048]{1,0:T(8,128)(2,1)S(1)}, u32[]{:S(2)}, u32[]{:S(2)}) collective-permute-start(bf16[76,2048]{1,0:T(8,128)(2,1)} %shard_map.46), channel_id=1, source_target_pairs={{1,0},{2,1},{3,2},{4,3},{5,4},{6,5},{7,6},{9,8},{10,9},{11,10},{12... | collective-permute-start | bytes 933896 | tf_op jit(solution)/shard_map/ppermute | solution.py:17
  4.2 0.0 copy-done.1
  4.2 10.0 %collective-permute-start.1 = (f32[2,2,2048]{2,1,0:T(2,128)S(1)}, f32[2,2,2048]{2,1,0:T(2,128)S(1)}, u32[]{:S(2)}, u32[]{:S(2)}) collective-permute-start(f32[2,2,2048]{2,1,0:T(2,128)S(1)} %bitcast.16), channel_id=1, source_target_pairs={{0,1},{1,2},{2,3},{3,4},{4,5},{5,6},{6,7},{8,9},{9,10},{10,11},{11... | collective-permute-start | bytes 98312 | tf_op jit(solution)/shard_map/ppermute | solution.py:17
  14.3 1.0 %collective-permute-done.1.previous_ref = f32[2,2,2048]{2,1,0:T(2,128)S(1)} collective-permute-done((f32[2,2,2048]{2,1,0:T(2,128)S(1)}, f32[2,2,2048]{2,1,0:T(2,128)S(1)}, u32[]{:S(2)}, u32[]{:S(2)}) %collective-permute-start.1) | collective-permute-done | bytes 32800 | tf_op jit(solution)/shard_map/ppermute | solution.py:17
  15.3 0.0 copy-start.2
  15.3 0.6 copy-done.2
  15.9 3.5 %shard_map.47 = (f32[2,2,64,64]{3,2,1,0:T(8,128)}, bf16[256,2048]{1,0:T(8,128)(2,1)}) custom-call(bf16[2,3,64,2048]{3,2,1,0:T(8,128)(2,1)} %bitcast.10, f32[2,2,2048]{2,1,0:T(2,128)} %copy-done.2, f32[2,2,2048]{2,1,0:T(2,128)} %bitcast.15), custom_call_target="tpu_custom_call" | custom-call | tf_op jit(solution)/shard_map/pallas_call | solution.py:117
  19.4 0.6 collective-permute-done.bundle_ref
  19.9 0.0 copy-start
  19.9 0.7 copy-done
  20.7 3.5 %shard_map.48 = bf16[4,2560]{1,0:T(4,128)(2,1)} custom-call(bf16[2,3,64,2048]{3,2,1,0:T(8,128)(2,1)} %bitcast.11, bf16[76,2048]{1,0:T(8,128)(2,1)} %copy-done, f32[2,2,64,64]{3,2,1,0:T(8,128)} %get-tuple-element.7.near_ref, bf16[256,2048]{1,0:T(8,128)(2,1)} %get-tuple-element.8.held_ref, s32[1,2560]{1,0:T(1,128)} %place_ref.3), custom_call_target="tpu_custom_call" | custom-call | tf_op jit(solution)/shard_map/pallas_call | solution.py:136
  24.1 0.9 %reshape.12 = bf16[4,64,40]{2,1,0:T(8,128)(2,1)S(1)} reshape(bf16[4,2560]{1,0:T(4,128)(2,1)} %shard_map.48) | data formatting | bytes 40960 | tf_op jit(solution)/shard_map/reshape | solution.py:259
  25.0 0.1 copy.7
  25.1 0.1 copy.8
  25.2 27.8 %all_to_all.10.in_ref = bf16[64,1,160]{2,1,0:T(2,128)(2,1)} all-to-all(bf16[64,1,160]{2,1,0:T(2,128)(2,1)S(1)} %copy.8), channel_id=1, replica_groups=mesh['energy'=64,'domain'=8] {'energy'}, dimensions={0} | all-to-all | bytes 40960 | tf_op jit(solution)/shard_map/all_to_all | solution.py:260
  53.0 3.3 %shard_map.49 = bf16[64,1,80]{2,1,0:T(2,128)(2,1)} custom-call(bf16[64,1,160]{2,1,0:T(2,128)(2,1)} %all_to_all.10.in_ref), custom_call_target="tpu_custom_call" | custom-call | tf_op jit(solution)/shard_map/pallas_call | solution.py:171
  56.3 14.1 %all_to_all.11 = bf16[64,1,80]{2,1,0:T(2,128)(2,1)S(1)} all-to-all(bf16[64,1,80]{2,1,0:T(2,128)(2,1)} %shard_map.49), channel_id=1, replica_groups=mesh['energy'=64,'domain'=8] {'energy'}, dimensions={0} | all-to-all | bytes 20480 | tf_op jit(solution)/shard_map/all_to_all | solution.py:262
  70.5 0.1 copy.9
  70.6 0.1 copy.10
  70.7 0.7 reshape.15.polar_ref
  71.4 2.2 %shard_map.50 = f32[2,64,64]{2,1,0:T(8,128)} custom-call(bf16[2,2560]{1,0:T(2,128)(2,1)} %reshape.15.polar_ref, s32[1,2560]{1,0:T(1,128)} %place_ref.3, bf16[2,64,80]{2,1,0:T(8,128)(2,1)} %bitcast.18), custom_call_target="tpu_custom_call" | custom-call | tf_op jit(solution)/shard_map/pallas_call | solution.py:216
Async XLA Ops:
  0.0 4.2 %copy-start.1 = (f32[1,1,2,2,2048]{4,3,2,1,0:T(2,128)S(1)}, f32[1,1,2,2,2048]{4,3,2,1,0:T(2,128)}, u32[]{:S(2)}) copy-start(f32[1,1,2,2,2048]{4,3,2,1,0:T(2,128)} %param.5) | copy-start | bytes 98308
  1.8 18.2 %collective-permute-start = (bf16[76,2048]{1,0:T(8,128)(2,1)}, bf16[76,2048]{1,0:T(8,128)(2,1)S(1)}, u32[]{:S(2)}, u32[]{:S(2)}) collective-permute-start(bf16[76,2048]{1,0:T(8,128)(2,1)} %shard_map.46), channel_id=1, source_target_pairs={{1,0},{2,1},{3,2},{4,3},{5,4},{6,5},{7,6},{9,8},{10,9},{11,10},{12... | collective-permute-start | bytes 933896 | tf_op jit(solution)/shard_map/ppermute | solution.py:17
  4.2 11.0 %collective-permute-start.1 = (f32[2,2,2048]{2,1,0:T(2,128)S(1)}, f32[2,2,2048]{2,1,0:T(2,128)S(1)}, u32[]{:S(2)}, u32[]{:S(2)}) collective-permute-start(f32[2,2,2048]{2,1,0:T(2,128)S(1)} %bitcast.16), channel_id=1, source_target_pairs={{0,1},{1,2},{2,3},{3,4},{4,5},{5,6},{6,7},{8,9},{9,10},{10,11},{11... | collective-permute-start | bytes 98312 | tf_op jit(solution)/shard_map/ppermute | solution.py:17
  15.3 0.6 copy-start.2
  19.9 0.7 copy-start

commit v17 on v15

--- a/solution.py
+++ b/solution.py
@@ -155,13 +155,17 @@
     lesser = values[:, 0:2 * width]
     greater = values[:, 2 * width:4 * width]
     swapped = jnp.concatenate([greater[:, width:], greater[:, :width]], axis=1)
-    rows = []
-    for lag in range(energy_count):
-        head = lesser[lag:]
-        straight = jnp.sum(head * greater[:energy_count - lag], axis=0, keepdims=True)
-        crossed = jnp.sum(head * swapped[:energy_count - lag], axis=0, keepdims=True)
-        rows.append(jnp.concatenate([straight[:, :width] - straight[:, width:], crossed[:, :width] + crossed[:, width:]], axis=1))
-    out_ref[:, 0, :] = (jnp.concatenate(rows, axis=0) * factor).astype(out_ref.dtype)
+    padded = jnp.concatenate([lesser, jnp.zeros_like(lesser)], axis=0)
+    straight = jnp.zeros_like(lesser)
+    crossed = jnp.zeros_like(lesser)
+    for k in range(energy_count):
+        window = padded[k:k + energy_count]
+        straight = straight + window * greater[k:k + 1]
+        crossed = crossed + window * swapped[k:k + 1]
+    joined = jnp.concatenate(
+        [straight[:, :width] - straight[:, width:], crossed[:, :width] + crossed[:, width:]], axis=1
+    )
+    out_ref[:, 0, :] = (joined * factor).astype(out_ref.dtype)
 
 
 def lag_sums(by_element):

time: 74 us -> 72.8 us (0.984)
  Pallas kernels: 12.5 us -> 11.2 us
    pallas_call x1, Pallas kernels: 3.32 us -> 2.08 us  [lag_sums(): pl.pallas_call(kernel, out_shape=jax.ShapeDtypeStruct((energy_count, 1, 2...]
where the time goes in v17:
time: 72.8 us; the launch traced here: 72.3 us
  blocking collectives  41.9 us (58%)
  starting transfers between devices  12.5 us (17%)
  Pallas kernels  11.2 us (15%)
  local copies, waits for them, and re-layouts  4.33 us (6%)
  waiting for transfers between devices  1.36 us (2%)
  other arithmetic  0.9 us (1%)
    all_to_all x1, blocking collectives, body(): lax.all_to_all(values, 'energy', split_axis=0, concat_axis=0, tiled=True)  27.8 us
    all_to_all x1, blocking collectives, body(): lax.all_to_all(polarization, 'energy', split_axis=0, concat_axis=0, tiled...  14.1 us
    ppermute x2, starting transfers between devices, passed_along(): return lax.ppermute(x, axis, pairs)  12.5 us
    pallas_call x1, Pallas kernels, element_values(): pl.pallas_call(functools.partial(_early_kernel, factor=factor, rows=rows)...  3.52 us
    pallas_call x1, Pallas kernels, element_values(): pl.pallas_call(functools.partial(_late_kernel, factor=factor, rows=rows,...  3.48 us
    pallas_call x1, Pallas kernels, screen(): pl.pallas_call(kernel, out_shape=jax.ShapeDtypeStruct((2, rows, rows), jn...  2.16 us
    pallas_call x1, Pallas kernels, lag_sums(): pl.pallas_call(kernel, out_shape=jax.ShapeDtypeStruct((energy_count, 1, 2...  2.08 us
  transfers between devices with their start and end apart: 2, of which 1 were waited for; matrix products, arithmetic and copies ran while one was open for 0% of the time, Pallas kernels for 5%

profile of v17, /device:TPU:7, one launch (start us, length us, event | category | flops | bytes accessed | tf_op | source)
XLA Modules:
  0.0 72.3 jit_solution(15346889248038721782)
XLA Ops:
  0.0 0.8 %reduce-precision_convert_fusion.1 = (bf16[1,2,2,2048]{3,2,1,0:T(2,128)(2,1)S(1)}, bf16[1,2,2,2048]{3,2,1,0:T(2,128)(2,1)S(1)}, bf16[1,2,2,2048]{3,2,1,0:T(2,128)(2,1)S(1)}) fusion(f32[1,1,2,2,2048]{4,3,2,1,0:T(2,128)} %param.5), kind=kLoop, calls=%fused_computation.5 | loop fusion | flops 57344 | bytes 81920 | tf_op jit(solution)/shard_map/convert
  0.8 0.1 pad_maximum_fusion.1
  0.9 1.0 %slice.3 = bf16[1,1,2,2,16,2048]{5,4,3,2,1,0:T(8,128)(2,1)S(1)} slice(bf16[1,1,2,3,64,2048]{5,4,3,2,1,0:T(8,128)(2,1)} %param.4), slice={[0:1], [0:1], [0:2], [0:2], [0:16], [0:2048]} | slice | bytes 524288 | tf_op jit(solution)/shard_map/slice | solution.py:238
  1.9 2.5 %collective-permute-start = (bf16[76,2048]{1,0:T(8,128)(2,1)S(1)}, bf16[76,2048]{1,0:T(8,128)(2,1)S(1)}, u32[]{:S(2)}, u32[]{:S(2)}) collective-permute-start(bf16[76,2048]{1,0:T(8,128)(2,1)S(1)} %pad_maximum_fusion), channel_id=1, source_target_pairs={{1,0},{2,1},{3,2},{4,3},{5,4},{6,5},{7,6},{9,8},{10,9},{11,10},{12... | collective-permute-start | bytes 933896 | tf_op jit(solution)/shard_map/ppermute | solution.py:17
  4.4 10.0 %collective-permute-start.1 = (f32[2,2,2048]{2,1,0:T(2,128)}, f32[2,2,2048]{2,1,0:T(2,128)S(1)}, u32[]{:S(2)}, u32[]{:S(2)}) collective-permute-start(f32[2,2,2048]{2,1,0:T(2,128)} %bitcast.22), channel_id=1, source_target_pairs={{0,1},{1,2},{2,3},{3,4},{4,5},{5,6},{6,7},{8,9},{9,10},{10,11},{11... | collective-permute-start | bytes 98312 | tf_op jit(solution)/shard_map/ppermute | solution.py:17
  14.4 1.3 %collective-permute-done.1.previous_ref = f32[2,2,2048]{2,1,0:T(2,128)S(1)} collective-permute-done((f32[2,2,2048]{2,1,0:T(2,128)}, f32[2,2,2048]{2,1,0:T(2,128)S(1)}, u32[]{:S(2)}, u32[]{:S(2)}) %collective-permute-start.1) | collective-permute-done | bytes 32800 | tf_op jit(solution)/shard_map/ppermute | solution.py:17
  15.7 0.0 copy-start.1
  15.7 0.6 copy-done.1
  16.3 3.5 %shard_map.46 = (f32[2,2,64,64]{3,2,1,0:T(8,128)}, bf16[256,2048]{1,0:T(8,128)(2,1)}) custom-call(bf16[2,3,64,2048]{3,2,1,0:T(8,128)(2,1)} %bitcast.17, f32[2,2,2048]{2,1,0:T(2,128)} %copy-done.1, f32[2,2,2048]{2,1,0:T(2,128)} %bitcast.23), custom_call_target="tpu_custom_call" | custom-call | tf_op jit(solution)/shard_map/pallas_call | solution.py:117
  19.9 0.0 collective-permute-done.bundle_ref
  19.9 0.0 copy-start
  19.9 0.7 %copy-done = bf16[76,2048]{1,0:T(8,128)(2,1)} copy-done((bf16[76,2048]{1,0:T(8,128)(2,1)}, bf16[76,2048]{1,0:T(8,128)(2,1)S(1)}, u32[]{:S(2)}) %copy-start) | copy-done | bytes 311320
  20.6 3.5 %shard_map.47 = bf16[4,2560]{1,0:T(4,128)(2,1)} custom-call(bf16[2,3,64,2048]{3,2,1,0:T(8,128)(2,1)} %bitcast.18, bf16[76,2048]{1,0:T(8,128)(2,1)} %copy-done, f32[2,2,64,64]{3,2,1,0:T(8,128)} %get-tuple-element.7.near_ref, bf16[256,2048]{1,0:T(8,128)(2,1)} %get-tuple-element.8.held_ref, s32[1,2560]{1,0:T(1,128)} %place_ref.3), custom_call_target="tpu_custom_call" | custom-call | tf_op jit(solution)/shard_map/pallas_call | solution.py:136
  24.1 0.9 %reshape.51 = bf16[4,64,40]{2,1,0:T(8,128)(2,1)S(1)} reshape(bf16[4,2560]{1,0:T(4,128)(2,1)} %shard_map.47) | data formatting | bytes 40960 | tf_op jit(solution)/shard_map/reshape | solution.py:245
  25.0 0.1 copy.7
  25.1 0.1 copy.8
  25.2 27.8 %all_to_all.10.in_ref = bf16[64,1,160]{2,1,0:T(2,128)(2,1)} all-to-all(bf16[64,1,160]{2,1,0:T(2,128)(2,1)S(1)} %copy.8), channel_id=1, replica_groups=mesh['energy'=64,'domain'=8] {'energy'}, dimensions={0} | all-to-all | bytes 40960 | tf_op jit(solution)/shard_map/all_to_all | solution.py:246
  53.0 2.1 %shard_map.48 = bf16[64,1,80]{2,1,0:T(2,128)(2,1)} custom-call(bf16[64,1,160]{2,1,0:T(2,128)(2,1)} %all_to_all.10.in_ref), custom_call_target="tpu_custom_call" | custom-call | tf_op jit(solution)/shard_map/pallas_call | solution.py:175
  55.0 14.1 %all_to_all.11 = bf16[64,1,80]{2,1,0:T(2,128)(2,1)S(1)} all-to-all(bf16[64,1,80]{2,1,0:T(2,128)(2,1)} %shard_map.48), channel_id=1, replica_groups=mesh['energy'=64,'domain'=8] {'energy'}, dimensions={0} | all-to-all | bytes 20480 | tf_op jit(solution)/shard_map/all_to_all | solution.py:248
  69.2 0.1 copy.9
  69.3 0.1 copy.10
  69.4 0.7 reshape.54.polar_ref
  70.1 2.2 %shard_map.49 = f32[2,64,64]{2,1,0:T(8,128)} custom-call(bf16[2,2560]{1,0:T(2,128)(2,1)} %reshape.54.polar_ref, s32[1,2560]{1,0:T(1,128)} %place_ref.3, bf16[2,64,80]{2,1,0:T(8,128)(2,1)} %bitcast.25), custom_call_target="tpu_custom_call" | custom-call | tf_op jit(solution)/shard_map/pallas_call | solution.py:220
  (2 shorter events, 0.1 us)
Async XLA Ops:
  1.9 18.0 %collective-permute-start = (bf16[76,2048]{1,0:T(8,128)(2,1)S(1)}, bf16[76,2048]{1,0:T(8,128)(2,1)S(1)}, u32[]{:S(2)}, u32[]{:S(2)}) collective-permute-start(bf16[76,2048]{1,0:T(8,128)(2,1)S(1)} %pad_maximum_fusion), channel_id=1, source_target_pairs={{1,0},{2,1},{3,2},{4,3},{5,4},{6,5},{7,6},{9,8},{10,9},{11,10},{12... | collective-permute-start | bytes 933896 | tf_op jit(solution)/shard_map/ppermute | solution.py:17
  4.4 11.3 %collective-permute-start.1 = (f32[2,2,2048]{2,1,0:T(2,128)}, f32[2,2,2048]{2,1,0:T(2,128)S(1)}, u32[]{:S(2)}, u32[]{:S(2)}) collective-permute-start(f32[2,2,2048]{2,1,0:T(2,128)} %bitcast.22), channel_id=1, source_target_pairs={{0,1},{1,2},{2,3},{3,4},{4,5},{5,6},{6,7},{8,9},{9,10},{10,11},{11... | collective-permute-start | bytes 98312 | tf_op jit(solution)/shard_map/ppermute | solution.py:17
  15.7 0.6 copy-start.1
  19.9 0.7 %copy-start = (bf16[76,2048]{1,0:T(8,128)(2,1)}, bf16[76,2048]{1,0:T(8,128)(2,1)S(1)}, u32[]{:S(2)}) copy-start(bf16[76,2048]{1,0:T(8,128)(2,1)S(1)} %collective-permute-done.bundle_ref) | copy-start | bytes 933892

commit v18 on v17

--- a/solution.py
+++ b/solution.py
@@ -178,7 +178,7 @@
     )(by_element)
 
 
-def _screen_kernel(polar_ref, place_ref, screen_ref, out_ref, *, rows, cols):
+def _screen_kernel(polar_ref, place_ref, screen_ref, out_ref, polar_scr, *, rows, cols):
     def nt(a, b):
         return lax.dot_general(a, b, (((1,), (1,)), ((), ())), preferred_element_type=jnp.float32)
 
@@ -187,7 +187,13 @@
 
     row_hit, col_hit = _place_hits(place_ref, rows, cols)
     col_hit = col_hit.astype(jnp.bfloat16)
-    polar = polar_ref[...].astype(jnp.float32)
+    chunks = polar_ref.shape[0]
+    width = polar_ref.shape[2] // 2
+    for chunk in range(chunks):
+        piece = polar_ref[chunk]
+        for part in range(2):
+            polar_scr[part:part + 1, chunk * width:(chunk + 1) * width] = piece[:, part * width:(part + 1) * width]
+    polar = polar_scr[...].astype(jnp.float32)
     dense = []
     for part in range(2):
         spread = jnp.where(row_hit, polar[part:part + 1, :], 0.0).astype(jnp.bfloat16)
@@ -220,6 +226,7 @@
     return pl.pallas_call(
         kernel,
         out_shape=jax.ShapeDtypeStruct((2, rows, rows), jnp.float32),
+        scratch_shapes=[pltpu.VMEM((2, pattern_row.shape[1]), polar_row.dtype)],
     )(polar_row, pattern_row, screen_block)
 
 
@@ -246,7 +253,6 @@
     by_element = lax.all_to_all(values, "energy", split_axis=0, concat_axis=0, tiled=True)
     polarization = lag_sums(by_element)
     per_energy = lax.all_to_all(polarization, "energy", split_axis=0, concat_axis=0, tiled=True)
-    per_energy = per_energy.reshape(chunks, 2, -1).transpose(1, 0, 2).reshape(2, -1)
     result = screen(per_energy, pattern, screened[0, 0])
     return result[None, None]
 

time: 72.8 us -> 72.8 us (level)
  local copies, waits for them, and re-layouts: 4.33 us -> 3.4 us
where the time goes in v18:
time: 72.8 us; the launch traced here: 72.3 us
  blocking collectives  42.6 us (59%)
  starting transfers between devices  12.5 us (17%)
  Pallas kernels  11.5 us (16%)
  local copies, waits for them, and re-layouts  3.4 us (5%)
  waiting for transfers between devices  1.36 us (2%)
  other arithmetic  0.9 us (1%)
    all_to_all x1, blocking collectives, body(): lax.all_to_all(values, 'energy', split_axis=0, concat_axis=0, tiled=True)  27.8 us
    all_to_all x1, blocking collectives, body(): lax.all_to_all(polarization, 'energy', split_axis=0, concat_axis=0, tiled...  14.8 us
    ppermute x2, starting transfers between devices, passed_along(): return lax.ppermute(x, axis, pairs)  12.5 us
    pallas_call x1, Pallas kernels, element_values(): pl.pallas_call(functools.partial(_early_kernel, factor=factor, rows=rows)...  3.52 us
    pallas_call x1, Pallas kernels, element_values(): pl.pallas_call(functools.partial(_late_kernel, factor=factor, rows=rows,...  3.48 us
    pallas_call x1, Pallas kernels, screen(): pl.pallas_call(kernel, out_shape=jax.ShapeDtypeStruct((2, rows, rows), jn...  2.42 us
    pallas_call x1, Pallas kernels, lag_sums(): pl.pallas_call(kernel, out_shape=jax.ShapeDtypeStruct((energy_count, 1, 2...  2.08 us
  transfers between devices with their start and end apart: 2, of which 1 were waited for; matrix products, arithmetic and copies ran while one was open for 0% of the time, Pallas kernels for 5%

profile of v18, /device:TPU:7, one launch (start us, length us, event | category | flops | bytes accessed | tf_op | source)
XLA Modules:
  0.0 72.3 jit_solution(14308540285125862815)
XLA Ops:
  0.0 0.8 %reduce-precision_convert_fusion.1 = (bf16[1,2,2,2048]{3,2,1,0:T(2,128)(2,1)S(1)}, bf16[1,2,2,2048]{3,2,1,0:T(2,128)(2,1)S(1)}, bf16[1,2,2,2048]{3,2,1,0:T(2,128)(2,1)S(1)}) fusion(f32[1,1,2,2,2048]{4,3,2,1,0:T(2,128)} %param.5), kind=kLoop, calls=%fused_computation.5 | loop fusion | flops 57344 | bytes 81920 | tf_op jit(solution)/shard_map/convert
  0.8 0.1 pad_maximum_fusion.1
  0.9 1.0 %slice.3 = bf16[1,1,2,2,16,2048]{5,4,3,2,1,0:T(8,128)(2,1)S(1)} slice(bf16[1,1,2,3,64,2048]{5,4,3,2,1,0:T(8,128)(2,1)} %param.4), slice={[0:1], [0:1], [0:2], [0:2], [0:16], [0:2048]} | slice | bytes 524288 | tf_op jit(solution)/shard_map/slice | solution.py:245
  1.9 2.5 %collective-permute-start = (bf16[76,2048]{1,0:T(8,128)(2,1)S(1)}, bf16[76,2048]{1,0:T(8,128)(2,1)S(1)}, u32[]{:S(2)}, u32[]{:S(2)}) collective-permute-start(bf16[76,2048]{1,0:T(8,128)(2,1)S(1)} %pad_maximum_fusion), channel_id=1, source_target_pairs={{1,0},{2,1},{3,2},{4,3},{5,4},{6,5},{7,6},{9,8},{10,9},{11,10},{12... | collective-permute-start | bytes 933896 | tf_op jit(solution)/shard_map/ppermute | solution.py:17
  4.4 10.0 %collective-permute-start.1 = (f32[2,2,2048]{2,1,0:T(2,128)}, f32[2,2,2048]{2,1,0:T(2,128)S(1)}, u32[]{:S(2)}, u32[]{:S(2)}) collective-permute-start(f32[2,2,2048]{2,1,0:T(2,128)} %bitcast.19), channel_id=1, source_target_pairs={{0,1},{1,2},{2,3},{3,4},{4,5},{5,6},{6,7},{8,9},{9,10},{10,11},{11... | collective-permute-start | bytes 98312 | tf_op jit(solution)/shard_map/ppermute | solution.py:17
  14.4 1.3 %collective-permute-done.1.previous_ref = f32[2,2,2048]{2,1,0:T(2,128)S(1)} collective-permute-done((f32[2,2,2048]{2,1,0:T(2,128)}, f32[2,2,2048]{2,1,0:T(2,128)S(1)}, u32[]{:S(2)}, u32[]{:S(2)}) %collective-permute-start.1) | collective-permute-done | bytes 32800 | tf_op jit(solution)/shard_map/ppermute | solution.py:17
  15.7 0.0 copy-start.1
  15.7 0.6 copy-done.1
  16.3 3.5 %shard_map.46 = (f32[2,2,64,64]{3,2,1,0:T(8,128)}, bf16[256,2048]{1,0:T(8,128)(2,1)}) custom-call(bf16[2,3,64,2048]{3,2,1,0:T(8,128)(2,1)} %bitcast.14, f32[2,2,2048]{2,1,0:T(2,128)} %copy-done.1, f32[2,2,2048]{2,1,0:T(2,128)} %bitcast.20), custom_call_target="tpu_custom_call" | custom-call | tf_op jit(solution)/shard_map/pallas_call | solution.py:117
  19.9 0.0 collective-permute-done.bundle_ref
  19.9 0.0 copy-start
  19.9 0.7 %copy-done = bf16[76,2048]{1,0:T(8,128)(2,1)} copy-done((bf16[76,2048]{1,0:T(8,128)(2,1)}, bf16[76,2048]{1,0:T(8,128)(2,1)S(1)}, u32[]{:S(2)}) %copy-start) | copy-done | bytes 311320
  20.6 3.5 %shard_map.47 = bf16[4,2560]{1,0:T(4,128)(2,1)} custom-call(bf16[2,3,64,2048]{3,2,1,0:T(8,128)(2,1)} %bitcast.15, bf16[76,2048]{1,0:T(8,128)(2,1)} %copy-done, f32[2,2,64,64]{3,2,1,0:T(8,128)} %get-tuple-element.7.near_ref, bf16[256,2048]{1,0:T(8,128)(2,1)} %get-tuple-element.8.held_ref, s32[1,2560]{1,0:T(1,128)} %place_ref.3), custom_call_target="tpu_custom_call" | custom-call | tf_op jit(solution)/shard_map/pallas_call | solution.py:136
  24.1 0.9 %reshape.45 = bf16[4,64,40]{2,1,0:T(8,128)(2,1)S(1)} reshape(bf16[4,2560]{1,0:T(4,128)(2,1)} %shard_map.47) | data formatting | bytes 40960 | tf_op jit(solution)/shard_map/reshape | solution.py:252
  25.0 0.1 copy.6
  25.1 0.1 copy.7
  25.2 27.8 %all_to_all.10.in_ref = bf16[64,1,160]{2,1,0:T(2,128)(2,1)} all-to-all(bf16[64,1,160]{2,1,0:T(2,128)(2,1)S(1)} %copy.7), channel_id=1, replica_groups=mesh['energy'=64,'domain'=8] {'energy'}, dimensions={0} | all-to-all | bytes 40960 | tf_op jit(solution)/shard_map/all_to_all | solution.py:253
  53.0 2.1 %shard_map.48 = bf16[64,1,80]{2,1,0:T(2,128)(2,1)} custom-call(bf16[64,1,160]{2,1,0:T(2,128)(2,1)} %all_to_all.10.in_ref), custom_call_target="tpu_custom_call" | custom-call | tf_op jit(solution)/shard_map/pallas_call | solution.py:175
  55.0 14.8 %all_to_all.11.polar_ref = bf16[64,1,80]{2,1,0:T(2,128)(2,1)} all-to-all(bf16[64,1,80]{2,1,0:T(2,128)(2,1)} %shard_map.48), channel_id=1, replica_groups=mesh['energy'=64,'domain'=8] {'energy'}, dimensions={0} | all-to-all | bytes 20480 | tf_op jit(solution)/shard_map/all_to_all | solution.py:255
  69.8 2.4 %shard_map.49 = f32[2,64,64]{2,1,0:T(8,128)} custom-call(bf16[64,1,80]{2,1,0:T(2,128)(2,1)} %all_to_all.11.polar_ref, s32[1,2560]{1,0:T(1,128)} %place_ref.3, bf16[2,64,80]{2,1,0:T(8,128)(2,1)} %bitcast.21), custom_call_target="tpu_custom_call" | custom-call | tf_op jit(solution)/shard_map/pallas_call | solution.py:226
  (2 shorter events, 0.1 us)
Async XLA Ops:
  1.9 18.0 %collective-permute-start = (bf16[76,2048]{1,0:T(8,128)(2,1)S(1)}, bf16[76,2048]{1,0:T(8,128)(2,1)S(1)}, u32[]{:S(2)}, u32[]{:S(2)}) collective-permute-start(bf16[76,2048]{1,0:T(8,128)(2,1)S(1)} %pad_maximum_fusion), channel_id=1, source_target_pairs={{1,0},{2,1},{3,2},{4,3},{5,4},{6,5},{7,6},{9,8},{10,9},{11,10},{12... | collective-permute-start | bytes 933896 | tf_op jit(solution)/shard_map/ppermute | solution.py:17
  4.4 11.3 %collective-permute-start.1 = (f32[2,2,2048]{2,1,0:T(2,128)}, f32[2,2,2048]{2,1,0:T(2,128)S(1)}, u32[]{:S(2)}, u32[]{:S(2)}) collective-permute-start(f32[2,2,2048]{2,1,0:T(2,128)} %bitcast.19), channel_id=1, source_target_pairs={{0,1},{1,2},{2,3},{3,4},{4,5},{5,6},{6,7},{8,9},{9,10},{10,11},{11... | collective-permute-start | bytes 98312 | tf_op jit(solution)/shard_map/ppermute | solution.py:17
  15.7 0.6 copy-start.1
  19.9 0.7 %copy-start = (bf16[76,2048]{1,0:T(8,128)(2,1)}, bf16[76,2048]{1,0:T(8,128)(2,1)S(1)}, u32[]{:S(2)}) copy-start(bf16[76,2048]{1,0:T(8,128)(2,1)S(1)} %collective-permute-done.bundle_ref) | copy-start | bytes 933892

commit v19 on v18

--- a/solution.py
+++ b/solution.py
@@ -105,12 +105,16 @@
     joined = jnp.concatenate(joined, axis=0).astype(jnp.bfloat16)
     row_hit, col_hit = _place_hits(place_ref, rows, cols)
     by_column = jnp.dot(joined, col_hit.astype(jnp.bfloat16), preferred_element_type=jnp.float32)
+    chunks = out_ref.shape[0]
+    width = out_ref.shape[2] // 4
     for k in range(4):
         picked = jnp.where(row_hit, by_column[k * rows:(k + 1) * rows], 0.0)
-        out_ref[k:k + 1, :] = jnp.sum(picked, axis=0, keepdims=True).astype(out_ref.dtype)
-
-
-def element_values(own_slab, bundle, previous_rate, own_rate, pattern_row, edge):
+        picked = jnp.sum(picked, axis=0, keepdims=True).astype(out_ref.dtype)
+        for chunk in range(chunks):
+            out_ref[chunk, :, k * width:(k + 1) * width] = picked[:, chunk * width:(chunk + 1) * width]
+
+
+def element_values(own_slab, bundle, previous_rate, own_rate, pattern_row, edge, chunks):
     _, blocks, rows, block_order = own_slab.shape
     count = pattern_row.shape[1]
     factor = 1.0 / math.sqrt(3.0 * block_order)
@@ -143,8 +147,8 @@
             pl.BlockSpec((4 * rows, block_order), lambda j: (0, 0)),
             pl.BlockSpec((1, count), lambda j: (0, 0)),
         ],
-        out_specs=pl.BlockSpec((4, count), lambda j: (0, 0)),
-        out_shape=jax.ShapeDtypeStruct((4, count), jnp.bfloat16),
+        out_specs=pl.BlockSpec((chunks, 1, 4 * count // chunks), lambda j: (0, 0, 0)),
+        out_shape=jax.ShapeDtypeStruct((chunks, 1, 4 * count // chunks), jnp.bfloat16),
         scratch_shapes=[pltpu.VMEM((1, 2, 2, block_order), jnp.float32)],
     )(own_slab, bundle, near, held, pattern_row)
 
@@ -247,9 +251,8 @@
         [edge_block.reshape(-1, block_order), split_exact(own_rate).reshape(-1, block_order)], axis=0
     )
     bundle = passed_along(bundle, "domain", -1)
-    values = element_values(green_slab[0, 0], bundle, previous_rate, own_rate, pattern, EDGE)
     chunks = lax.axis_size("energy")
-    values = values.reshape(4, chunks, -1).transpose(1, 0, 2).reshape(chunks, 1, -1)
+    values = element_values(green_slab[0, 0], bundle, previous_rate, own_rate, pattern, EDGE, chunks)
     by_element = lax.all_to_all(values, "energy", split_axis=0, concat_axis=0, tiled=True)
     polarization = lag_sums(by_element)
     per_energy = lax.all_to_all(polarization, "energy", split_axis=0, concat_axis=0, tiled=True)

time: 72.8 us -> 72 us (0.989)
  local copies, waits for them, and re-layouts: 3.4 us -> 2.34 us
    reshape x2 -> x0, local copies, waits for them, and re-layouts: 0.97 us -> none  [body(): values.reshape(4, chunks, -1).transpose(1, 0, 2).reshape(chunks, 1, -1)]
where the time goes in v19:
time: 72 us; the launch traced here: 71.6 us
  blocking collectives  42.8 us (59%)
  starting transfers between devices  12.5 us (17%)
  Pallas kernels  11.7 us (16%)
  local copies, waits for them, and re-layouts  2.34 us (3%)
  waiting for transfers between devices  1.36 us (2%)
  other arithmetic  0.9 us (1%)
    all_to_all x1, blocking collectives, body(): lax.all_to_all(values, 'energy', split_axis=0, concat_axis=0, tiled=True)  28 us
    all_to_all x1, blocking collectives, body(): lax.all_to_all(polarization, 'energy', split_axis=0, concat_axis=0, tiled...  14.8 us
    ppermute x2, starting transfers between devices, passed_along(): return lax.ppermute(x, axis, pairs)  12.5 us
    pallas_call x1, Pallas kernels, element_values(): pl.pallas_call(functools.partial(_late_kernel, factor=factor, rows=rows,...  3.65 us
    pallas_call x1, Pallas kernels, element_values(): pl.pallas_call(functools.partial(_early_kernel, factor=factor, rows=rows)...  3.52 us
    pallas_call x1, Pallas kernels, screen(): pl.pallas_call(kernel, out_shape=jax.ShapeDtypeStruct((2, rows, rows), jn...  2.42 us
    pallas_call x1, Pallas kernels, lag_sums(): pl.pallas_call(kernel, out_shape=jax.ShapeDtypeStruct((energy_count, 1, 2...  2.08 us
  transfers between devices with their start and end apart: 2, of which 1 were waited for; matrix products, arithmetic and copies ran while one was open for 0% of the time, Pallas kernels for 5%

profile of v19, /device:TPU:7, one launch (start us, length us, event | category | flops | bytes accessed | tf_op | source)
XLA Modules:
  0.0 71.6 jit_solution(5564832448178555822)
XLA Ops:
  0.0 0.8 %reduce-precision_convert_fusion.1 = (bf16[1,2,2,2048]{3,2,1,0:T(2,128)(2,1)S(1)}, bf16[1,2,2,2048]{3,2,1,0:T(2,128)(2,1)S(1)}, bf16[1,2,2,2048]{3,2,1,0:T(2,128)(2,1)S(1)}) fusion(f32[1,1,2,2,2048]{4,3,2,1,0:T(2,128)} %param.5), kind=kLoop, calls=%fused_computation.5 | loop fusion | flops 57344 | bytes 81920 | tf_op jit(solution)/shard_map/convert
  0.8 0.1 pad_maximum_fusion.1
  0.9 1.0 %slice.3 = bf16[1,1,2,2,16,2048]{5,4,3,2,1,0:T(8,128)(2,1)S(1)} slice(bf16[1,1,2,3,64,2048]{5,4,3,2,1,0:T(8,128)(2,1)} %param.4), slice={[0:1], [0:1], [0:2], [0:2], [0:16], [0:2048]} | slice | bytes 524288 | tf_op jit(solution)/shard_map/slice | solution.py:249
  1.9 2.5 %collective-permute-start = (bf16[76,2048]{1,0:T(8,128)(2,1)S(1)}, bf16[76,2048]{1,0:T(8,128)(2,1)S(1)}, u32[]{:S(2)}, u32[]{:S(2)}) collective-permute-start(bf16[76,2048]{1,0:T(8,128)(2,1)S(1)} %pad_maximum_fusion), channel_id=1, source_target_pairs={{1,0},{2,1},{3,2},{4,3},{5,4},{6,5},{7,6},{9,8},{10,9},{11,10},{12... | collective-permute-start | bytes 933896 | tf_op jit(solution)/shard_map/ppermute | solution.py:17
  4.4 10.0 %collective-permute-start.1 = (f32[2,2,2048]{2,1,0:T(2,128)}, f32[2,2,2048]{2,1,0:T(2,128)S(1)}, u32[]{:S(2)}, u32[]{:S(2)}) collective-permute-start(f32[2,2,2048]{2,1,0:T(2,128)} %bitcast.15), channel_id=1, source_target_pairs={{0,1},{1,2},{2,3},{3,4},{4,5},{5,6},{6,7},{8,9},{9,10},{10,11},{11... | collective-permute-start | bytes 98312 | tf_op jit(solution)/shard_map/ppermute | solution.py:17
  14.4 1.3 %collective-permute-done.1.previous_ref = f32[2,2,2048]{2,1,0:T(2,128)S(1)} collective-permute-done((f32[2,2,2048]{2,1,0:T(2,128)}, f32[2,2,2048]{2,1,0:T(2,128)S(1)}, u32[]{:S(2)}, u32[]{:S(2)}) %collective-permute-start.1) | collective-permute-done | bytes 32800 | tf_op jit(solution)/shard_map/ppermute | solution.py:17
  15.7 0.0 copy-start.1
  15.7 0.6 copy-done.1
  16.3 3.5 %shard_map.46 = (f32[2,2,64,64]{3,2,1,0:T(8,128)}, bf16[256,2048]{1,0:T(8,128)(2,1)}) custom-call(bf16[2,3,64,2048]{3,2,1,0:T(8,128)(2,1)} %bitcast.12, f32[2,2,2048]{2,1,0:T(2,128)} %copy-done.1, f32[2,2,2048]{2,1,0:T(2,128)} %bitcast.16), custom_call_target="tpu_custom_call" | custom-call | tf_op jit(solution)/shard_map/pallas_call | solution.py:121
  19.9 0.0 collective-permute-done.bundle_ref
  19.9 0.0 copy-start
  19.9 0.7 %copy-done = bf16[76,2048]{1,0:T(8,128)(2,1)} copy-done((bf16[76,2048]{1,0:T(8,128)(2,1)}, bf16[76,2048]{1,0:T(8,128)(2,1)S(1)}, u32[]{:S(2)}) %copy-start) | copy-done | bytes 311320
  20.6 3.6 %shard_map.47 = bf16[64,1,160]{2,1,0:T(2,128)(2,1)} custom-call(bf16[2,3,64,2048]{3,2,1,0:T(8,128)(2,1)} %bitcast.13, bf16[76,2048]{1,0:T(8,128)(2,1)} %copy-done, f32[2,2,64,64]{3,2,1,0:T(8,128)} %get-tuple-element.7.near_ref, bf16[256,2048]{1,0:T(8,128)(2,1)} %get-tuple-element.8.held_ref, s32[1,2560]{1,0:T(1,128)} %place_ref.3), custom_call_target="tpu_custom_call" | custom-call | tf_op jit(solution)/shard_map/pallas_call | solution.py:140
  24.3 28.0 %all_to_all.10.in_ref = bf16[64,1,160]{2,1,0:T(2,128)(2,1)} all-to-all(bf16[64,1,160]{2,1,0:T(2,128)(2,1)} %shard_map.47), channel_id=1, replica_groups=mesh['energy'=64,'domain'=8] {'energy'}, dimensions={0} | all-to-all | bytes 40960 | tf_op jit(solution)/shard_map/all_to_all | solution.py:256
  52.3 2.1 %shard_map.48 = bf16[64,1,80]{2,1,0:T(2,128)(2,1)} custom-call(bf16[64,1,160]{2,1,0:T(2,128)(2,1)} %all_to_all.10.in_ref), custom_call_target="tpu_custom_call" | custom-call | tf_op jit(solution)/shard_map/pallas_call | solution.py:179
  54.3 14.8 %all_to_all.11.polar_ref = bf16[64,1,80]{2,1,0:T(2,128)(2,1)} all-to-all(bf16[64,1,80]{2,1,0:T(2,128)(2,1)} %shard_map.48), channel_id=1, replica_groups=mesh['energy'=64,'domain'=8] {'energy'}, dimensions={0} | all-to-all | bytes 20480 | tf_op jit(solution)/shard_map/all_to_all | solution.py:258
  69.1 2.4 %shard_map.49 = f32[2,64,64]{2,1,0:T(8,128)} custom-call(bf16[64,1,80]{2,1,0:T(2,128)(2,1)} %all_to_all.11.polar_ref, s32[1,2560]{1,0:T(1,128)} %place_ref.3, bf16[2,64,80]{2,1,0:T(8,128)(2,1)} %bitcast.17), custom_call_target="tpu_custom_call" | custom-call | tf_op jit(solution)/shard_map/pallas_call | solution.py:230
  (2 shorter events, 0.1 us)
Async XLA Ops:
  1.9 18.0 %collective-permute-start = (bf16[76,2048]{1,0:T(8,128)(2,1)S(1)}, bf16[76,2048]{1,0:T(8,128)(2,1)S(1)}, u32[]{:S(2)}, u32[]{:S(2)}) collective-permute-start(bf16[76,2048]{1,0:T(8,128)(2,1)S(1)} %pad_maximum_fusion), channel_id=1, source_target_pairs={{1,0},{2,1},{3,2},{4,3},{5,4},{6,5},{7,6},{9,8},{10,9},{11,10},{12... | collective-permute-start | bytes 933896 | tf_op jit(solution)/shard_map/ppermute | solution.py:17
  4.4 11.3 %collective-permute-start.1 = (f32[2,2,2048]{2,1,0:T(2,128)}, f32[2,2,2048]{2,1,0:T(2,128)S(1)}, u32[]{:S(2)}, u32[]{:S(2)}) collective-permute-start(f32[2,2,2048]{2,1,0:T(2,128)} %bitcast.15), channel_id=1, source_target_pairs={{0,1},{1,2},{2,3},{3,4},{4,5},{5,6},{6,7},{8,9},{9,10},{10,11},{11... | collective-permute-start | bytes 98312 | tf_op jit(solution)/shard_map/ppermute | solution.py:17
  15.7 0.6 copy-start.1
  19.9 0.7 %copy-start = (bf16[76,2048]{1,0:T(8,128)(2,1)}, bf16[76,2048]{1,0:T(8,128)(2,1)S(1)}, u32[]{:S(2)}) copy-start(bf16[76,2048]{1,0:T(8,128)(2,1)S(1)} %collective-permute-done.bundle_ref) | copy-start | bytes 933892

commit v20 on v19

--- a/solution.py
+++ b/solution.py
@@ -198,29 +198,27 @@
         for part in range(2):
             polar_scr[part:part + 1, chunk * width:(chunk + 1) * width] = piece[:, part * width:(part + 1) * width]
     polar = polar_scr[...].astype(jnp.float32)
-    dense = []
-    for part in range(2):
-        spread = jnp.where(row_hit, polar[part:part + 1, :], 0.0).astype(jnp.bfloat16)
-        dense.append(nt(spread, col_hit).astype(jnp.bfloat16))
-    dense_real, dense_imag = dense
+    spread = jnp.concatenate(
+        [jnp.where(row_hit, polar[part:part + 1, :], 0.0) for part in range(2)], axis=0
+    ).astype(jnp.bfloat16)
+    dense = nt(spread, col_hit).astype(jnp.bfloat16)
+    dense_real = dense[:rows]
+    dense_imag = dense[rows:]
     screen_real = screen_ref[0]
     screen_imag = screen_ref[1]
-    inner_real = (nt(dense_real, screen_real) + nt(dense_imag, screen_imag)).astype(jnp.bfloat16)
-    inner_imag = (nt(dense_imag, screen_real) - nt(dense_real, screen_imag)).astype(jnp.bfloat16)
-    near_real = screen_real[:, :rows]
-    near_imag = screen_imag[:, :rows]
-    side_real = screen_real[:, rows:]
-    side_imag = screen_imag[:, rows:]
-    edge_real = dense_real[:, rows:]
-    edge_imag = dense_imag[:, rows:]
-    across_real = (nn(near_real, edge_real) - nn(near_imag, edge_imag)).astype(jnp.bfloat16)
-    across_imag = (nn(near_real, edge_imag) + nn(near_imag, edge_real)).astype(jnp.bfloat16)
-    first_real = nn(near_real, inner_real) - nn(near_imag, inner_imag)
-    first_imag = nn(near_real, inner_imag) + nn(near_imag, inner_real)
-    second_real = nt(side_real, across_real) + nt(side_imag, across_imag)
-    second_imag = nt(side_imag, across_real) - nt(side_real, across_imag)
-    out_ref[0] = first_real + second_real
-    out_ref[1] = first_imag + second_imag
+    both = nt(dense, jnp.concatenate([screen_real, screen_imag], axis=0))
+    inner_real = (both[:rows, :rows] + both[rows:, rows:]).astype(jnp.bfloat16)
+    inner_imag = (both[rows:, :rows] - both[:rows, rows:]).astype(jnp.bfloat16)
+    near = jnp.concatenate([screen_real[:, :rows], screen_imag[:, :rows]], axis=0)
+    edge = cols - rows
+    across = nn(near, jnp.concatenate([dense_real[:, rows:], dense_imag[:, rows:]], axis=1))
+    across_real = (across[:rows, :edge] - across[rows:, edge:]).astype(jnp.bfloat16)
+    across_imag = (across[:rows, edge:] + across[rows:, :edge]).astype(jnp.bfloat16)
+    first = nn(near, jnp.concatenate([inner_real, inner_imag], axis=1))
+    side = jnp.concatenate([screen_real[:, rows:], screen_imag[:, rows:]], axis=0)
+    second = nt(side, jnp.concatenate([across_real, across_imag], axis=0))
+    out_ref[0] = (first[:rows, :rows] - first[rows:, rows:]) + (second[:rows, :rows] + second[rows:, rows:])
+    out_ref[1] = (first[:rows, rows:] + first[rows:, :rows]) + (second[rows:, :rows] - second[:rows, rows:])
 
 
 def screen(polar_row, pattern_row, screen_block):

time: 72 us -> 72.3 us (level)
  no operation moved by 1% of the time
where the time goes in v20:
time: 72.3 us; the launch traced here: 71.8 us
  blocking collectives  42.8 us (59%)
  starting transfers between devices  12.5 us (17%)
  Pallas kernels  11.9 us (16%)
  local copies, waits for them, and re-layouts  2.34 us (3%)
  waiting for transfers between devices  1.36 us (2%)
  other arithmetic  0.9 us (1%)
    all_to_all x1, blocking collectives, body(): lax.all_to_all(values, 'energy', split_axis=0, concat_axis=0, tiled=True)  28 us
    all_to_all x1, blocking collectives, body(): lax.all_to_all(polarization, 'energy', split_axis=0, concat_axis=0, tiled...  14.8 us
    ppermute x2, starting transfers between devices, passed_along(): return lax.ppermute(x, axis, pairs)  12.5 us
    pallas_call x1, Pallas kernels, element_values(): pl.pallas_call(functools.partial(_late_kernel, factor=factor, rows=rows,...  3.65 us
    pallas_call x1, Pallas kernels, element_values(): pl.pallas_call(functools.partial(_early_kernel, factor=factor, rows=rows)...  3.52 us
    pallas_call x1, Pallas kernels, screen(): pl.pallas_call(kernel, out_shape=jax.ShapeDtypeStruct((2, rows, rows), jn...  2.69 us
    pallas_call x1, Pallas kernels, lag_sums(): pl.pallas_call(kernel, out_shape=jax.ShapeDtypeStruct((energy_count, 1, 2...  2.08 us
  transfers between devices with their start and end apart: 2, of which 1 were waited for; matrix products, arithmetic and copies ran while one was open for 0% of the time, Pallas kernels for 5%

profile of v20, /device:TPU:7, one launch (start us, length us, event | category | flops | bytes accessed | tf_op | source)
XLA Modules:
  0.0 71.8 jit_solution(5331376708628846370)
XLA Ops:
  0.0 0.8 %reduce-precision_convert_fusion.1 = (bf16[1,2,2,2048]{3,2,1,0:T(2,128)(2,1)S(1)}, bf16[1,2,2,2048]{3,2,1,0:T(2,128)(2,1)S(1)}, bf16[1,2,2,2048]{3,2,1,0:T(2,128)(2,1)S(1)}) fusion(f32[1,1,2,2,2048]{4,3,2,1,0:T(2,128)} %param.5), kind=kLoop, calls=%fused_computation.5 | loop fusion | flops 57344 | bytes 81920 | tf_op jit(solution)/shard_map/convert
  0.8 0.1 pad_maximum_fusion.1
  0.9 1.0 %slice.3 = bf16[1,1,2,2,16,2048]{5,4,3,2,1,0:T(8,128)(2,1)S(1)} slice(bf16[1,1,2,3,64,2048]{5,4,3,2,1,0:T(8,128)(2,1)} %param.4), slice={[0:1], [0:1], [0:2], [0:2], [0:16], [0:2048]} | slice | bytes 524288 | tf_op jit(solution)/shard_map/slice | solution.py:247
  1.9 2.5 %collective-permute-start = (bf16[76,2048]{1,0:T(8,128)(2,1)S(1)}, bf16[76,2048]{1,0:T(8,128)(2,1)S(1)}, u32[]{:S(2)}, u32[]{:S(2)}) collective-permute-start(bf16[76,2048]{1,0:T(8,128)(2,1)S(1)} %pad_maximum_fusion), channel_id=1, source_target_pairs={{1,0},{2,1},{3,2},{4,3},{5,4},{6,5},{7,6},{9,8},{10,9},{11,10},{12... | collective-permute-start | bytes 933896 | tf_op jit(solution)/shard_map/ppermute | solution.py:17
  4.4 10.0 %collective-permute-start.1 = (f32[2,2,2048]{2,1,0:T(2,128)}, f32[2,2,2048]{2,1,0:T(2,128)S(1)}, u32[]{:S(2)}, u32[]{:S(2)}) collective-permute-start(f32[2,2,2048]{2,1,0:T(2,128)} %bitcast.15), channel_id=1, source_target_pairs={{0,1},{1,2},{2,3},{3,4},{4,5},{5,6},{6,7},{8,9},{9,10},{10,11},{11... | collective-permute-start | bytes 98312 | tf_op jit(solution)/shard_map/ppermute | solution.py:17
  14.4 1.3 %collective-permute-done.1.previous_ref = f32[2,2,2048]{2,1,0:T(2,128)S(1)} collective-permute-done((f32[2,2,2048]{2,1,0:T(2,128)}, f32[2,2,2048]{2,1,0:T(2,128)S(1)}, u32[]{:S(2)}, u32[]{:S(2)}) %collective-permute-start.1) | collective-permute-done | bytes 32800 | tf_op jit(solution)/shard_map/ppermute | solution.py:17
  15.7 0.0 copy-start.1
  15.7 0.6 copy-done.1
  16.3 3.5 %shard_map.46 = (f32[2,2,64,64]{3,2,1,0:T(8,128)}, bf16[256,2048]{1,0:T(8,128)(2,1)}) custom-call(bf16[2,3,64,2048]{3,2,1,0:T(8,128)(2,1)} %bitcast.12, f32[2,2,2048]{2,1,0:T(2,128)} %copy-done.1, f32[2,2,2048]{2,1,0:T(2,128)} %bitcast.16), custom_call_target="tpu_custom_call" | custom-call | tf_op jit(solution)/shard_map/pallas_call | solution.py:121
  19.9 0.0 collective-permute-done.bundle_ref
  19.9 0.0 copy-start
  19.9 0.7 %copy-done = bf16[76,2048]{1,0:T(8,128)(2,1)} copy-done((bf16[76,2048]{1,0:T(8,128)(2,1)}, bf16[76,2048]{1,0:T(8,128)(2,1)S(1)}, u32[]{:S(2)}) %copy-start) | copy-done | bytes 311320
  20.6 3.6 %shard_map.47 = bf16[64,1,160]{2,1,0:T(2,128)(2,1)} custom-call(bf16[2,3,64,2048]{3,2,1,0:T(8,128)(2,1)} %bitcast.13, bf16[76,2048]{1,0:T(8,128)(2,1)} %copy-done, f32[2,2,64,64]{3,2,1,0:T(8,128)} %get-tuple-element.7.near_ref, bf16[256,2048]{1,0:T(8,128)(2,1)} %get-tuple-element.8.held_ref, s32[1,2560]{1,0:T(1,128)} %place_ref.3), custom_call_target="tpu_custom_call" | custom-call | tf_op jit(solution)/shard_map/pallas_call | solution.py:140
  24.3 28.0 %all_to_all.10.in_ref = bf16[64,1,160]{2,1,0:T(2,128)(2,1)} all-to-all(bf16[64,1,160]{2,1,0:T(2,128)(2,1)} %shard_map.47), channel_id=1, replica_groups=mesh['energy'=64,'domain'=8] {'energy'}, dimensions={0} | all-to-all | bytes 40960 | tf_op jit(solution)/shard_map/all_to_all | solution.py:254
  52.3 2.1 %shard_map.48 = bf16[64,1,80]{2,1,0:T(2,128)(2,1)} custom-call(bf16[64,1,160]{2,1,0:T(2,128)(2,1)} %all_to_all.10.in_ref), custom_call_target="tpu_custom_call" | custom-call | tf_op jit(solution)/shard_map/pallas_call | solution.py:179
  54.3 14.8 %all_to_all.11.polar_ref = bf16[64,1,80]{2,1,0:T(2,128)(2,1)} all-to-all(bf16[64,1,80]{2,1,0:T(2,128)(2,1)} %shard_map.48), channel_id=1, replica_groups=mesh['energy'=64,'domain'=8] {'energy'}, dimensions={0} | all-to-all | bytes 20480 | tf_op jit(solution)/shard_map/all_to_all | solution.py:256
  69.1 2.7 %shard_map.49 = f32[2,64,64]{2,1,0:T(8,128)} custom-call(bf16[64,1,80]{2,1,0:T(2,128)(2,1)} %all_to_all.11.polar_ref, s32[1,2560]{1,0:T(1,128)} %place_ref.3, bf16[2,64,80]{2,1,0:T(8,128)(2,1)} %bitcast.17), custom_call_target="tpu_custom_call" | custom-call | tf_op jit(solution)/shard_map/pallas_call | solution.py:228
  (2 shorter events, 0.1 us)
Async XLA Ops:
  1.9 18.0 %collective-permute-start = (bf16[76,2048]{1,0:T(8,128)(2,1)S(1)}, bf16[76,2048]{1,0:T(8,128)(2,1)S(1)}, u32[]{:S(2)}, u32[]{:S(2)}) collective-permute-start(bf16[76,2048]{1,0:T(8,128)(2,1)S(1)} %pad_maximum_fusion), channel_id=1, source_target_pairs={{1,0},{2,1},{3,2},{4,3},{5,4},{6,5},{7,6},{9,8},{10,9},{11,10},{12... | collective-permute-start | bytes 933896 | tf_op jit(solution)/shard_map/ppermute | solution.py:17
  4.4 11.3 %collective-permute-start.1 = (f32[2,2,2048]{2,1,0:T(2,128)}, f32[2,2,2048]{2,1,0:T(2,128)S(1)}, u32[]{:S(2)}, u32[]{:S(2)}) collective-permute-start(f32[2,2,2048]{2,1,0:T(2,128)} %bitcast.15), channel_id=1, source_target_pairs={{0,1},{1,2},{2,3},{3,4},{4,5},{5,6},{6,7},{8,9},{9,10},{10,11},{11... | collective-permute-start | bytes 98312 | tf_op jit(solution)/shard_map/ppermute | solution.py:17
  15.7 0.6 copy-start.1
  19.9 0.7 %copy-start = (bf16[76,2048]{1,0:T(8,128)(2,1)}, bf16[76,2048]{1,0:T(8,128)(2,1)S(1)}, u32[]{:S(2)}) copy-start(bf16[76,2048]{1,0:T(8,128)(2,1)S(1)} %collective-permute-done.bundle_ref) | copy-start | bytes 933892

commit v21 on v19

--- a/solution.py
+++ b/solution.py
@@ -20,10 +20,10 @@
 def _weigh(real_f, imag_f, rate_ref, block, factor):
     pieces = []
     for q in range(2):
-        rate_real = rate_ref[block, q, 0:1, :]
-        rate_imag = rate_ref[block, q, 1:2, :]
-        pieces.append(((real_f * rate_real - imag_f * rate_imag) * factor).astype(jnp.bfloat16))
-        pieces.append(((real_f * rate_imag + imag_f * rate_real) * factor).astype(jnp.bfloat16))
+        rate_real = rate_ref[block, q, 0:1, :] * factor
+        rate_imag = rate_ref[block, q, 1:2, :] * factor
+        pieces.append((real_f * rate_real - imag_f * rate_imag).astype(jnp.bfloat16))
+        pieces.append((real_f * rate_imag + imag_f * rate_real).astype(jnp.bfloat16))
     return jnp.concatenate(pieces, axis=0)
 
 

time: 72 us -> 72 us (level)
  transfers between devices with their start and end apart: 2 -> 2, of which waited for: 1 -> 2; matrix products, arithmetic and copies ran while one was open for 0% -> 0% of each run, Pallas kernels for 5% -> 5%
where the time goes in v21:
time: 72 us; the launch traced here: 71.5 us
  blocking collectives  42.8 us (59%)
  starting transfers between devices  12.5 us (17%)
  Pallas kernels  11.4 us (16%)
  local copies, waits for them, and re-layouts  2.34 us (3%)
  waiting for transfers between devices  1.57 us (2%)
  other arithmetic  0.9 us (1%)
    all_to_all x1, blocking collectives, body(): lax.all_to_all(values, 'energy', split_axis=0, concat_axis=0, tiled=True)  28 us
    all_to_all x1, blocking collectives, body(): lax.all_to_all(polarization, 'energy', split_axis=0, concat_axis=0, tiled...  14.8 us
    ppermute x2, starting transfers between devices, passed_along(): return lax.ppermute(x, axis, pairs)  12.5 us
    pallas_call x1, Pallas kernels, element_values(): pl.pallas_call(functools.partial(_late_kernel, factor=factor, rows=rows,...  3.62 us
    pallas_call x1, Pallas kernels, element_values(): pl.pallas_call(functools.partial(_early_kernel, factor=factor, rows=rows)...  3.31 us
    pallas_call x1, Pallas kernels, screen(): pl.pallas_call(kernel, out_shape=jax.ShapeDtypeStruct((2, rows, rows), jn...  2.41 us
    pallas_call x1, Pallas kernels, lag_sums(): pl.pallas_call(kernel, out_shape=jax.ShapeDtypeStruct((energy_count, 1, 2...  2.08 us
    ppermute x2, waiting for transfers between devices, passed_along(): return lax.ppermute(x, axis, pairs)  1.57 us
  transfers between devices with their start and end apart: 2, of which 2 were waited for; matrix products, arithmetic and copies ran while one was open for 0% of the time, Pallas kernels for 5%

profile of v21, /device:TPU:7, one launch (start us, length us, event | category | flops | bytes accessed | tf_op | source)
XLA Modules:
  0.0 71.5 jit_solution(10793218889995800451)
XLA Ops:
  0.0 0.8 %reduce-precision_convert_fusion.1 = (bf16[1,2,2,2048]{3,2,1,0:T(2,128)(2,1)S(1)}, bf16[1,2,2,2048]{3,2,1,0:T(2,128)(2,1)S(1)}, bf16[1,2,2,2048]{3,2,1,0:T(2,128)(2,1)S(1)}) fusion(f32[1,1,2,2,2048]{4,3,2,1,0:T(2,128)} %param.5), kind=kLoop, calls=%fused_computation.5 | loop fusion | flops 57344 | bytes 81920 | tf_op jit(solution)/shard_map/convert
  0.8 0.1 pad_maximum_fusion.1
  0.9 1.0 %slice.3 = bf16[1,1,2,2,16,2048]{5,4,3,2,1,0:T(8,128)(2,1)S(1)} slice(bf16[1,1,2,3,64,2048]{5,4,3,2,1,0:T(8,128)(2,1)} %param.4), slice={[0:1], [0:1], [0:2], [0:2], [0:16], [0:2048]} | slice | bytes 524288 | tf_op jit(solution)/shard_map/slice | solution.py:249
  1.9 2.5 %collective-permute-start = (bf16[76,2048]{1,0:T(8,128)(2,1)S(1)}, bf16[76,2048]{1,0:T(8,128)(2,1)S(1)}, u32[]{:S(2)}, u32[]{:S(2)}) collective-permute-start(bf16[76,2048]{1,0:T(8,128)(2,1)S(1)} %pad_maximum_fusion), channel_id=1, source_target_pairs={{1,0},{2,1},{3,2},{4,3},{5,4},{6,5},{7,6},{9,8},{10,9},{11,10},{12... | collective-permute-start | bytes 933896 | tf_op jit(solution)/shard_map/ppermute | solution.py:17
  4.4 10.0 %collective-permute-start.1 = (f32[2,2,2048]{2,1,0:T(2,128)}, f32[2,2,2048]{2,1,0:T(2,128)S(1)}, u32[]{:S(2)}, u32[]{:S(2)}) collective-permute-start(f32[2,2,2048]{2,1,0:T(2,128)} %bitcast.15), channel_id=1, source_target_pairs={{0,1},{1,2},{2,3},{3,4},{4,5},{5,6},{6,7},{8,9},{9,10},{10,11},{11... | collective-permute-start | bytes 98312 | tf_op jit(solution)/shard_map/ppermute | solution.py:17
  14.4 1.3 %collective-permute-done.1.previous_ref = f32[2,2,2048]{2,1,0:T(2,128)S(1)} collective-permute-done((f32[2,2,2048]{2,1,0:T(2,128)}, f32[2,2,2048]{2,1,0:T(2,128)S(1)}, u32[]{:S(2)}, u32[]{:S(2)}) %collective-permute-start.1) | collective-permute-done | bytes 32800 | tf_op jit(solution)/shard_map/ppermute | solution.py:17
  15.7 0.0 copy-start.1
  15.7 0.6 copy-done.1
  16.3 3.3 %shard_map.46 = (f32[2,2,64,64]{3,2,1,0:T(8,128)}, bf16[256,2048]{1,0:T(8,128)(2,1)}) custom-call(bf16[2,3,64,2048]{3,2,1,0:T(8,128)(2,1)} %bitcast.12, f32[2,2,2048]{2,1,0:T(2,128)} %copy-done.1, f32[2,2,2048]{2,1,0:T(2,128)} %bitcast.16), custom_call_target="tpu_custom_call" | custom-call | tf_op jit(solution)/shard_map/pallas_call | solution.py:121
  19.7 0.2 collective-permute-done.bundle_ref
  19.9 0.0 copy-start
  19.9 0.7 %copy-done = bf16[76,2048]{1,0:T(8,128)(2,1)} copy-done((bf16[76,2048]{1,0:T(8,128)(2,1)}, bf16[76,2048]{1,0:T(8,128)(2,1)S(1)}, u32[]{:S(2)}) %copy-start) | copy-done | bytes 311320
  20.6 3.6 %shard_map.47 = bf16[64,1,160]{2,1,0:T(2,128)(2,1)} custom-call(bf16[2,3,64,2048]{3,2,1,0:T(8,128)(2,1)} %bitcast.13, bf16[76,2048]{1,0:T(8,128)(2,1)} %copy-done, f32[2,2,64,64]{3,2,1,0:T(8,128)} %get-tuple-element.7.near_ref, bf16[256,2048]{1,0:T(8,128)(2,1)} %get-tuple-element.8.held_ref, s32[1,2560]{1,0:T(1,128)} %place_ref.3), custom_call_target="tpu_custom_call" | custom-call | tf_op jit(solution)/shard_map/pallas_call | solution.py:140
  24.3 28.0 %all_to_all.10.in_ref = bf16[64,1,160]{2,1,0:T(2,128)(2,1)} all-to-all(bf16[64,1,160]{2,1,0:T(2,128)(2,1)} %shard_map.47), channel_id=1, replica_groups=mesh['energy'=64,'domain'=8] {'energy'}, dimensions={0} | all-to-all | bytes 40960 | tf_op jit(solution)/shard_map/all_to_all | solution.py:256
  52.2 2.1 %shard_map.48 = bf16[64,1,80]{2,1,0:T(2,128)(2,1)} custom-call(bf16[64,1,160]{2,1,0:T(2,128)(2,1)} %all_to_all.10.in_ref), custom_call_target="tpu_custom_call" | custom-call | tf_op jit(solution)/shard_map/pallas_call | solution.py:179
  54.3 14.8 %all_to_all.11.polar_ref = bf16[64,1,80]{2,1,0:T(2,128)(2,1)} all-to-all(bf16[64,1,80]{2,1,0:T(2,128)(2,1)} %shard_map.48), channel_id=1, replica_groups=mesh['energy'=64,'domain'=8] {'energy'}, dimensions={0} | all-to-all | bytes 20480 | tf_op jit(solution)/shard_map/all_to_all | solution.py:258
  69.1 2.4 %shard_map.49 = f32[2,64,64]{2,1,0:T(8,128)} custom-call(bf16[64,1,80]{2,1,0:T(2,128)(2,1)} %all_to_all.11.polar_ref, s32[1,2560]{1,0:T(1,128)} %place_ref.3, bf16[2,64,80]{2,1,0:T(8,128)(2,1)} %bitcast.17), custom_call_target="tpu_custom_call" | custom-call | tf_op jit(solution)/shard_map/pallas_call | solution.py:230
  (2 shorter events, 0.1 us)
Async XLA Ops:
  1.9 18.0 %collective-permute-start = (bf16[76,2048]{1,0:T(8,128)(2,1)S(1)}, bf16[76,2048]{1,0:T(8,128)(2,1)S(1)}, u32[]{:S(2)}, u32[]{:S(2)}) collective-permute-start(bf16[76,2048]{1,0:T(8,128)(2,1)S(1)} %pad_maximum_fusion), channel_id=1, source_target_pairs={{1,0},{2,1},{3,2},{4,3},{5,4},{6,5},{7,6},{9,8},{10,9},{11,10},{12... | collective-permute-start | bytes 933896 | tf_op jit(solution)/shard_map/ppermute | solution.py:17
  4.4 11.3 %collective-permute-start.1 = (f32[2,2,2048]{2,1,0:T(2,128)}, f32[2,2,2048]{2,1,0:T(2,128)S(1)}, u32[]{:S(2)}, u32[]{:S(2)}) collective-permute-start(f32[2,2,2048]{2,1,0:T(2,128)} %bitcast.15), channel_id=1, source_target_pairs={{0,1},{1,2},{2,3},{3,4},{4,5},{5,6},{6,7},{8,9},{9,10},{10,11},{11... | collective-permute-start | bytes 98312 | tf_op jit(solution)/shard_map/ppermute | solution.py:17
  15.7 0.6 copy-start.1
  19.9 0.7 %copy-start = (bf16[76,2048]{1,0:T(8,128)(2,1)}, bf16[76,2048]{1,0:T(8,128)(2,1)S(1)}, u32[]{:S(2)}) copy-start(bf16[76,2048]{1,0:T(8,128)(2,1)S(1)} %collective-permute-done.bundle_ref) | copy-start | bytes 933892

commit v22 on v19

--- a/solution.py
+++ b/solution.py
@@ -39,9 +39,10 @@
     count = pattern_ref.shape[1]
     position = pattern_ref[...].astype(jnp.float32)
     row = jnp.floor((position + 0.5) * (1.0 / cols))
-    col = position - row * cols
-    row_hit = lax.broadcasted_iota(jnp.int32, (rows, count), 0).astype(jnp.float32) == row
-    col_hit = lax.broadcasted_iota(jnp.int32, (cols, count), 0).astype(jnp.float32) == col
+    col = (position - row * cols).astype(jnp.int32)
+    row = row.astype(jnp.int32)
+    row_hit = lax.broadcasted_iota(jnp.int32, (rows, count), 0) == row
+    col_hit = lax.broadcasted_iota(jnp.int32, (cols, count), 0) == col
     return row_hit, col_hit
 
 

time: 72 us -> 72.1 us (level)
  no operation moved by 1% of the time
where the time goes in v22:
time: 72.1 us; the launch traced here: 71.6 us
  blocking collectives  42.8 us (59%)
  starting transfers between devices  12.5 us (17%)
  Pallas kernels  11.7 us (16%)
  local copies, waits for them, and re-layouts  2.34 us (3%)
  waiting for transfers between devices  1.36 us (2%)
  other arithmetic  0.9 us (1%)
    all_to_all x1, blocking collectives, body(): lax.all_to_all(values, 'energy', split_axis=0, concat_axis=0, tiled=True)  28 us
    all_to_all x1, blocking collectives, body(): lax.all_to_all(polarization, 'energy', split_axis=0, concat_axis=0, tiled...  14.8 us
    ppermute x2, starting transfers between devices, passed_along(): return lax.ppermute(x, axis, pairs)  12.5 us
    pallas_call x1, Pallas kernels, element_values(): pl.pallas_call(functools.partial(_late_kernel, factor=factor, rows=rows,...  3.71 us
    pallas_call x1, Pallas kernels, element_values(): pl.pallas_call(functools.partial(_early_kernel, factor=factor, rows=rows)...  3.52 us
    pallas_call x1, Pallas kernels, screen(): pl.pallas_call(kernel, out_shape=jax.ShapeDtypeStruct((2, rows, rows), jn...  2.42 us
    pallas_call x1, Pallas kernels, lag_sums(): pl.pallas_call(kernel, out_shape=jax.ShapeDtypeStruct((energy_count, 1, 2...  2.08 us
  transfers between devices with their start and end apart: 2, of which 1 were waited for; matrix products, arithmetic and copies ran while one was open for 0% of the time, Pallas kernels for 5%

profile of v22, /device:TPU:7, one launch (start us, length us, event | category | flops | bytes accessed | tf_op | source)
XLA Modules:
  0.0 71.6 jit_solution(7965384621361685824)
XLA Ops:
  0.0 0.8 %reduce-precision_convert_fusion.1 = (bf16[1,2,2,2048]{3,2,1,0:T(2,128)(2,1)S(1)}, bf16[1,2,2,2048]{3,2,1,0:T(2,128)(2,1)S(1)}, bf16[1,2,2,2048]{3,2,1,0:T(2,128)(2,1)S(1)}) fusion(f32[1,1,2,2,2048]{4,3,2,1,0:T(2,128)} %param.5), kind=kLoop, calls=%fused_computation.5 | loop fusion | flops 57344 | bytes 81920 | tf_op jit(solution)/shard_map/convert
  0.8 0.1 pad_maximum_fusion.1
  0.9 1.0 %slice.3 = bf16[1,1,2,2,16,2048]{5,4,3,2,1,0:T(8,128)(2,1)S(1)} slice(bf16[1,1,2,3,64,2048]{5,4,3,2,1,0:T(8,128)(2,1)} %param.4), slice={[0:1], [0:1], [0:2], [0:2], [0:16], [0:2048]} | slice | bytes 524288 | tf_op jit(solution)/shard_map/slice | solution.py:250
  1.9 2.5 %collective-permute-start = (bf16[76,2048]{1,0:T(8,128)(2,1)S(1)}, bf16[76,2048]{1,0:T(8,128)(2,1)S(1)}, u32[]{:S(2)}, u32[]{:S(2)}) collective-permute-start(bf16[76,2048]{1,0:T(8,128)(2,1)S(1)} %pad_maximum_fusion), channel_id=1, source_target_pairs={{1,0},{2,1},{3,2},{4,3},{5,4},{6,5},{7,6},{9,8},{10,9},{11,10},{12... | collective-permute-start | bytes 933896 | tf_op jit(solution)/shard_map/ppermute | solution.py:17
  4.4 10.0 %collective-permute-start.1 = (f32[2,2,2048]{2,1,0:T(2,128)}, f32[2,2,2048]{2,1,0:T(2,128)S(1)}, u32[]{:S(2)}, u32[]{:S(2)}) collective-permute-start(f32[2,2,2048]{2,1,0:T(2,128)} %bitcast.15), channel_id=1, source_target_pairs={{0,1},{1,2},{2,3},{3,4},{4,5},{5,6},{6,7},{8,9},{9,10},{10,11},{11... | collective-permute-start | bytes 98312 | tf_op jit(solution)/shard_map/ppermute | solution.py:17
  14.4 1.3 %collective-permute-done.1.previous_ref = f32[2,2,2048]{2,1,0:T(2,128)S(1)} collective-permute-done((f32[2,2,2048]{2,1,0:T(2,128)}, f32[2,2,2048]{2,1,0:T(2,128)S(1)}, u32[]{:S(2)}, u32[]{:S(2)}) %collective-permute-start.1) | collective-permute-done | bytes 32800 | tf_op jit(solution)/shard_map/ppermute | solution.py:17
  15.7 0.0 copy-start.1
  15.7 0.6 copy-done.1
  16.3 3.5 %shard_map.46 = (f32[2,2,64,64]{3,2,1,0:T(8,128)}, bf16[256,2048]{1,0:T(8,128)(2,1)}) custom-call(bf16[2,3,64,2048]{3,2,1,0:T(8,128)(2,1)} %bitcast.12, f32[2,2,2048]{2,1,0:T(2,128)} %copy-done.1, f32[2,2,2048]{2,1,0:T(2,128)} %bitcast.16), custom_call_target="tpu_custom_call" | custom-call | tf_op jit(solution)/shard_map/pallas_call | solution.py:122
  19.9 0.0 collective-permute-done.bundle_ref
  19.9 0.0 copy-start
  19.9 0.7 %copy-done = bf16[76,2048]{1,0:T(8,128)(2,1)} copy-done((bf16[76,2048]{1,0:T(8,128)(2,1)}, bf16[76,2048]{1,0:T(8,128)(2,1)S(1)}, u32[]{:S(2)}) %copy-start) | copy-done | bytes 311320
  20.6 3.7 %shard_map.47 = bf16[64,1,160]{2,1,0:T(2,128)(2,1)} custom-call(bf16[2,3,64,2048]{3,2,1,0:T(8,128)(2,1)} %bitcast.13, bf16[76,2048]{1,0:T(8,128)(2,1)} %copy-done, f32[2,2,64,64]{3,2,1,0:T(8,128)} %get-tuple-element.7.near_ref, bf16[256,2048]{1,0:T(8,128)(2,1)} %get-tuple-element.8.held_ref, s32[1,2560]{1,0:T(1,128)} %place_ref.3), custom_call_target="tpu_custom_call" | custom-call | tf_op jit(solution)/shard_map/pallas_call | solution.py:141
  24.3 28.0 %all_to_all.10.in_ref = bf16[64,1,160]{2,1,0:T(2,128)(2,1)} all-to-all(bf16[64,1,160]{2,1,0:T(2,128)(2,1)} %shard_map.47), channel_id=1, replica_groups=mesh['energy'=64,'domain'=8] {'energy'}, dimensions={0} | all-to-all | bytes 40960 | tf_op jit(solution)/shard_map/all_to_all | solution.py:257
  52.3 2.1 %shard_map.48 = bf16[64,1,80]{2,1,0:T(2,128)(2,1)} custom-call(bf16[64,1,160]{2,1,0:T(2,128)(2,1)} %all_to_all.10.in_ref), custom_call_target="tpu_custom_call" | custom-call | tf_op jit(solution)/shard_map/pallas_call | solution.py:180
  54.4 14.8 %all_to_all.11.polar_ref = bf16[64,1,80]{2,1,0:T(2,128)(2,1)} all-to-all(bf16[64,1,80]{2,1,0:T(2,128)(2,1)} %shard_map.48), channel_id=1, replica_groups=mesh['energy'=64,'domain'=8] {'energy'}, dimensions={0} | all-to-all | bytes 20480 | tf_op jit(solution)/shard_map/all_to_all | solution.py:259
  69.2 2.4 %shard_map.49 = f32[2,64,64]{2,1,0:T(8,128)} custom-call(bf16[64,1,80]{2,1,0:T(2,128)(2,1)} %all_to_all.11.polar_ref, s32[1,2560]{1,0:T(1,128)} %place_ref.3, bf16[2,64,80]{2,1,0:T(8,128)(2,1)} %bitcast.17), custom_call_target="tpu_custom_call" | custom-call | tf_op jit(solution)/shard_map/pallas_call | solution.py:231
  (2 shorter events, 0.1 us)
Async XLA Ops:
  1.9 18.0 %collective-permute-start = (bf16[76,2048]{1,0:T(8,128)(2,1)S(1)}, bf16[76,2048]{1,0:T(8,128)(2,1)S(1)}, u32[]{:S(2)}, u32[]{:S(2)}) collective-permute-start(bf16[76,2048]{1,0:T(8,128)(2,1)S(1)} %pad_maximum_fusion), channel_id=1, source_target_pairs={{1,0},{2,1},{3,2},{4,3},{5,4},{6,5},{7,6},{9,8},{10,9},{11,10},{12... | collective-permute-start | bytes 933896 | tf_op jit(solution)/shard_map/ppermute | solution.py:17
  4.4 11.3 %collective-permute-start.1 = (f32[2,2,2048]{2,1,0:T(2,128)}, f32[2,2,2048]{2,1,0:T(2,128)S(1)}, u32[]{:S(2)}, u32[]{:S(2)}) collective-permute-start(f32[2,2,2048]{2,1,0:T(2,128)} %bitcast.15), channel_id=1, source_target_pairs={{0,1},{1,2},{2,3},{3,4},{4,5},{5,6},{6,7},{8,9},{9,10},{10,11},{11... | collective-permute-start | bytes 98312 | tf_op jit(solution)/shard_map/ppermute | solution.py:17
  15.7 0.6 copy-start.1
  19.9 0.7 %copy-start = (bf16[76,2048]{1,0:T(8,128)(2,1)}, bf16[76,2048]{1,0:T(8,128)(2,1)S(1)}, u32[]{:S(2)}) copy-start(bf16[76,2048]{1,0:T(8,128)(2,1)S(1)} %collective-permute-done.bundle_ref) | copy-start | bytes 933892
